TPU v7x, 32 devices: a whole 2x2x4 slice. The times are simulated.
32 devices in a mesh: tm: 4 (over y, x), sta: 8 (over z, core).
Axes of the slice: x: 2, y: 2, z: 4, core: 2. Of those that a mesh axis runs over, the one named last changes fastest.
Arguments:
- records: float32 [320, 64, 4096], P('sta', 'tm'), may hold values from -480 to 480
- partners: int32 [8, 5], P('sta'), may hold values from 0 to 7, as said below
- counts: int32 [8], P('sta'), may hold values from 1 to 5, as said below
Outputs:
- cross: float32 [8, 5, 40, 10240], P('sta', None, None, 'tm')
Inputs may be any that keep to these rules, and one draw needn't show every extreme that they name: `partners`: row i lists distinct blocks j with |i - j| <= 2 in its first counts[i] slots, in no particular order; the later slots hold i itself. counts[i] is at most the number of blocks j with |i - j| <= 2; some block has 5.
All inputs are finite; a program needn't handle non-finite values.
Results may differ from a plain program's by a relative error of at most 0.00077.
Values may be sent and summed in bfloat16 or wider, within the bound.
No kernel may reach another device: no remote copies, remote signals or barrier semaphores. Data moves between devices by JAX's collectives and lax.ppermute only.
A program may use at most 128 MiB of HBM per device.

v0:
```python
import math

import jax
import jax.numpy as jnp
from jax import lax
from jax.experimental import pallas as pl
from jax.sharding import PartitionSpec as P

BINS = 128
R = 2
BINS_PER_STEP = 8


def passed_along(array, axis, by):
    peers = lax.axis_size(axis)
    pairs = [(i, i + by) for i in range(peers) if 0 <= i + by < peers]
    return lax.ppermute(array, axis, pairs)


def dft_columns(samples, bins, groups):
    local = bins // groups
    column = jnp.arange(2 * bins, dtype=jnp.int32)
    group_of = column // (2 * local)
    part_of = column // local % 2
    harmonic = group_of * local + column % local + 1
    positions = jnp.arange(samples, dtype=jnp.int32)
    phases = positions[:, None] * harmonic[None, :] % samples
    angles = phases.astype(jnp.float32) * (2.0 * math.pi / samples)
    return jnp.where(part_of[None, :] == 0, jnp.cos(angles), -jnp.sin(angles))


def whiten(records, groups):
    dft_table = dft_columns(records.shape[2], BINS, groups)
    spectra = jnp.einsum("swn,nk->swk", records, dft_table, precision=lax.Precision.HIGHEST)
    mean_power = jnp.mean(spectra * spectra, axis=2, keepdims=True)
    white = (spectra / jnp.sqrt(mean_power + 1e-06)).astype(jnp.bfloat16)
    return white.reshape(1, records.shape[0], records.shape[1], groups, 2 * (BINS // groups))


def cross_kernel(scale, lx_ref, y_ref, o_ref):
    bins, two_s, _ = lx_ref.shape
    s = two_s // 2
    slots = y_ref.shape[1] // s
    for b in range(bins):
        r = lax.dot_general(
            lx_ref[b], y_ref[b], (((1,), (1,)), ((), ())), preferred_element_type=jnp.float32
        )
        r = r * scale
        for p in range(slots):
            for x in range(2):
                col = (2 * b + x) * s
                o_ref[p, :, col:col + s] = r[x * s:(x + 1) * s, p * s:(p + 1) * s]


def cross_block(lx, ysel, windows):
    nb, two_s, k = lx.shape
    s = two_s // 2
    slots = ysel.shape[1] // s
    step = BINS_PER_STEP
    kernel = lambda *refs: cross_kernel(1.0 / windows, *refs)
    return pl.pallas_call(
        kernel,
        grid=(nb // step,),
        in_specs=[
            pl.BlockSpec((step, two_s, k), lambda g: (g, 0, 0)),
            pl.BlockSpec((step, slots * s, k), lambda g: (g, 0, 0)),
        ],
        out_specs=pl.BlockSpec((slots, s, step * two_s), lambda g: (0, 0, g)),
        out_shape=jax.ShapeDtypeStruct((slots, s, nb * two_s), jnp.float32),
    )(lx, ysel)


def body(records, partners, counts):
    own_spec = whiten(records, lax.axis_size("tm"))
    block_index = lax.axis_index("sta")
    partner_row = partners[0]
    slots = partner_row.shape[0]
    live_slots = jnp.arange(slots, dtype=jnp.int32) < counts[0]
    regrouped = lax.all_to_all(own_spec, "tm", split_axis=3, concat_axis=2, tiled=True)
    stations, windows, width = regrouped.shape[1], regrouped.shape[2], regrouped.shape[4]
    nb = width // 2
    spec = (
        regrouped.reshape(stations, windows, 2, nb)
        .transpose(3, 0, 2, 1)
        .reshape(nb, stations, 2 * windows)
    )
    pieces = []
    for offset in range(-R, R + 1):
        pieces.append(spec if offset == 0 else passed_along(spec, "sta", -offset))
    stacked = jnp.stack(pieces, axis=1)
    where_at = jnp.clip(partner_row - block_index + R, 0, 2 * R)
    chosen = jnp.take(stacked, where_at, axis=1)
    chosen = jnp.where(live_slots[None, :, None, None], chosen, jnp.zeros((), chosen.dtype))
    ysel = chosen.reshape(nb, slots * stations, 2 * windows)
    x_re = spec[:, :, :windows]
    x_im = spec[:, :, windows:]
    lx = jnp.concatenate([spec, jnp.concatenate([-x_im, x_re], axis=2)], axis=1)
    result = cross_block(lx, ysel, windows)
    return result[None]


def solution(mesh):
    in_specs = (P("sta", "tm", None), P("sta", None), P("sta"))
    out_specs = P("sta", None, None, "tm")
    return jax.shard_map(body, mesh=mesh, in_specs=in_specs, out_specs=out_specs, check_vma=False)
```

profile of v0, /device:TPU:0, one launch (start us, length us, event | category | flops | bytes accessed | tf_op | source)
XLA Modules:
  0.0 81.5 jit_solution(8767396294152420578)
XLA Ops:
  0.0 16.8 %fusion.5.clone.4 = f32[4096,256,1]{1,0,2:T(8,128)S(1)} fusion(s32[256]{0:T(256)S(1)} %fusion.28, pred[256]{0:T(512)(128)(4,1)S(1)} %fusion.31), kind=kLoop, calls=%fused_computation.9.clone.clone.clone.1 | loop fusion | flops 16777216 | bytes 4195584 | tf_op jit(solution)/shard_map/reduce_sum | solution.py:35
  16.8 17.6 %multiply_reduce_fusion = (f32[40,16]{0,1:T(8,128)S(1)}, f32[256,40,16]{0,1,2:T(8,128)S(1)}) fusion(f32[40,16,4096]{2,1,0:T(8,128)} %param.3, f32[4096,256,1]{1,0,2:T(8,128)S(1)} %fusion.5.clone.4), kind=kOutput, calls=%fused_computation.27 | convolution fusion | flops 8053390848 | bytes 15337984 | tf_op jit(solution)/shard_map/swn,nk->swk/dot_general | solution.py:34
  34.4 0.2 fusion.23
  34.6 0.3 reshape.118
  34.9 0.3 copy.23
  35.2 1.2 %reshape.130 = bf16[4,2,20480]{2,1,0:T(2,128)(2,1)} reshape(bf16[4,1,40,16,64]{4,3,2,1,0:T(8,128)(2,1)S(1)} %bitcast.49) | data formatting | bytes 655360
  36.4 5.2 %all-to-all-start = ((bf16[4,2,20480]{2,1,0:T(2,128)(2,1)}), bf16[4,2,20480]{2,1,0:T(2,128)(2,1)S(1)}, u32[]{:S(2)}, u32[]{:S(2)}) async-start(bf16[4,2,20480]{2,1,0:T(2,128)(2,1)} %reshape.130), calls=%async_computation | async-start | bytes 655360 | tf_op jit(solution)/shard_map/all_to_all | solution.py:79
  41.6 0.1 broadcast_in_dim.50
  41.6 0.1 broadcast_in_dim.51
  42.4 0.1 broadcast_in_dim.47
  42.5 0.1 broadcast_in_dim.48
  42.6 4.9 %all-to-all-done = bf16[4,2,20480]{2,1,0:T(2,128)(2,1)S(1)} async-done(((bf16[4,2,20480]{2,1,0:T(2,128)(2,1)}), bf16[4,2,20480]{2,1,0:T(2,128)(2,1)S(1)}, u32[]{:S(2)}, u32[]{:S(2)}) %all-to-all-start) | async-done | bytes 327712 | tf_op jit(solution)/shard_map/all_to_all | solution.py:79
  47.4 0.4 reshape.131
  47.9 0.1 bitcast_bitcast_fusion
  48.0 0.8 copy.13
  48.8 1.3 %copy.14 = bf16[32,40,2,64]{3,2,1,0:T(2,128)(2,1)S(1)} copy(bf16[32,40,2,64]{1,0,2,3:T(8,128)(2,1)S(1)} %bitcast.48) | data formatting | bytes 655360 | tf_op jit(solution)/shard_map/transpose | solution.py:84
  50.1 0.3 reshape.120
  50.4 4.2 %collective-permute-start = (bf16[32,40,128]{2,1,0:T(8,128)(2,1)S(1)}, bf16[32,40,128]{2,1,0:T(8,128)(2,1)}, u32[]{:S(2)}, u32[]{:S(2)}) collective-permute-start(bf16[32,40,128]{2,1,0:T(8,128)(2,1)S(1)} %reshape.120), channel_id=1, source_target_pairs={{0,2},{1,3},{2,4},{3,5},{4,6},{5,7},{8,10},{9,11},{10,12},{11,13},... | collective-permute-start | bytes 983048 | tf_op jit(solution)/shard_map/ppermute | solution.py:17
  54.6 2.0 %collective-permute-start.1 = (bf16[32,40,128]{2,1,0:T(8,128)(2,1)S(1)}, bf16[32,40,128]{2,1,0:T(8,128)(2,1)}, u32[]{:S(2)}, u32[]{:S(2)}) collective-permute-start(bf16[32,40,128]{2,1,0:T(8,128)(2,1)S(1)} %reshape.120), channel_id=1, source_target_pairs={{0,1},{1,2},{2,3},{3,4},{4,5},{5,6},{6,7},{8,9},{9,10},{10,11},{11... | collective-permute-start | bytes 983048 | tf_op jit(solution)/shard_map/ppermute | solution.py:17
  56.6 0.3 stack_reshape.3
  56.9 1.3 %collective-permute-start.2 = (bf16[32,40,128]{2,1,0:T(8,128)(2,1)S(1)}, bf16[32,40,128]{2,1,0:T(8,128)(2,1)S(1)}, u32[]{:S(2)}, u32[]{:S(2)}) collective-permute-start(bf16[32,40,128]{2,1,0:T(8,128)(2,1)S(1)} %reshape.120), channel_id=1, source_target_pairs={{1,0},{2,1},{3,2},{4,3},{5,4},{6,5},{7,6},{9,8},{10,9},{11,10},{12... | collective-permute-start | bytes 983048 | tf_op jit(solution)/shard_map/ppermute | solution.py:17
  58.2 1.3 %collective-permute-start.3 = (bf16[32,40,128]{2,1,0:T(8,128)(2,1)S(1)}, bf16[32,40,128]{2,1,0:T(8,128)(2,1)S(1)}, u32[]{:S(2)}, u32[]{:S(2)}) collective-permute-start(bf16[32,40,128]{2,1,0:T(8,128)(2,1)S(1)} %reshape.120), channel_id=1, source_target_pairs={{2,0},{3,1},{4,2},{5,3},{6,4},{7,5},{10,8},{11,9},{12,10},{13,11},... | collective-permute-start | bytes 983048 | tf_op jit(solution)/shard_map/ppermute | solution.py:17
  59.5 0.2 slice_negate_fusion
  59.7 1.0 %maximum_maximum_fusion.refs_0_ = bf16[32,80,128]{2,1,0:T(8,128)(2,1)} fusion(bf16[32,40,64]{2,1,0:T(8,128)(2,1)S(1)} %get-tuple-element.6, bf16[32,40,64]{2,1,0:T(8,128)(2,1)S(1)} %get-tuple-element.5, bf16[32,40,128]{2,1,0:T(8,128)(2,1)S(1)} %reshape.120), kind=kLoop, calls=%fused_computation.25 | loop fusion | flops 1966080 | bytes 1310720 | tf_op jit(solution)/shard_map/concatenate | solution.py:97
  60.7 0.6 collective-permute-done
  61.3 1.0 %bitcast_dynamic-update-slice_fusion.3 = bf16[32,5,40,128]{3,2,0,1:T(8,128)(2,1)S(1)} fusion(bf16[32,40,128]{2,1,0:T(8,128)(2,1)} %collective-permute-done), kind=kLoop, calls=%fused_computation.32 | loop fusion | bytes 655360
  62.3 1.0 %bitcast_dynamic-update-slice_fusion.2 = bf16[32,5,40,128]{3,2,0,1:T(8,128)(2,1)S(1)} fusion(bf16[32,5,40,128]{3,2,0,1:T(8,128)(2,1)S(1)} %bitcast_dynamic-update-slice_fusion.3, bf16[32,40,128]{2,1,0:T(8,128)(2,1)} %collective-permute-done.1), kind=kLoop, calls=%fused_computation.31 | loop fusion | bytes 655360
  63.5 9.9 %collective-permute-done.3 = bf16[32,40,128]{2,1,0:T(8,128)(2,1)S(1)} collective-permute-done((bf16[32,40,128]{2,1,0:T(8,128)(2,1)S(1)}, bf16[32,40,128]{2,1,0:T(8,128)(2,1)S(1)}, u32[]{:S(2)}, u32[]{:S(2)}) %collective-permute-start.3) | collective-permute-done | bytes 327712 | tf_op jit(solution)/shard_map/ppermute | solution.py:17
  73.4 0.9 %gather_fusion = bf16[5,32,40,128]{3,2,1,0:T(8,128)(2,1)S(1)} fusion(bf16[32,5,40,128]{3,2,0,1:T(8,128)(2,1)S(1)} %bitcast_dynamic-update-slice_fusion, s32[1024]{0:T(1024)S(1)} %pad_clamp_fusion), kind=kCustom, calls=%fused_computation | custom fusion | bytes 3276820 | tf_op jit(solution)/shard_map/jit(_take)/gather | solution.py:92
  74.3 0.3 copy.16
  74.6 1.5 %fusion.22.refs_1_ = bf16[32,200,128]{2,1,0:T(8,128)(2,1)} fusion(bf16[32,5,40,128]{3,2,1,0:T(8,128)(2,1)S(1)} %copy.16, pred[200]{0:T(512)(128)(4,1)S(1)} %broadcast_in_dim.51, pred[200]{0:T(512)(128)(4,1)S(1)} %broadcast_in_dim.48), kind=kLoop, calls=%fused_computation.24 | loop fusion | flops 1638400 | bytes 3277200 | tf_op jit(solution)/shard_map/jit(_where)/select_n | solution.py:93
  76.1 5.4 %shard_map.37 = f32[5,40,2560]{2,1,0:T(8,128)} custom-call(bf16[32,80,128]{2,1,0:T(8,128)(2,1)} %maximum_maximum_fusion.refs_0_, bf16[32,200,128]{2,1,0:T(8,128)(2,1)} %fusion.22.refs_1_), custom_call_target="tpu_custom_call" | custom-call | tf_op jit(solution)/shard_map/pallas_call | solution.py:61
  (14 shorter events, 0.2 us)
Async XLA Ops:
  34.9 6.7 %copy-start = (s32[1,5]{1,0:T(1,128)S(1)}, s32[1,5]{1,0:T(1,128)}, u32[]{:S(2)}) copy-start(s32[1,5]{1,0:T(1,128)} %param.4) | copy-start | bytes 64
  36.4 11.1 %all-to-all-start = ((bf16[4,2,20480]{2,1,0:T(2,128)(2,1)}), bf16[4,2,20480]{2,1,0:T(2,128)(2,1)S(1)}, u32[]{:S(2)}, u32[]{:S(2)}) async-start(bf16[4,2,20480]{2,1,0:T(2,128)(2,1)} %reshape.130), calls=%async_computation | async-start | bytes 655360 | tf_op jit(solution)/shard_map/all_to_all | solution.py:79
  50.4 10.9 %collective-permute-start = (bf16[32,40,128]{2,1,0:T(8,128)(2,1)S(1)}, bf16[32,40,128]{2,1,0:T(8,128)(2,1)}, u32[]{:S(2)}, u32[]{:S(2)}) collective-permute-start(bf16[32,40,128]{2,1,0:T(8,128)(2,1)S(1)} %reshape.120), channel_id=1, source_target_pairs={{0,2},{1,3},{2,4},{3,5},{4,6},{5,7},{8,10},{9,11},{10,12},{11,13},... | collective-permute-start | bytes 983048 | tf_op jit(solution)/shard_map/ppermute | solution.py:17
  54.6 7.7 %collective-permute-start.1 = (bf16[32,40,128]{2,1,0:T(8,128)(2,1)S(1)}, bf16[32,40,128]{2,1,0:T(8,128)(2,1)}, u32[]{:S(2)}, u32[]{:S(2)}) collective-permute-start(bf16[32,40,128]{2,1,0:T(8,128)(2,1)S(1)} %reshape.120), channel_id=1, source_target_pairs={{0,1},{1,2},{2,3},{3,4},{4,5},{5,6},{6,7},{8,9},{9,10},{10,11},{11... | collective-permute-start | bytes 983048 | tf_op jit(solution)/shard_map/ppermute | solution.py:17
  56.9 6.5 %collective-permute-start.2 = (bf16[32,40,128]{2,1,0:T(8,128)(2,1)S(1)}, bf16[32,40,128]{2,1,0:T(8,128)(2,1)S(1)}, u32[]{:S(2)}, u32[]{:S(2)}) collective-permute-start(bf16[32,40,128]{2,1,0:T(8,128)(2,1)S(1)} %reshape.120), channel_id=1, source_target_pairs={{1,0},{2,1},{3,2},{4,3},{5,4},{6,5},{7,6},{9,8},{10,9},{11,10},{12... | collective-permute-start | bytes 983048 | tf_op jit(solution)/shard_map/ppermute | solution.py:17
  58.2 15.1 %collective-permute-start.3 = (bf16[32,40,128]{2,1,0:T(8,128)(2,1)S(1)}, bf16[32,40,128]{2,1,0:T(8,128)(2,1)S(1)}, u32[]{:S(2)}, u32[]{:S(2)}) collective-permute-start(bf16[32,40,128]{2,1,0:T(8,128)(2,1)S(1)} %reshape.120), channel_id=1, source_target_pairs={{2,0},{3,1},{4,2},{5,3},{6,4},{7,5},{10,8},{11,9},{12,10},{13,11},... | collective-permute-start | bytes 983048 | tf_op jit(solution)/shard_map/ppermute | solution.py:17
where the time goes:
time: 81.9 us; the launch traced here: 81.5 us
  other arithmetic  19.7 us (24%)
  matrix products  17.6 us (21%)
  waiting for transfers between devices  15.3 us (19%)
  starting transfers between devices  14 us (17%)
  local copies, waits for them, and re-layouts  8.59 us (10%)
  Pallas kernels  5.39 us (7%)
  between operations  0.85 us (1%)
    dot_general x1, matrix products, whiten(): jnp.einsum('swn,nk->swk', records, dft_table, precision=lax.Precision.HIG...  17.6 us
    reduce_sum x1, other arithmetic, whiten(): mean_power = jnp.mean(spectra * spectra, axis=2, keepdims=True)  16.8 us
    ppermute x4, waiting for transfers between devices, passed_along(): return lax.ppermute(array, axis, pairs)  10.5 us
    ppermute x4, starting transfers between devices, passed_along(): return lax.ppermute(array, axis, pairs)  8.83 us
    pallas_call x1, Pallas kernels, cross_block(): pl.pallas_call(kernel, grid=(nb // step,), in_specs=[pl.BlockSpec((step,...  5.39 us
    all_to_all x1, starting transfers between devices, body(): lax.all_to_all(own_spec, 'tm', split_axis=3, concat_axis=2, tiled=True)  5.16 us
    all_to_all x1, waiting for transfers between devices, body(): lax.all_to_all(own_spec, 'tm', split_axis=3, concat_axis=2, tiled=True)  4.86 us
    unnamed x8, local copies, waits for them, and re-layouts  3.76 us
  transfers between devices with their start and end apart: 5, of which 3 were waited for; matrix products, arithmetic and copies ran while one was open for 5% of the time, Pallas kernels for 0%

commit v1 on v0

--- a/solution.py
+++ b/solution.py
@@ -23,10 +23,19 @@
     group_of = column // (2 * local)
     part_of = column // local % 2
     harmonic = group_of * local + column % local + 1
-    positions = jnp.arange(samples, dtype=jnp.int32)
-    phases = positions[:, None] * harmonic[None, :] % samples
-    angles = phases.astype(jnp.float32) * (2.0 * math.pi / samples)
-    return jnp.where(part_of[None, :] == 0, jnp.cos(angles), -jnp.sin(angles))
+    fine = 1 << ((samples.bit_length() - 1) // 2)
+    coarse = samples // fine
+    unit = 2.0 * math.pi / samples
+    outer = (jnp.arange(coarse, dtype=jnp.int32)[:, None] * fine * harmonic[None, :]) % samples
+    inner = (jnp.arange(fine, dtype=jnp.int32)[:, None] * harmonic[None, :]) % samples
+    c1 = jnp.cos(outer.astype(jnp.float32) * unit)[:, None, :]
+    s1 = jnp.sin(outer.astype(jnp.float32) * unit)[:, None, :]
+    c2 = jnp.cos(inner.astype(jnp.float32) * unit)[None, :, :]
+    s2 = jnp.sin(inner.astype(jnp.float32) * unit)[None, :, :]
+    cosine = c1 * c2 - s1 * s2
+    minus_sine = -(s1 * c2 + c1 * s2)
+    table = jnp.where(part_of[None, None, :] == 0, cosine, minus_sine)
+    return table.reshape(samples, 2 * bins)
 
 
 def whiten(records, groups):

time: 81.9 us -> 65.8 us (0.80)
  other arithmetic: 19.7 us -> 5.84 us
  matrix products: 17.6 us -> 13.4 us
  local copies, waits for them, and re-layouts: 8.59 us -> 10.5 us
    reduce_sum x1 -> x0, other arithmetic: 16.8 us -> none  [whiten(): mean_power = jnp.mean(spectra * spectra, axis=2, keepdims=True)]
    dot_general x1, matrix products: 17.6 us -> 13.4 us  [whiten(): jnp.einsum('swn,nk->swk', records, dft_table, precision=lax.Precision.HIG...]
    unnamed x8 -> x14, local copies, waits for them, and re-layouts: 3.76 us -> 5.7 us
    sub x0 -> x1, other arithmetic: none -> 1.17 us  [dft_columns(): cosine = c1 * c2 - s1 * s2]
    select_n x0 -> x1, other arithmetic: none -> 1.14 us  [dft_columns(): table = jnp.where(part_of[None, None, :] == 0, cosine, minus_sine)]
  transfers between devices with their start and end apart: 5 -> 5, of which waited for: 3 -> 3; matrix products, arithmetic and copies ran while one was open for 5% -> 6% of each run, Pallas kernels for 0% -> 0%
where the time goes in v1:
time: 65.8 us; the launch traced here: 65.4 us
  waiting for transfers between devices  15.4 us (23%)
  starting transfers between devices  14 us (21%)
  matrix products  13.4 us (20%)
  local copies, waits for them, and re-layouts  10.5 us (16%)
  other arithmetic  5.84 us (9%)
  Pallas kernels  5.39 us (8%)
  between operations  0.89 us (1%)
    dot_general x1, matrix products, whiten(): jnp.einsum('swn,nk->swk', records, dft_table, precision=lax.Precision.HIG...  13.4 us
    ppermute x4, waiting for transfers between devices, passed_along(): return lax.ppermute(array, axis, pairs)  10.5 us
    ppermute x4, starting transfers between devices, passed_along(): return lax.ppermute(array, axis, pairs)  8.82 us
    unnamed x14, local copies, waits for them, and re-layouts  5.7 us
    pallas_call x1, Pallas kernels, cross_block(): pl.pallas_call(kernel, grid=(nb // step,), in_specs=[pl.BlockSpec((step,...  5.39 us
    all_to_all x1, starting transfers between devices, body(): lax.all_to_all(own_spec, 'tm', split_axis=3, concat_axis=2, tiled=True)  5.17 us
    all_to_all x1, waiting for transfers between devices, body(): lax.all_to_all(own_spec, 'tm', split_axis=3, concat_axis=2, tiled=True)  4.86 us
    select_n x1, other arithmetic, body(): jnp.where(live_slots[None, :, None, None], chosen, jnp.zeros((), chosen.d...  1.56 us
  transfers between devices with their start and end apart: 5, of which 3 were waited for; matrix products, arithmetic and copies ran while one was open for 6% of the time, Pallas kernels for 0%

profile of v1, /device:TPU:0, one launch (start us, length us, event | category | flops | bytes accessed | tf_op | source)
XLA Modules:
  0.0 65.4 jit_solution(5280167518201537226)
XLA Ops:
  0.0 0.6 fusion.17
  0.6 1.2 %multiply_subtract_fusion = (f32[64,64,256]{2,1,0:T(8,128)S(1)}, f32[64,64,256]{2,1,0:T(8,128)S(1)}) fusion(f32[64,256]{1,0:T(8,128)S(1)} %get-tuple-element.11, f32[64,256]{1,0:T(8,128)S(1)} %get-tuple-element.10, f32[64,256]{1,0:T(8,128)S(1)} %get-tuple-element.12, f32[64,256]{1,0:T(8,128)S(1)} %get-tuple-element.9), kind=kLoop, calls=%fused_computation.6 | loop fusion | flops 7340032 | bytes 8650752 | tf_op jit(solution)/shard_map/sub | solution.py:35
  1.8 1.1 %bitcast_select_fusion = f32[4096,256]{1,0:T(8,128)S(1)} fusion(f32[64,64,256]{2,1,0:T(8,128)S(1)} %get-tuple-element.8, f32[64,64,256]{2,1,0:T(8,128)S(1)} %get-tuple-element.7, pred[256]{0:T(512)(128)(4,1)S(1)} %fusion.25), kind=kLoop, calls=%fused_computation.4 | loop fusion | flops 1048576 | bytes 12583168 | tf_op jit(solution)/shard_map/jit(_where)/select_n | solution.py:37
  2.9 1.1 %slice-done.1 = s8[4194304]{0:T(1024)(128)(4,1)S(1)} async-done(((s8[10485760]{0:T(1024)(128)(4,1)}), s8[4194304]{0:T(1024)(128)(4,1)S(1)}, s32[]{:S(2)}) %slice-start.1) | async-done | bytes 4194328
  4.0 0.8 %slice-done.2 = s8[2097152]{0:T(1024)(128)(4,1)S(1)} async-done(((s8[10485760]{0:T(1024)(128)(4,1)}), s8[2097152]{0:T(1024)(128)(4,1)S(1)}, s32[]{:S(2)}) %slice-start.2) | async-done | bytes 2097176
  4.9 13.4 %multiply_reduce_fusion = (f32[40,16]{0,1:T(8,128)S(1)}, f32[256,40,16]{0,1,2:T(8,128)S(1)}) fusion(f32[40,16,4096]{2,1,0:T(8,128)S(1)} %bitcast.51, f32[4096,256]{1,0:T(8,128)S(1)} %bitcast_select_fusion), kind=kOutput, calls=%fused_computation.11 | convolution fusion | flops 8053390848 | bytes 15337984 | tf_op jit(solution)/shard_map/swn,nk->swk/dot_general | solution.py:43
  18.3 0.2 fusion.4
  18.5 0.3 reshape.254
  18.8 0.3 copy.22
  19.1 1.2 %reshape.266 = bf16[4,2,20480]{2,1,0:T(2,128)(2,1)} reshape(bf16[4,1,40,16,64]{4,3,2,1,0:T(8,128)(2,1)S(1)} %bitcast.49) | data formatting | bytes 655360
  20.3 5.2 %all-to-all-start = ((bf16[4,2,20480]{2,1,0:T(2,128)(2,1)}), bf16[4,2,20480]{2,1,0:T(2,128)(2,1)S(1)}, u32[]{:S(2)}, u32[]{:S(2)}) async-start(bf16[4,2,20480]{2,1,0:T(2,128)(2,1)} %reshape.266), calls=%async_computation | async-start | bytes 655360 | tf_op jit(solution)/shard_map/all_to_all | solution.py:88
  26.5 4.9 %all-to-all-done = bf16[4,2,20480]{2,1,0:T(2,128)(2,1)S(1)} async-done(((bf16[4,2,20480]{2,1,0:T(2,128)(2,1)}), bf16[4,2,20480]{2,1,0:T(2,128)(2,1)S(1)}, u32[]{:S(2)}, u32[]{:S(2)}) %all-to-all-start) | async-done | bytes 327712 | tf_op jit(solution)/shard_map/all_to_all | solution.py:88
  31.3 0.4 reshape.267
  31.8 0.1 bitcast_bitcast_fusion
  31.9 0.8 %copy.13 = bf16[1,40,4,16,1,64]{1,5,3,2,4,0:T(8,128)(2,1)S(1)} copy(bf16[1,40,4,16,1,64]{5,3,1,2,4,0:T(8,128)(2,1)S(1)} %bitcast_bitcast_fusion) | data formatting | bytes 655360 | tf_op jit(solution)/shard_map/all_to_all | solution.py:88
  32.7 1.3 %copy.14 = bf16[32,40,2,64]{3,2,1,0:T(2,128)(2,1)S(1)} copy(bf16[32,40,2,64]{1,0,2,3:T(8,128)(2,1)S(1)} %bitcast.48) | data formatting | bytes 655360 | tf_op jit(solution)/shard_map/transpose | solution.py:93
  34.0 0.3 reshape.256
  34.3 4.2 %collective-permute-start = (bf16[32,40,128]{2,1,0:T(8,128)(2,1)S(1)}, bf16[32,40,128]{2,1,0:T(8,128)(2,1)}, u32[]{:S(2)}, u32[]{:S(2)}) collective-permute-start(bf16[32,40,128]{2,1,0:T(8,128)(2,1)S(1)} %reshape.256), channel_id=1, source_target_pairs={{0,2},{1,3},{2,4},{3,5},{4,6},{5,7},{8,10},{9,11},{10,12},{11,13},... | collective-permute-start | bytes 983048 | tf_op jit(solution)/shard_map/ppermute | solution.py:17
  38.5 2.0 %collective-permute-start.1 = (bf16[32,40,128]{2,1,0:T(8,128)(2,1)S(1)}, bf16[32,40,128]{2,1,0:T(8,128)(2,1)}, u32[]{:S(2)}, u32[]{:S(2)}) collective-permute-start(bf16[32,40,128]{2,1,0:T(8,128)(2,1)S(1)} %reshape.256), channel_id=1, source_target_pairs={{0,1},{1,2},{2,3},{3,4},{4,5},{5,6},{6,7},{8,9},{9,10},{10,11},{11... | collective-permute-start | bytes 983048 | tf_op jit(solution)/shard_map/ppermute | solution.py:17
  40.5 0.3 stack_reshape.3
  40.8 1.3 %collective-permute-start.2 = (bf16[32,40,128]{2,1,0:T(8,128)(2,1)S(1)}, bf16[32,40,128]{2,1,0:T(8,128)(2,1)S(1)}, u32[]{:S(2)}, u32[]{:S(2)}) collective-permute-start(bf16[32,40,128]{2,1,0:T(8,128)(2,1)S(1)} %reshape.256), channel_id=1, source_target_pairs={{1,0},{2,1},{3,2},{4,3},{5,4},{6,5},{7,6},{9,8},{10,9},{11,10},{12... | collective-permute-start | bytes 983048 | tf_op jit(solution)/shard_map/ppermute | solution.py:17
  42.1 1.3 %collective-permute-start.3 = (bf16[32,40,128]{2,1,0:T(8,128)(2,1)S(1)}, bf16[32,40,128]{2,1,0:T(8,128)(2,1)S(1)}, u32[]{:S(2)}, u32[]{:S(2)}) collective-permute-start(bf16[32,40,128]{2,1,0:T(8,128)(2,1)S(1)} %reshape.256), channel_id=1, source_target_pairs={{2,0},{3,1},{4,2},{5,3},{6,4},{7,5},{10,8},{11,9},{12,10},{13,11},... | collective-permute-start | bytes 983048 | tf_op jit(solution)/shard_map/ppermute | solution.py:17
  43.4 0.2 slice_negate_fusion
  43.6 1.0 %maximum_maximum_fusion.refs_0_ = bf16[32,80,128]{2,1,0:T(8,128)(2,1)} fusion(bf16[32,40,64]{2,1,0:T(8,128)(2,1)S(1)} %get-tuple-element.6, bf16[32,40,64]{2,1,0:T(8,128)(2,1)S(1)} %get-tuple-element.5, bf16[32,40,128]{2,1,0:T(8,128)(2,1)S(1)} %reshape.256), kind=kLoop, calls=%fused_computation.9 | loop fusion | flops 1966080 | bytes 1310720 | tf_op jit(solution)/shard_map/concatenate | solution.py:106
  44.6 0.6 collective-permute-done
  45.2 1.0 %bitcast_dynamic-update-slice_fusion.3 = bf16[32,5,40,128]{3,2,0,1:T(8,128)(2,1)S(1)} fusion(bf16[32,40,128]{2,1,0:T(8,128)(2,1)} %collective-permute-done), kind=kLoop, calls=%fused_computation.16 | loop fusion | bytes 655360
  46.2 1.0 %bitcast_dynamic-update-slice_fusion.2 = bf16[32,5,40,128]{3,2,0,1:T(8,128)(2,1)S(1)} fusion(bf16[32,5,40,128]{3,2,0,1:T(8,128)(2,1)S(1)} %bitcast_dynamic-update-slice_fusion.3, bf16[32,40,128]{2,1,0:T(8,128)(2,1)} %collective-permute-done.1), kind=kLoop, calls=%fused_computation.15 | loop fusion | bytes 655360
  47.4 9.9 %collective-permute-done.3 = bf16[32,40,128]{2,1,0:T(8,128)(2,1)S(1)} collective-permute-done((bf16[32,40,128]{2,1,0:T(8,128)(2,1)S(1)}, bf16[32,40,128]{2,1,0:T(8,128)(2,1)S(1)}, u32[]{:S(2)}, u32[]{:S(2)}) %collective-permute-start.3) | collective-permute-done | bytes 327712 | tf_op jit(solution)/shard_map/ppermute | solution.py:17
  57.3 0.9 %gather_fusion = bf16[5,32,40,128]{3,2,1,0:T(8,128)(2,1)S(1)} fusion(bf16[32,5,40,128]{3,2,0,1:T(8,128)(2,1)S(1)} %bitcast_dynamic-update-slice_fusion, s32[1024]{0:T(1024)S(1)} %pad_clamp_fusion), kind=kCustom, calls=%fused_computation | custom fusion | bytes 3276820 | tf_op jit(solution)/shard_map/jit(_take)/gather | solution.py:101
  58.2 0.3 copy.16
  58.5 1.6 %fusion.3.refs_1_ = bf16[32,200,128]{2,1,0:T(8,128)(2,1)} fusion(bf16[32,5,40,128]{3,2,1,0:T(8,128)(2,1)S(1)} %copy.16, pred[200]{0:T(512)(128)(4,1)S(1)} %broadcast_in_dim.57, pred[200]{0:T(512)(128)(4,1)S(1)} %broadcast_in_dim.54), kind=kLoop, calls=%fused_computation.8 | loop fusion | flops 1638400 | bytes 3277200 | tf_op jit(solution)/shard_map/jit(_where)/select_n | solution.py:102
  60.0 5.4 %shard_map.37 = f32[5,40,2560]{2,1,0:T(8,128)} custom-call(bf16[32,80,128]{2,1,0:T(8,128)(2,1)} %maximum_maximum_fusion.refs_0_, bf16[32,200,128]{2,1,0:T(8,128)(2,1)} %fusion.3.refs_1_), custom_call_target="tpu_custom_call" | custom-call | tf_op jit(solution)/shard_map/pallas_call | solution.py:70
  (24 shorter events, 0.6 us)
Async XLA Ops:
  0.6 2.4 %slice-start = ((s8[10485760]{0:T(1024)(128)(4,1)}), s8[4194304]{0:T(1024)(128)(4,1)S(1)}, s32[]{:S(2)}) async-start(s8[10485760]{0:T(1024)(128)(4,1)} %bitcast.50), calls=%async_computation.1 | async-start | bytes 8388608
  0.6 3.5 %slice-start.1 = ((s8[10485760]{0:T(1024)(128)(4,1)}), s8[4194304]{0:T(1024)(128)(4,1)S(1)}, s32[]{:S(2)}) async-start(s8[10485760]{0:T(1024)(128)(4,1)} %bitcast.50), calls=%async_computation.2 | async-start | bytes 8388608
  1.8 3.1 %slice-start.2 = ((s8[10485760]{0:T(1024)(128)(4,1)}), s8[2097152]{0:T(1024)(128)(4,1)S(1)}, s32[]{:S(2)}) async-start(s8[10485760]{0:T(1024)(128)(4,1)} %bitcast.50), calls=%async_computation.3 | async-start | bytes 4194304
  18.8 6.7 %copy-start = (s32[1,5]{1,0:T(1,128)S(1)}, s32[1,5]{1,0:T(1,128)}, u32[]{:S(2)}) copy-start(s32[1,5]{1,0:T(1,128)} %param.4) | copy-start | bytes 64
  20.3 11.1 %all-to-all-start = ((bf16[4,2,20480]{2,1,0:T(2,128)(2,1)}), bf16[4,2,20480]{2,1,0:T(2,128)(2,1)S(1)}, u32[]{:S(2)}, u32[]{:S(2)}) async-start(bf16[4,2,20480]{2,1,0:T(2,128)(2,1)} %reshape.266), calls=%async_computation | async-start | bytes 655360 | tf_op jit(solution)/shard_map/all_to_all | solution.py:88
  34.3 10.9 %collective-permute-start = (bf16[32,40,128]{2,1,0:T(8,128)(2,1)S(1)}, bf16[32,40,128]{2,1,0:T(8,128)(2,1)}, u32[]{:S(2)}, u32[]{:S(2)}) collective-permute-start(bf16[32,40,128]{2,1,0:T(8,128)(2,1)S(1)} %reshape.256), channel_id=1, source_target_pairs={{0,2},{1,3},{2,4},{3,5},{4,6},{5,7},{8,10},{9,11},{10,12},{11,13},... | collective-permute-start | bytes 983048 | tf_op jit(solution)/shard_map/ppermute | solution.py:17
  38.5 7.7 %collective-permute-start.1 = (bf16[32,40,128]{2,1,0:T(8,128)(2,1)S(1)}, bf16[32,40,128]{2,1,0:T(8,128)(2,1)}, u32[]{:S(2)}, u32[]{:S(2)}) collective-permute-start(bf16[32,40,128]{2,1,0:T(8,128)(2,1)S(1)} %reshape.256), channel_id=1, source_target_pairs={{0,1},{1,2},{2,3},{3,4},{4,5},{5,6},{6,7},{8,9},{9,10},{10,11},{11... | collective-permute-start | bytes 983048 | tf_op jit(solution)/shard_map/ppermute | solution.py:17
  40.8 6.5 %collective-permute-start.2 = (bf16[32,40,128]{2,1,0:T(8,128)(2,1)S(1)}, bf16[32,40,128]{2,1,0:T(8,128)(2,1)S(1)}, u32[]{:S(2)}, u32[]{:S(2)}) collective-permute-start(bf16[32,40,128]{2,1,0:T(8,128)(2,1)S(1)} %reshape.256), channel_id=1, source_target_pairs={{1,0},{2,1},{3,2},{4,3},{5,4},{6,5},{7,6},{9,8},{10,9},{11,10},{12... | collective-permute-start | bytes 983048 | tf_op jit(solution)/shard_map/ppermute | solution.py:17
  42.1 15.2 %collective-permute-start.3 = (bf16[32,40,128]{2,1,0:T(8,128)(2,1)S(1)}, bf16[32,40,128]{2,1,0:T(8,128)(2,1)S(1)}, u32[]{:S(2)}, u32[]{:S(2)}) collective-permute-start(bf16[32,40,128]{2,1,0:T(8,128)(2,1)S(1)} %reshape.256), channel_id=1, source_target_pairs={{2,0},{3,1},{4,2},{5,3},{6,4},{7,5},{10,8},{11,9},{12,10},{13,11},... | collective-permute-start | bytes 983048 | tf_op jit(solution)/shard_map/ppermute | solution.py:17

commit v2 on v1

--- a/solution.py
+++ b/solution.py
@@ -40,7 +40,7 @@
 
 def whiten(records, groups):
     dft_table = dft_columns(records.shape[2], BINS, groups)
-    spectra = jnp.einsum("swn,nk->swk", records, dft_table, precision=lax.Precision.HIGHEST)
+    spectra = jnp.einsum("swn,nk->swk", records, dft_table, precision=lax.Precision.HIGH)
     mean_power = jnp.mean(spectra * spectra, axis=2, keepdims=True)
     white = (spectra / jnp.sqrt(mean_power + 1e-06)).astype(jnp.bfloat16)
     return white.reshape(1, records.shape[0], records.shape[1], groups, 2 * (BINS // groups))

time: 65.8 us -> 62.7 us (0.953)
  matrix products: 13.4 us -> 10.1 us
    dot_general x1, matrix products: 13.4 us -> 10.1 us  [whiten(): jnp.einsum('swn,nk->swk', records, dft_table, precision=lax.Precision.HIGH)]
where the time goes in v2:
time: 62.7 us; the launch traced here: 62.3 us
  waiting for transfers between devices  15.4 us (25%)
  starting transfers between devices  14.2 us (23%)
  local copies, waits for them, and re-layouts  10.5 us (17%)
  matrix products  10.1 us (16%)
  other arithmetic  5.84 us (9%)
  Pallas kernels  5.4 us (9%)
  between operations  0.89 us (1%)
    ppermute x4, waiting for transfers between devices, passed_along(): return lax.ppermute(array, axis, pairs)  10.5 us
    dot_general x1, matrix products, whiten(): jnp.einsum('swn,nk->swk', records, dft_table, precision=lax.Precision.HIGH)  10.1 us
    ppermute x4, starting transfers between devices, passed_along(): return lax.ppermute(array, axis, pairs)  8.82 us
    unnamed x14, local copies, waits for them, and re-layouts  5.7 us
    pallas_call x1, Pallas kernels, cross_block(): pl.pallas_call(kernel, grid=(nb // step,), in_specs=[pl.BlockSpec((step,...  5.4 us
    all_to_all x1, starting transfers between devices, body(): lax.all_to_all(own_spec, 'tm', split_axis=3, concat_axis=2, tiled=True)  5.35 us
    all_to_all x1, waiting for transfers between devices, body(): lax.all_to_all(own_spec, 'tm', split_axis=3, concat_axis=2, tiled=True)  4.86 us
    select_n x1, other arithmetic, body(): jnp.where(live_slots[None, :, None, None], chosen, jnp.zeros((), chosen.d...  1.56 us
  transfers between devices with their start and end apart: 5, of which 3 were waited for; matrix products, arithmetic and copies ran while one was open for 6% of the time, Pallas kernels for 0%

profile of v2, /device:TPU:0, one launch (start us, length us, event | category | flops | bytes accessed | tf_op | source)
XLA Modules:
  0.0 62.3 jit_solution(17643177599367666306)
XLA Ops:
  0.0 0.6 fusion.17
  0.6 1.2 %multiply_subtract_fusion = (f32[64,64,256]{2,1,0:T(8,128)S(1)}, f32[64,64,256]{2,1,0:T(8,128)S(1)}) fusion(f32[64,256]{1,0:T(8,128)S(1)} %get-tuple-element.11, f32[64,256]{1,0:T(8,128)S(1)} %get-tuple-element.10, f32[64,256]{1,0:T(8,128)S(1)} %get-tuple-element.12, f32[64,256]{1,0:T(8,128)S(1)} %get-tuple-element.9), kind=kLoop, calls=%fused_computation.6 | loop fusion | flops 7340032 | bytes 8650752 | tf_op jit(solution)/shard_map/sub | solution.py:35
  1.8 1.1 %bitcast_select_fusion = f32[4096,256]{1,0:T(8,128)S(1)} fusion(f32[64,64,256]{2,1,0:T(8,128)S(1)} %get-tuple-element.8, f32[64,64,256]{2,1,0:T(8,128)S(1)} %get-tuple-element.7, pred[256]{0:T(512)(128)(4,1)S(1)} %fusion.25), kind=kLoop, calls=%fused_computation.4 | loop fusion | flops 1048576 | bytes 12583168 | tf_op jit(solution)/shard_map/jit(_where)/select_n | solution.py:37
  2.9 1.1 %slice-done.1 = s8[4194304]{0:T(1024)(128)(4,1)S(1)} async-done(((s8[10485760]{0:T(1024)(128)(4,1)}), s8[4194304]{0:T(1024)(128)(4,1)S(1)}, s32[]{:S(2)}) %slice-start.1) | async-done | bytes 4194328
  4.0 0.8 %slice-done.2 = s8[2097152]{0:T(1024)(128)(4,1)S(1)} async-done(((s8[10485760]{0:T(1024)(128)(4,1)}), s8[2097152]{0:T(1024)(128)(4,1)S(1)}, s32[]{:S(2)}) %slice-start.2) | async-done | bytes 2097176
  4.9 10.1 %multiply_reduce_fusion = (f32[40,16]{0,1:T(8,128)S(1)}, f32[256,40,16]{0,1,2:T(8,128)S(1)}) fusion(f32[40,16,4096]{2,1,0:T(8,128)S(1)} %bitcast.51, f32[4096,256]{1,0:T(8,128)S(1)} %bitcast_select_fusion), kind=kOutput, calls=%fused_computation.11 | convolution fusion | flops 4026859008 | bytes 15337984 | tf_op jit(solution)/shard_map/swn,nk->swk/dot_general | solution.py:43
  15.0 0.2 fusion.4
  15.2 0.3 reshape.254
  15.5 0.3 copy.22
  15.8 1.2 %reshape.266 = bf16[4,2,20480]{2,1,0:T(2,128)(2,1)} reshape(bf16[4,1,40,16,64]{4,3,2,1,0:T(8,128)(2,1)S(1)} %bitcast.49) | data formatting | bytes 655360
  17.0 5.3 %all-to-all-start = ((bf16[4,2,20480]{2,1,0:T(2,128)(2,1)}), bf16[4,2,20480]{2,1,0:T(2,128)(2,1)S(1)}, u32[]{:S(2)}, u32[]{:S(2)}) async-start(bf16[4,2,20480]{2,1,0:T(2,128)(2,1)} %reshape.266), calls=%async_computation | async-start | bytes 655360 | tf_op jit(solution)/shard_map/all_to_all | solution.py:88
  23.4 4.9 %all-to-all-done = bf16[4,2,20480]{2,1,0:T(2,128)(2,1)S(1)} async-done(((bf16[4,2,20480]{2,1,0:T(2,128)(2,1)}), bf16[4,2,20480]{2,1,0:T(2,128)(2,1)S(1)}, u32[]{:S(2)}, u32[]{:S(2)}) %all-to-all-start) | async-done | bytes 327712 | tf_op jit(solution)/shard_map/all_to_all | solution.py:88
  28.2 0.4 reshape.267
  28.6 0.1 bitcast_bitcast_fusion
  28.8 0.8 %copy.13 = bf16[1,40,4,16,1,64]{1,5,3,2,4,0:T(8,128)(2,1)S(1)} copy(bf16[1,40,4,16,1,64]{5,3,1,2,4,0:T(8,128)(2,1)S(1)} %bitcast_bitcast_fusion) | data formatting | bytes 655360 | tf_op jit(solution)/shard_map/all_to_all | solution.py:88
  29.6 1.3 %copy.14 = bf16[32,40,2,64]{3,2,1,0:T(2,128)(2,1)S(1)} copy(bf16[32,40,2,64]{1,0,2,3:T(8,128)(2,1)S(1)} %bitcast.48) | data formatting | bytes 655360 | tf_op jit(solution)/shard_map/transpose | solution.py:93
  30.9 0.3 reshape.256
  31.2 4.2 %collective-permute-start = (bf16[32,40,128]{2,1,0:T(8,128)(2,1)S(1)}, bf16[32,40,128]{2,1,0:T(8,128)(2,1)}, u32[]{:S(2)}, u32[]{:S(2)}) collective-permute-start(bf16[32,40,128]{2,1,0:T(8,128)(2,1)S(1)} %reshape.256), channel_id=1, source_target_pairs={{0,2},{1,3},{2,4},{3,5},{4,6},{5,7},{8,10},{9,11},{10,12},{11,13},... | collective-permute-start | bytes 983048 | tf_op jit(solution)/shard_map/ppermute | solution.py:17
  35.4 2.0 %collective-permute-start.1 = (bf16[32,40,128]{2,1,0:T(8,128)(2,1)S(1)}, bf16[32,40,128]{2,1,0:T(8,128)(2,1)}, u32[]{:S(2)}, u32[]{:S(2)}) collective-permute-start(bf16[32,40,128]{2,1,0:T(8,128)(2,1)S(1)} %reshape.256), channel_id=1, source_target_pairs={{0,1},{1,2},{2,3},{3,4},{4,5},{5,6},{6,7},{8,9},{9,10},{10,11},{11... | collective-permute-start | bytes 983048 | tf_op jit(solution)/shard_map/ppermute | solution.py:17
  37.4 0.3 stack_reshape.3
  37.7 1.3 %collective-permute-start.2 = (bf16[32,40,128]{2,1,0:T(8,128)(2,1)S(1)}, bf16[32,40,128]{2,1,0:T(8,128)(2,1)S(1)}, u32[]{:S(2)}, u32[]{:S(2)}) collective-permute-start(bf16[32,40,128]{2,1,0:T(8,128)(2,1)S(1)} %reshape.256), channel_id=1, source_target_pairs={{1,0},{2,1},{3,2},{4,3},{5,4},{6,5},{7,6},{9,8},{10,9},{11,10},{12... | collective-permute-start | bytes 983048 | tf_op jit(solution)/shard_map/ppermute | solution.py:17
  39.0 1.3 %collective-permute-start.3 = (bf16[32,40,128]{2,1,0:T(8,128)(2,1)S(1)}, bf16[32,40,128]{2,1,0:T(8,128)(2,1)S(1)}, u32[]{:S(2)}, u32[]{:S(2)}) collective-permute-start(bf16[32,40,128]{2,1,0:T(8,128)(2,1)S(1)} %reshape.256), channel_id=1, source_target_pairs={{2,0},{3,1},{4,2},{5,3},{6,4},{7,5},{10,8},{11,9},{12,10},{13,11},... | collective-permute-start | bytes 983048 | tf_op jit(solution)/shard_map/ppermute | solution.py:17
  40.3 0.2 slice_negate_fusion
  40.4 1.0 %maximum_maximum_fusion.refs_0_ = bf16[32,80,128]{2,1,0:T(8,128)(2,1)} fusion(bf16[32,40,64]{2,1,0:T(8,128)(2,1)S(1)} %get-tuple-element.6, bf16[32,40,64]{2,1,0:T(8,128)(2,1)S(1)} %get-tuple-element.5, bf16[32,40,128]{2,1,0:T(8,128)(2,1)S(1)} %reshape.256), kind=kLoop, calls=%fused_computation.9 | loop fusion | flops 1966080 | bytes 1310720 | tf_op jit(solution)/shard_map/concatenate | solution.py:106
  41.5 0.6 collective-permute-done
  42.1 1.0 %bitcast_dynamic-update-slice_fusion.3 = bf16[32,5,40,128]{3,2,0,1:T(8,128)(2,1)S(1)} fusion(bf16[32,40,128]{2,1,0:T(8,128)(2,1)} %collective-permute-done), kind=kLoop, calls=%fused_computation.16 | loop fusion | bytes 655360
  43.1 1.0 %bitcast_dynamic-update-slice_fusion.2 = bf16[32,5,40,128]{3,2,0,1:T(8,128)(2,1)S(1)} fusion(bf16[32,5,40,128]{3,2,0,1:T(8,128)(2,1)S(1)} %bitcast_dynamic-update-slice_fusion.3, bf16[32,40,128]{2,1,0:T(8,128)(2,1)} %collective-permute-done.1), kind=kLoop, calls=%fused_computation.15 | loop fusion | bytes 655360
  44.2 9.9 %collective-permute-done.3 = bf16[32,40,128]{2,1,0:T(8,128)(2,1)S(1)} collective-permute-done((bf16[32,40,128]{2,1,0:T(8,128)(2,1)S(1)}, bf16[32,40,128]{2,1,0:T(8,128)(2,1)S(1)}, u32[]{:S(2)}, u32[]{:S(2)}) %collective-permute-start.3) | collective-permute-done | bytes 327712 | tf_op jit(solution)/shard_map/ppermute | solution.py:17
  54.2 0.9 %gather_fusion = bf16[5,32,40,128]{3,2,1,0:T(8,128)(2,1)S(1)} fusion(bf16[32,5,40,128]{3,2,0,1:T(8,128)(2,1)S(1)} %bitcast_dynamic-update-slice_fusion, s32[1024]{0:T(1024)S(1)} %pad_clamp_fusion), kind=kCustom, calls=%fused_computation | custom fusion | bytes 3276820 | tf_op jit(solution)/shard_map/jit(_take)/gather | solution.py:101
  55.1 0.3 copy.16
  55.4 1.6 %fusion.3.refs_1_ = bf16[32,200,128]{2,1,0:T(8,128)(2,1)} fusion(bf16[32,5,40,128]{3,2,1,0:T(8,128)(2,1)S(1)} %copy.16, pred[200]{0:T(512)(128)(4,1)S(1)} %broadcast_in_dim.57, pred[200]{0:T(512)(128)(4,1)S(1)} %broadcast_in_dim.54), kind=kLoop, calls=%fused_computation.8 | loop fusion | flops 1638400 | bytes 3277200 | tf_op jit(solution)/shard_map/jit(_where)/select_n | solution.py:102
  56.9 5.4 %shard_map.37 = f32[5,40,2560]{2,1,0:T(8,128)} custom-call(bf16[32,80,128]{2,1,0:T(8,128)(2,1)} %maximum_maximum_fusion.refs_0_, bf16[32,200,128]{2,1,0:T(8,128)(2,1)} %fusion.3.refs_1_), custom_call_target="tpu_custom_call" | custom-call | tf_op jit(solution)/shard_map/pallas_call | solution.py:70
  (24 shorter events, 0.6 us)
Async XLA Ops:
  0.6 2.4 %slice-start = ((s8[10485760]{0:T(1024)(128)(4,1)}), s8[4194304]{0:T(1024)(128)(4,1)S(1)}, s32[]{:S(2)}) async-start(s8[10485760]{0:T(1024)(128)(4,1)} %bitcast.50), calls=%async_computation.1 | async-start | bytes 8388608
  0.6 3.5 %slice-start.1 = ((s8[10485760]{0:T(1024)(128)(4,1)}), s8[4194304]{0:T(1024)(128)(4,1)S(1)}, s32[]{:S(2)}) async-start(s8[10485760]{0:T(1024)(128)(4,1)} %bitcast.50), calls=%async_computation.2 | async-start | bytes 8388608
  1.8 3.1 %slice-start.2 = ((s8[10485760]{0:T(1024)(128)(4,1)}), s8[2097152]{0:T(1024)(128)(4,1)S(1)}, s32[]{:S(2)}) async-start(s8[10485760]{0:T(1024)(128)(4,1)} %bitcast.50), calls=%async_computation.3 | async-start | bytes 4194304
  15.5 6.8 %copy-start = (s32[1,5]{1,0:T(1,128)S(1)}, s32[1,5]{1,0:T(1,128)}, u32[]{:S(2)}) copy-start(s32[1,5]{1,0:T(1,128)} %param.4) | copy-start | bytes 64
  17.0 11.2 %all-to-all-start = ((bf16[4,2,20480]{2,1,0:T(2,128)(2,1)}), bf16[4,2,20480]{2,1,0:T(2,128)(2,1)S(1)}, u32[]{:S(2)}, u32[]{:S(2)}) async-start(bf16[4,2,20480]{2,1,0:T(2,128)(2,1)} %reshape.266), calls=%async_computation | async-start | bytes 655360 | tf_op jit(solution)/shard_map/all_to_all | solution.py:88
  31.2 10.9 %collective-permute-start = (bf16[32,40,128]{2,1,0:T(8,128)(2,1)S(1)}, bf16[32,40,128]{2,1,0:T(8,128)(2,1)}, u32[]{:S(2)}, u32[]{:S(2)}) collective-permute-start(bf16[32,40,128]{2,1,0:T(8,128)(2,1)S(1)} %reshape.256), channel_id=1, source_target_pairs={{0,2},{1,3},{2,4},{3,5},{4,6},{5,7},{8,10},{9,11},{10,12},{11,13},... | collective-permute-start | bytes 983048 | tf_op jit(solution)/shard_map/ppermute | solution.py:17
  35.4 7.7 %collective-permute-start.1 = (bf16[32,40,128]{2,1,0:T(8,128)(2,1)S(1)}, bf16[32,40,128]{2,1,0:T(8,128)(2,1)}, u32[]{:S(2)}, u32[]{:S(2)}) collective-permute-start(bf16[32,40,128]{2,1,0:T(8,128)(2,1)S(1)} %reshape.256), channel_id=1, source_target_pairs={{0,1},{1,2},{2,3},{3,4},{4,5},{5,6},{6,7},{8,9},{9,10},{10,11},{11... | collective-permute-start | bytes 983048 | tf_op jit(solution)/shard_map/ppermute | solution.py:17
  37.7 6.5 %collective-permute-start.2 = (bf16[32,40,128]{2,1,0:T(8,128)(2,1)S(1)}, bf16[32,40,128]{2,1,0:T(8,128)(2,1)S(1)}, u32[]{:S(2)}, u32[]{:S(2)}) collective-permute-start(bf16[32,40,128]{2,1,0:T(8,128)(2,1)S(1)} %reshape.256), channel_id=1, source_target_pairs={{1,0},{2,1},{3,2},{4,3},{5,4},{6,5},{7,6},{9,8},{10,9},{11,10},{12... | collective-permute-start | bytes 983048 | tf_op jit(solution)/shard_map/ppermute | solution.py:17
  39.0 15.2 %collective-permute-start.3 = (bf16[32,40,128]{2,1,0:T(8,128)(2,1)S(1)}, bf16[32,40,128]{2,1,0:T(8,128)(2,1)S(1)}, u32[]{:S(2)}, u32[]{:S(2)}) collective-permute-start(bf16[32,40,128]{2,1,0:T(8,128)(2,1)S(1)} %reshape.256), channel_id=1, source_target_pairs={{2,0},{3,1},{4,2},{5,3},{6,4},{7,5},{10,8},{11,9},{12,10},{13,11},... | collective-permute-start | bytes 983048 | tf_op jit(solution)/shard_map/ppermute | solution.py:17

commit v3 on v2

--- a/solution.py
+++ b/solution.py
@@ -85,7 +85,17 @@
     partner_row = partners[0]
     slots = partner_row.shape[0]
     live_slots = jnp.arange(slots, dtype=jnp.int32) < counts[0]
-    regrouped = lax.all_to_all(own_spec, "tm", split_axis=3, concat_axis=2, tiled=True)
+    groups = lax.axis_size("tm")
+    group_index = lax.axis_index("tm")
+    chunks = []
+    for shift in range(groups):
+        target = (group_index + shift) % groups
+        chunk = lax.dynamic_index_in_dim(own_spec, target, axis=3, keepdims=True)
+        if shift:
+            pairs = [(i, (i + shift) % groups) for i in range(groups)]
+            chunk = lax.ppermute(chunk, "tm", pairs)
+        chunks.append(chunk)
+    regrouped = jnp.concatenate(chunks, axis=2)
     stations, windows, width = regrouped.shape[1], regrouped.shape[2], regrouped.shape[4]
     nb = width // 2
     spec = (

time: 62.7 us -> 64.2 us (1.024)
  waiting for transfers between devices: 15.4 us -> 16.6 us
  other arithmetic: 5.84 us -> 6.69 us
    ppermute x0 -> x3, waiting for transfers between devices: none -> 6.09 us  [body(): chunk = lax.ppermute(chunk, 'tm', pairs)]
    all_to_all x1 -> x0, starting transfers between devices: 5.35 us -> none  [body(): lax.all_to_all(own_spec, 'tm', split_axis=3, concat_axis=2, tiled=True)]
    ppermute x0 -> x3, starting transfers between devices: none -> 5.17 us  [body(): chunk = lax.ppermute(chunk, 'tm', pairs)]
    all_to_all x1 -> x0, waiting for transfers between devices: 4.86 us -> none  [body(): lax.all_to_all(own_spec, 'tm', split_axis=3, concat_axis=2, tiled=True)]
    dynamic_slice x0 -> x1, local copies, waits for them, and re-layouts: none -> 1.54 us  [body(): chunk = lax.dynamic_index_in_dim(own_spec, target, axis=3, keepdims=True)]
    ppermute x0 -> x3, local copies, waits for them, and re-layouts: none -> 0.97 us  [body(): chunk = lax.ppermute(chunk, 'tm', pairs)]
    unnamed x14 -> x16, local copies, waits for them, and re-layouts: 5.7 us -> 4.76 us
    all_to_all x2 -> x0, local copies, waits for them, and re-layouts: 0.9 us -> none  [body(): lax.all_to_all(own_spec, 'tm', split_axis=3, concat_axis=2, tiled=True)]
  transfers between devices with their start and end apart: 5 -> 7, of which waited for: 3 -> 3; matrix products, arithmetic and copies ran while one was open for 6% -> 8% of each run, Pallas kernels for 0% -> 0%
where the time goes in v3:
time: 64.2 us; the launch traced here: 63.8 us
  waiting for transfers between devices  16.6 us (26%)
  starting transfers between devices  14 us (22%)
  local copies, waits for them, and re-layouts  10.2 us (16%)
  matrix products  10 us (16%)
  other arithmetic  6.69 us (10%)
  Pallas kernels  5.39 us (8%)
  between operations  0.99 us (2%)
    ppermute x4, waiting for transfers between devices, passed_along(): return lax.ppermute(array, axis, pairs)  10.5 us
    dot_general x1, matrix products, whiten(): jnp.einsum('swn,nk->swk', records, dft_table, precision=lax.Precision.HIGH)  10 us
    ppermute x4, starting transfers between devices, passed_along(): return lax.ppermute(array, axis, pairs)  8.81 us
    ppermute x3, waiting for transfers between devices, body(): chunk = lax.ppermute(chunk, 'tm', pairs)  6.09 us
    pallas_call x1, Pallas kernels, cross_block(): pl.pallas_call(kernel, grid=(nb // step,), in_specs=[pl.BlockSpec((step,...  5.39 us
    ppermute x3, starting transfers between devices, body(): chunk = lax.ppermute(chunk, 'tm', pairs)  5.17 us
    unnamed x16, local copies, waits for them, and re-layouts  4.76 us
    select_n x1, other arithmetic, body(): jnp.where(live_slots[None, :, None, None], chosen, jnp.zeros((), chosen.d...  1.57 us
  transfers between devices with their start and end apart: 7, of which 3 were waited for; matrix products, arithmetic and copies ran while one was open for 8% of the time, Pallas kernels for 0%

profile of v3, /device:TPU:0, one launch (start us, length us, event | category | flops | bytes accessed | tf_op | source)
XLA Modules:
  0.0 63.8 jit_solution(2777298014835881119)
XLA Ops:
  0.1 0.6 fusion.17
  0.6 1.2 %multiply_subtract_fusion = (f32[64,64,256]{2,1,0:T(8,128)S(1)}, f32[64,64,256]{2,1,0:T(8,128)S(1)}) fusion(f32[64,256]{1,0:T(8,128)S(1)} %get-tuple-element.15, f32[64,256]{1,0:T(8,128)S(1)} %get-tuple-element.14, f32[64,256]{1,0:T(8,128)S(1)} %get-tuple-element.16, f32[64,256]{1,0:T(8,128)S(1)} %get-tuple-element.13), kind=kLoop, calls=%fused_computation.6 | loop fusion | flops 7340032 | bytes 8650752 | tf_op jit(solution)/shard_map/sub | solution.py:35
  1.8 1.1 %bitcast_select_fusion = f32[4096,256]{1,0:T(8,128)S(1)} fusion(f32[64,64,256]{2,1,0:T(8,128)S(1)} %get-tuple-element.12, f32[64,64,256]{2,1,0:T(8,128)S(1)} %get-tuple-element.11, pred[256]{0:T(512)(128)(4,1)S(1)} %fusion.25), kind=kLoop, calls=%fused_computation.4 | loop fusion | flops 1048576 | bytes 12583168 | tf_op jit(solution)/shard_map/jit(_where)/select_n | solution.py:37
  3.0 1.1 %slice-done.1 = s8[4194304]{0:T(1024)(128)(4,1)S(1)} async-done(((s8[10485760]{0:T(1024)(128)(4,1)}), s8[4194304]{0:T(1024)(128)(4,1)S(1)}, s32[]{:S(2)}) %slice-start.1) | async-done | bytes 4194328
  4.1 0.8 %slice-done.2 = s8[2097152]{0:T(1024)(128)(4,1)S(1)} async-done(((s8[10485760]{0:T(1024)(128)(4,1)}), s8[2097152]{0:T(1024)(128)(4,1)S(1)}, s32[]{:S(2)}) %slice-start.2) | async-done | bytes 2097176
  4.9 10.0 %multiply_reduce_fusion = (f32[40,16]{0,1:T(8,128)S(1)}, f32[256,40,16]{0,1,2:T(8,128)S(1)}) fusion(f32[40,16,4096]{2,1,0:T(8,128)S(1)} %bitcast.41, f32[4096,256]{1,0:T(8,128)S(1)} %bitcast_select_fusion), kind=kOutput, calls=%fused_computation.12 | convolution fusion | flops 4026859008 | bytes 15337984 | tf_op jit(solution)/shard_map/swn,nk->swk/dot_general | solution.py:43
  15.1 0.3 reshape.253
  15.4 1.5 %constant_dynamic-slice_fusion.3 = (bf16[1,40,16,1,64]{4,3,1,2,0:T(2,128)(2,1)S(1)}, bf16[1,40,16,1,64]{4,3,1,2,0:T(2,128)(2,1)S(1)}, bf16[1,40,16,1,64]{4,3,1,2,0:T(2,128)(2,1)S(1)}, bf16[1,40,16,1,64]{4,3,1,2,0:T(2,128)(2,1)S(1)}) fusion(bf16[1,40,16,4,64]{4,3,1,2,0:T(4,128)(2,1)S(1)} %reshape.253, s32[]{:T(128)S(6)} %select_n.129, s32[]{:T(128)S(6)} %select_n.131, ...), kind=kLoop, calls=%fused_computation.68 | loop fusion | bytes 655376 | tf_op jit(solution)/shard_map/jit(dynamic_index_in_dim)/dynamic_slice | solution.py:93
  17.1 4.0 %collective-permute-start.2 = (bf16[1,40,16,1,64]{4,2,3,1,0:T(8,128)(2,1)S(1)}, bf16[1,40,16,1,64]{4,2,3,1,0:T(8,128)(2,1)S(1)}, u32[]{:S(2)}, u32[]{:S(2)}) collective-permute-start(bf16[1,40,16,1,64]{4,2,3,1,0:T(8,128)(2,1)S(1)} %copy.28), channel_id=1, source_target_pairs={{0,24},{8,0},{16,8},{24,16},{1,25},{9,1},{17,9},{25,17},{2,26},{10... | collective-permute-start | bytes 245768 | tf_op jit(solution)/shard_map/ppermute | solution.py:96
  21.1 0.6 collective-permute-start.1
  21.7 0.6 %collective-permute-start = (bf16[1,40,16,1,64]{4,2,3,1,0:T(8,128)(2,1)S(1)}, bf16[1,40,16,1,64]{4,2,3,1,0:T(8,128)(2,1)S(1)}, u32[]{:S(2)}, u32[]{:S(2)}) collective-permute-start(bf16[1,40,16,1,64]{4,2,3,1,0:T(8,128)(2,1)S(1)} %copy.26), channel_id=1, source_target_pairs={{0,8},{8,16},{16,24},{24,0},{1,9},{9,17},{17,25},{25,1},{2,10},{10... | collective-permute-start | bytes 245768 | tf_op jit(solution)/shard_map/ppermute | solution.py:96
  22.4 0.5 copy.25
  23.9 1.7 %collective-permute-done.2 = bf16[1,40,16,1,64]{4,2,3,1,0:T(8,128)(2,1)S(1)} collective-permute-done((bf16[1,40,16,1,64]{4,2,3,1,0:T(8,128)(2,1)S(1)}, bf16[1,40,16,1,64]{4,2,3,1,0:T(8,128)(2,1)S(1)}, u32[]{:S(2)}, u32[]{:S(2)}) %collective-permute-start.2) | collective-permute-done | bytes 81952 | tf_op jit(solution)/shard_map/ppermute | solution.py:96
  25.6 0.3 copy.21
  25.9 4.4 %collective-permute-done.1 = bf16[1,40,16,1,64]{4,2,3,1,0:T(8,128)(2,1)S(1)} collective-permute-done((bf16[1,40,16,1,64]{4,2,3,1,0:T(8,128)(2,1)S(1)}, bf16[1,40,16,1,64]{4,2,3,1,0:T(8,128)(2,1)S(1)}, u32[]{:S(2)}, u32[]{:S(2)}) %collective-permute-start.1) | collective-permute-done | bytes 81952 | tf_op jit(solution)/shard_map/ppermute | solution.py:96
  30.3 0.3 copy.20
  30.7 0.3 copy.19
  31.0 0.9 %pad_maximum_fusion = bf16[1,40,64,1,64]{2,4,1,3,0:T(8,128)(2,1)S(1)} fusion(bf16[1,40,16,1,64]{2,4,1,3,0:T(8,128)(2,1)S(1)} %copy.21, bf16[1,40,16,1,64]{2,4,1,3,0:T(8,128)(2,1)S(1)} %copy.20, bf16[1,40,16,1,64]{2,4,1,3,0:T(8,128)(2,1)S(1)} %copy.19, bf16[1,40,16,1,64]{2,4,1,3,0:T(8,128)(2,1)S(1)} %copy.25), kind=kLoop, calls=%fused_computation.9 | loop fusion | flops 1310720 | bytes 655360 | tf_op jit(solution)/shard_map/concatenate | solution.py:98
  31.8 0.5 copy.22
  32.4 0.3 reshape.255
  32.6 4.2 %collective-permute-start.3 = (bf16[32,40,128]{2,1,0:T(8,128)(2,1)S(1)}, bf16[32,40,128]{2,1,0:T(8,128)(2,1)}, u32[]{:S(2)}, u32[]{:S(2)}) collective-permute-start(bf16[32,40,128]{2,1,0:T(8,128)(2,1)S(1)} %reshape.255), channel_id=1, source_target_pairs={{0,2},{1,3},{2,4},{3,5},{4,6},{5,7},{8,10},{9,11},{10,12},{11,13},... | collective-permute-start | bytes 983048 | tf_op jit(solution)/shard_map/ppermute | solution.py:17
  36.9 2.0 %collective-permute-start.4 = (bf16[32,40,128]{2,1,0:T(8,128)(2,1)S(1)}, bf16[32,40,128]{2,1,0:T(8,128)(2,1)}, u32[]{:S(2)}, u32[]{:S(2)}) collective-permute-start(bf16[32,40,128]{2,1,0:T(8,128)(2,1)S(1)} %reshape.255), channel_id=1, source_target_pairs={{0,1},{1,2},{2,3},{3,4},{4,5},{5,6},{6,7},{8,9},{9,10},{10,11},{11... | collective-permute-start | bytes 983048 | tf_op jit(solution)/shard_map/ppermute | solution.py:17
  38.9 0.3 stack_reshape.3
  39.2 1.3 %collective-permute-start.5 = (bf16[32,40,128]{2,1,0:T(8,128)(2,1)S(1)}, bf16[32,40,128]{2,1,0:T(8,128)(2,1)S(1)}, u32[]{:S(2)}, u32[]{:S(2)}) collective-permute-start(bf16[32,40,128]{2,1,0:T(8,128)(2,1)S(1)} %reshape.255), channel_id=1, source_target_pairs={{1,0},{2,1},{3,2},{4,3},{5,4},{6,5},{7,6},{9,8},{10,9},{11,10},{12... | collective-permute-start | bytes 983048 | tf_op jit(solution)/shard_map/ppermute | solution.py:17
  40.5 1.3 %collective-permute-start.6 = (bf16[32,40,128]{2,1,0:T(8,128)(2,1)S(1)}, bf16[32,40,128]{2,1,0:T(8,128)(2,1)S(1)}, u32[]{:S(2)}, u32[]{:S(2)}) collective-permute-start(bf16[32,40,128]{2,1,0:T(8,128)(2,1)S(1)} %reshape.255), channel_id=1, source_target_pairs={{2,0},{3,1},{4,2},{5,3},{6,4},{7,5},{10,8},{11,9},{12,10},{13,11},... | collective-permute-start | bytes 983048 | tf_op jit(solution)/shard_map/ppermute | solution.py:17
  41.9 1.0 %maximum_maximum_fusion.refs_0_ = bf16[32,80,128]{2,1,0:T(8,128)(2,1)} fusion(bf16[32,40,64]{2,1,0:T(8,128)(2,1)S(1)} %get-tuple-element.10, bf16[32,40,64]{2,1,0:T(8,128)(2,1)S(1)} %get-tuple-element.9, bf16[32,40,128]{2,1,0:T(8,128)(2,1)S(1)} %reshape.255), kind=kLoop, calls=%fused_computation.10 | loop fusion | flops 1966080 | bytes 1310720 | tf_op jit(solution)/shard_map/concatenate | solution.py:116
  43.0 1.0 %bitcast_dynamic-update-slice_fusion.3 = bf16[32,5,40,128]{3,2,0,1:T(8,128)(2,1)S(1)} fusion(bf16[32,40,128]{2,1,0:T(8,128)(2,1)} %collective-permute-done.3), kind=kLoop, calls=%fused_computation.17 | loop fusion | bytes 655360
  44.0 1.0 %bitcast_dynamic-update-slice_fusion.2 = bf16[32,5,40,128]{3,2,0,1:T(8,128)(2,1)S(1)} fusion(bf16[32,5,40,128]{3,2,0,1:T(8,128)(2,1)S(1)} %bitcast_dynamic-update-slice_fusion.3, bf16[32,40,128]{2,1,0:T(8,128)(2,1)} %collective-permute-done.4), kind=kLoop, calls=%fused_computation.16 | loop fusion | bytes 655360
  45.1 10.5 %collective-permute-done.6 = bf16[32,40,128]{2,1,0:T(8,128)(2,1)S(1)} collective-permute-done((bf16[32,40,128]{2,1,0:T(8,128)(2,1)S(1)}, bf16[32,40,128]{2,1,0:T(8,128)(2,1)S(1)}, u32[]{:S(2)}, u32[]{:S(2)}) %collective-permute-start.6) | collective-permute-done | bytes 327712 | tf_op jit(solution)/shard_map/ppermute | solution.py:17
  55.7 0.9 %gather_fusion = bf16[5,32,40,128]{3,2,1,0:T(8,128)(2,1)S(1)} fusion(bf16[32,5,40,128]{3,2,0,1:T(8,128)(2,1)S(1)} %bitcast_dynamic-update-slice_fusion, s32[1024]{0:T(1024)S(1)} %pad_clamp_fusion), kind=kCustom, calls=%fused_computation | custom fusion | bytes 3276820 | tf_op jit(solution)/shard_map/jit(_take)/gather | solution.py:111
  56.9 1.6 %fusion.3.refs_1_ = bf16[32,200,128]{2,1,0:T(8,128)(2,1)} fusion(bf16[32,5,40,128]{3,2,1,0:T(8,128)(2,1)S(1)} %copy.24, pred[200]{0:T(512)(128)(4,1)S(1)} %broadcast_in_dim.57, pred[200]{0:T(512)(128)(4,1)S(1)} %broadcast_in_dim.54), kind=kLoop, calls=%fused_computation.8 | loop fusion | flops 1638400 | bytes 3277200 | tf_op jit(solution)/shard_map/jit(_where)/select_n | solution.py:112
  58.4 5.4 %shard_map.37 = f32[5,40,2560]{2,1,0:T(8,128)} custom-call(bf16[32,80,128]{2,1,0:T(8,128)(2,1)} %maximum_maximum_fusion.refs_0_, bf16[32,200,128]{2,1,0:T(8,128)(2,1)} %fusion.3.refs_1_), custom_call_target="tpu_custom_call" | custom-call | tf_op jit(solution)/shard_map/pallas_call | solution.py:70
  (32 shorter events, 1.4 us)
Async XLA Ops:
  0.6 2.4 %slice-start = ((s8[10485760]{0:T(1024)(128)(4,1)}), s8[4194304]{0:T(1024)(128)(4,1)S(1)}, s32[]{:S(2)}) async-start(s8[10485760]{0:T(1024)(128)(4,1)} %bitcast.40), calls=%async_computation | async-start | bytes 8388608
  0.6 3.5 %slice-start.1 = ((s8[10485760]{0:T(1024)(128)(4,1)}), s8[4194304]{0:T(1024)(128)(4,1)S(1)}, s32[]{:S(2)}) async-start(s8[10485760]{0:T(1024)(128)(4,1)} %bitcast.40), calls=%async_computation.1 | async-start | bytes 8388608
  1.8 3.1 %slice-start.2 = ((s8[10485760]{0:T(1024)(128)(4,1)}), s8[2097152]{0:T(1024)(128)(4,1)S(1)}, s32[]{:S(2)}) async-start(s8[10485760]{0:T(1024)(128)(4,1)} %bitcast.40), calls=%async_computation.2 | async-start | bytes 4194304
  15.4 6.9 %copy-start = (s32[1,5]{1,0:T(1,128)S(1)}, s32[1,5]{1,0:T(1,128)}, u32[]{:S(2)}) copy-start(s32[1,5]{1,0:T(1,128)} %param.4) | copy-start | bytes 64
  17.1 8.6 %collective-permute-start.2 = (bf16[1,40,16,1,64]{4,2,3,1,0:T(8,128)(2,1)S(1)}, bf16[1,40,16,1,64]{4,2,3,1,0:T(8,128)(2,1)S(1)}, u32[]{:S(2)}, u32[]{:S(2)}) collective-permute-start(bf16[1,40,16,1,64]{4,2,3,1,0:T(8,128)(2,1)S(1)} %copy.28), channel_id=1, source_target_pairs={{0,24},{8,0},{16,8},{24,16},{1,25},{9,1},{17,9},{25,17},{2,26},{10... | collective-permute-start | bytes 245768 | tf_op jit(solution)/shard_map/ppermute | solution.py:96
  21.1 9.2 %collective-permute-start.1 = (bf16[1,40,16,1,64]{4,2,3,1,0:T(8,128)(2,1)S(1)}, bf16[1,40,16,1,64]{4,2,3,1,0:T(8,128)(2,1)S(1)}, u32[]{:S(2)}, u32[]{:S(2)}) collective-permute-start(bf16[1,40,16,1,64]{4,2,3,1,0:T(8,128)(2,1)S(1)} %copy.27), channel_id=1, source_target_pairs={{0,16},{8,24},{16,0},{24,8},{1,17},{9,25},{17,1},{25,9},{2,18},{10... | collective-permute-start | bytes 245768 | tf_op jit(solution)/shard_map/ppermute | solution.py:96
  21.7 8.9 %collective-permute-start = (bf16[1,40,16,1,64]{4,2,3,1,0:T(8,128)(2,1)S(1)}, bf16[1,40,16,1,64]{4,2,3,1,0:T(8,128)(2,1)S(1)}, u32[]{:S(2)}, u32[]{:S(2)}) collective-permute-start(bf16[1,40,16,1,64]{4,2,3,1,0:T(8,128)(2,1)S(1)} %copy.26), channel_id=1, source_target_pairs={{0,8},{8,16},{16,24},{24,0},{1,9},{9,17},{17,25},{25,1},{2,10},{10... | collective-permute-start | bytes 245768 | tf_op jit(solution)/shard_map/ppermute | solution.py:96
  32.6 10.3 %collective-permute-start.3 = (bf16[32,40,128]{2,1,0:T(8,128)(2,1)S(1)}, bf16[32,40,128]{2,1,0:T(8,128)(2,1)}, u32[]{:S(2)}, u32[]{:S(2)}) collective-permute-start(bf16[32,40,128]{2,1,0:T(8,128)(2,1)S(1)} %reshape.255), channel_id=1, source_target_pairs={{0,2},{1,3},{2,4},{3,5},{4,6},{5,7},{8,10},{9,11},{10,12},{11,13},... | collective-permute-start | bytes 983048 | tf_op jit(solution)/shard_map/ppermute | solution.py:17
  36.9 7.1 %collective-permute-start.4 = (bf16[32,40,128]{2,1,0:T(8,128)(2,1)S(1)}, bf16[32,40,128]{2,1,0:T(8,128)(2,1)}, u32[]{:S(2)}, u32[]{:S(2)}) collective-permute-start(bf16[32,40,128]{2,1,0:T(8,128)(2,1)S(1)} %reshape.255), channel_id=1, source_target_pairs={{0,1},{1,2},{2,3},{3,4},{4,5},{5,6},{6,7},{8,9},{9,10},{10,11},{11... | collective-permute-start | bytes 983048 | tf_op jit(solution)/shard_map/ppermute | solution.py:17
  39.2 5.9 %collective-permute-start.5 = (bf16[32,40,128]{2,1,0:T(8,128)(2,1)S(1)}, bf16[32,40,128]{2,1,0:T(8,128)(2,1)S(1)}, u32[]{:S(2)}, u32[]{:S(2)}) collective-permute-start(bf16[32,40,128]{2,1,0:T(8,128)(2,1)S(1)} %reshape.255), channel_id=1, source_target_pairs={{1,0},{2,1},{3,2},{4,3},{5,4},{6,5},{7,6},{9,8},{10,9},{11,10},{12... | collective-permute-start | bytes 983048 | tf_op jit(solution)/shard_map/ppermute | solution.py:17
  40.5 15.2 %collective-permute-start.6 = (bf16[32,40,128]{2,1,0:T(8,128)(2,1)S(1)}, bf16[32,40,128]{2,1,0:T(8,128)(2,1)S(1)}, u32[]{:S(2)}, u32[]{:S(2)}) collective-permute-start(bf16[32,40,128]{2,1,0:T(8,128)(2,1)S(1)} %reshape.255), channel_id=1, source_target_pairs={{2,0},{3,1},{4,2},{5,3},{6,4},{7,5},{10,8},{11,9},{12,10},{13,11},... | collective-permute-start | bytes 983048 | tf_op jit(solution)/shard_map/ppermute | solution.py:17

commit v4 on v2

--- a/solution.py
+++ b/solution.py
@@ -4,6 +4,7 @@
 import jax.numpy as jnp
 from jax import lax
 from jax.experimental import pallas as pl
+from jax.experimental.pallas import tpu as pltpu
 from jax.sharding import PartitionSpec as P
 
 BINS = 128
@@ -46,37 +47,49 @@
     return white.reshape(1, records.shape[0], records.shape[1], groups, 2 * (BINS // groups))
 
 
-def cross_kernel(scale, lx_ref, y_ref, o_ref):
+def cross_kernel(scale, sel_ref, lx_ref, *refs):
+    *y_refs, o_ref = refs
     bins, two_s, _ = lx_ref.shape
     s = two_s // 2
-    slots = y_ref.shape[1] // s
-    for b in range(bins):
-        r = lax.dot_general(
-            lx_ref[b], y_ref[b], (((1,), (1,)), ((), ())), preferred_element_type=jnp.float32
-        )
-        r = r * scale
+    slots = o_ref.shape[0]
+    for j in range(bins // 2):
+        picked = []
         for p in range(slots):
-            for x in range(2):
-                col = (2 * b + x) * s
-                o_ref[p, :, col:col + s] = r[x * s:(x + 1) * s, p * s:(p + 1) * s]
+            y = jnp.zeros(y_refs[0].shape[1:], y_refs[0].dtype)
+            for o, y_ref in enumerate(y_refs):
+                y = jnp.where(sel_ref[p] == o, y_ref[j], y)
+            picked.append(y)
+        ycat = jnp.concatenate(picked, axis=0)
+        for h in range(2):
+            b = 2 * j + h
+            r = lax.dot_general(
+                lx_ref[b], ycat, (((1,), (1,)), ((), ())), preferred_element_type=jnp.float32
+            )
+            r = r * scale
+            for p in range(slots):
+                src = (2 * p + h) * s
+                for x in range(2):
+                    col = (2 * b + x) * s
+                    o_ref[p, :, col:col + s] = r[x * s:(x + 1) * s, src:src + s]
 
 
-def cross_block(lx, ysel, windows):
+def cross_block(sel, lx, ys, windows, slots):
     nb, two_s, k = lx.shape
     s = two_s // 2
-    slots = ysel.shape[1] // s
     step = BINS_PER_STEP
     kernel = lambda *refs: cross_kernel(1.0 / windows, *refs)
+    y_spec = pl.BlockSpec((step // 2, two_s, k), lambda g, sel: (g, 0, 0))
+    grid_spec = pltpu.PrefetchScalarGridSpec(
+        num_scalar_prefetch=1,
+        grid=(nb // step,),
+        in_specs=[pl.BlockSpec((step, two_s, k), lambda g, sel: (g, 0, 0))] + [y_spec] * len(ys),
+        out_specs=pl.BlockSpec((slots, s, step * two_s), lambda g, sel: (0, 0, g)),
+    )
     return pl.pallas_call(
         kernel,
-        grid=(nb // step,),
-        in_specs=[
-            pl.BlockSpec((step, two_s, k), lambda g: (g, 0, 0)),
-            pl.BlockSpec((step, slots * s, k), lambda g: (g, 0, 0)),
-        ],
-        out_specs=pl.BlockSpec((slots, s, step * two_s), lambda g: (0, 0, g)),
+        grid_spec=grid_spec,
         out_shape=jax.ShapeDtypeStruct((slots, s, nb * two_s), jnp.float32),
-    )(lx, ysel)
+    )(sel, lx, *ys)
 
 
 def body(records, partners, counts):
@@ -93,18 +106,16 @@
         .transpose(3, 0, 2, 1)
         .reshape(nb, stations, 2 * windows)
     )
-    pieces = []
+    paired = spec.reshape(nb // 2, 2 * stations, 2 * windows)
+    ys = []
     for offset in range(-R, R + 1):
-        pieces.append(spec if offset == 0 else passed_along(spec, "sta", -offset))
-    stacked = jnp.stack(pieces, axis=1)
+        ys.append(paired if offset == 0 else passed_along(paired, "sta", -offset))
     where_at = jnp.clip(partner_row - block_index + R, 0, 2 * R)
-    chosen = jnp.take(stacked, where_at, axis=1)
-    chosen = jnp.where(live_slots[None, :, None, None], chosen, jnp.zeros((), chosen.dtype))
-    ysel = chosen.reshape(nb, slots * stations, 2 * windows)
+    sel = jnp.where(live_slots, where_at, -1).astype(jnp.int32)
     x_re = spec[:, :, :windows]
     x_im = spec[:, :, windows:]
     lx = jnp.concatenate([spec, jnp.concatenate([-x_im, x_re], axis=2)], axis=1)
-    result = cross_block(lx, ysel, windows)
+    result = cross_block(sel, lx, ys, windows, slots)
     return result[None]
 
 

time: 62.7 us -> 61.6 us (0.982)
  waiting for transfers between devices: 15.4 us -> 18.7 us
  local copies, waits for them, and re-layouts: 10.5 us -> 7.61 us
  starting transfers between devices: 14.2 us -> 12.7 us
  other arithmetic: 5.84 us -> 4.78 us
  Pallas kernels: 5.4 us -> 6.39 us
    ppermute x4, waiting for transfers between devices: 10.5 us -> 14 us  [passed_along(): return lax.ppermute(array, axis, pairs)]
    ppermute x4, starting transfers between devices: 8.82 us -> 7.39 us  [passed_along(): return lax.ppermute(array, axis, pairs)]
    unnamed x14 -> x20, local copies, waits for them, and re-layouts: 5.7 us -> 4.3 us
    gather x2 -> x0, local copies, waits for them, and re-layouts: 1.15 us -> none  [body(): chosen = jnp.take(stacked, where_at, axis=1)]
    select_n x2 -> x1, other arithmetic: 1.57 us -> 0.53 us  [body(): sel = jnp.where(live_slots, where_at, -1).astype(jnp.int32)]
    pallas_call x1, Pallas kernels: 5.4 us -> 6.39 us  [cross_block(): pl.pallas_call(kernel, grid_spec=grid_spec, out_shape=jax.ShapeDtypeStruc...]
  transfers between devices with their start and end apart: 5 -> 5, of which waited for: 3 -> 3; matrix products, arithmetic and copies ran while one was open for 6% -> 3% of each run, Pallas kernels for 0% -> 0%
where the time goes in v4:
time: 61.6 us; the launch traced here: 61.3 us
  waiting for transfers between devices  18.7 us (30%)
  starting transfers between devices  12.7 us (21%)
  matrix products  10.1 us (16%)
  local copies, waits for them, and re-layouts  7.61 us (12%)
  Pallas kernels  6.39 us (10%)
  other arithmetic  4.78 us (8%)
  between operations  0.88 us (1%)
    ppermute x4, waiting for transfers between devices, passed_along(): return lax.ppermute(array, axis, pairs)  14 us
    dot_general x1, matrix products, whiten(): jnp.einsum('swn,nk->swk', records, dft_table, precision=lax.Precision.HIGH)  10.1 us
    ppermute x4, starting transfers between devices, passed_along(): return lax.ppermute(array, axis, pairs)  7.39 us
    pallas_call x1, Pallas kernels, cross_block(): pl.pallas_call(kernel, grid_spec=grid_spec, out_shape=jax.ShapeDtypeStruc...  6.39 us
    all_to_all x1, starting transfers between devices, body(): lax.all_to_all(own_spec, 'tm', split_axis=3, concat_axis=2, tiled=True)  5.35 us
    all_to_all x1, waiting for transfers between devices, body(): lax.all_to_all(own_spec, 'tm', split_axis=3, concat_axis=2, tiled=True)  4.7 us
    unnamed x20, local copies, waits for them, and re-layouts  4.3 us
    transpose x1, local copies, waits for them, and re-layouts, body(): spec = regrouped.reshape(stations, windows, 2, nb).transpose(3, 0, 2, 1)....  1.31 us
  transfers between devices with their start and end apart: 5, of which 3 were waited for; matrix products, arithmetic and copies ran while one was open for 3% of the time, Pallas kernels for 0%

profile of v4, /device:TPU:0, one launch (start us, length us, event | category | flops | bytes accessed | tf_op | source)
XLA Modules:
  0.0 61.3 jit_solution(12036690255714326626)
XLA Ops:
  0.0 0.6 fusion.16
  0.6 0.0 slice-start
  0.6 0.0 slice-start.1
  0.6 1.2 %multiply_subtract_fusion = (f32[64,64,256]{2,1,0:T(8,128)S(1)}, f32[64,64,256]{2,1,0:T(8,128)S(1)}) fusion(f32[64,256]{1,0:T(8,128)S(1)} %get-tuple-element.11, f32[64,256]{1,0:T(8,128)S(1)} %get-tuple-element.10, f32[64,256]{1,0:T(8,128)S(1)} %get-tuple-element.12, f32[64,256]{1,0:T(8,128)S(1)} %get-tuple-element.9), kind=kLoop, calls=%fused_computation.5 | loop fusion | flops 7340032 | bytes 8650752 | tf_op jit(solution)/shard_map/sub | solution.py:36
  1.8 0.0 slice-start.2
  1.8 1.1 %bitcast_select_fusion = f32[4096,256]{1,0:T(8,128)S(1)} fusion(f32[64,64,256]{2,1,0:T(8,128)S(1)} %get-tuple-element.8, f32[64,64,256]{2,1,0:T(8,128)S(1)} %get-tuple-element.7, pred[256]{0:T(512)(128)(4,1)S(1)} %fusion.24), kind=kLoop, calls=%fused_computation.3 | loop fusion | flops 1048576 | bytes 12583168 | tf_op jit(solution)/shard_map/jit(_where)/select_n | solution.py:38
  2.9 1.1 %slice-done.1 = s8[4194304]{0:T(1024)(128)(4,1)S(1)} async-done(((s8[10485760]{0:T(1024)(128)(4,1)}), s8[4194304]{0:T(1024)(128)(4,1)S(1)}, s32[]{:S(2)}) %slice-start.1) | async-done | bytes 4194328
  4.0 0.8 %slice-done.2 = s8[2097152]{0:T(1024)(128)(4,1)S(1)} async-done(((s8[10485760]{0:T(1024)(128)(4,1)}), s8[2097152]{0:T(1024)(128)(4,1)S(1)}, s32[]{:S(2)}) %slice-start.2) | async-done | bytes 2097176
  4.9 10.1 %multiply_reduce_fusion = (f32[40,16]{0,1:T(8,128)S(1)}, f32[256,40,16]{0,1,2:T(8,128)S(1)}) fusion(f32[40,16,4096]{2,1,0:T(8,128)S(1)} %bitcast.33, f32[4096,256]{1,0:T(8,128)S(1)} %bitcast_select_fusion), kind=kOutput, calls=%fused_computation.8 | convolution fusion | flops 4026859008 | bytes 15337984 | tf_op jit(solution)/shard_map/swn,nk->swk/dot_general | solution.py:44
  15.0 0.2 fusion.3
  15.2 0.3 reshape.208
  15.5 0.3 copy.19
  15.8 1.2 %reshape.212 = bf16[4,2,20480]{2,1,0:T(2,128)(2,1)} reshape(bf16[4,1,40,16,64]{4,3,2,1,0:T(8,128)(2,1)S(1)} %bitcast.31) | data formatting | bytes 655360
  17.0 5.3 %all-to-all-start = ((bf16[4,2,20480]{2,1,0:T(2,128)(2,1)}), bf16[4,2,20480]{2,1,0:T(2,128)(2,1)S(1)}, u32[]{:S(2)}, u32[]{:S(2)}) async-start(bf16[4,2,20480]{2,1,0:T(2,128)(2,1)} %reshape.212), calls=%async_computation | async-start | bytes 655360 | tf_op jit(solution)/shard_map/all_to_all | solution.py:101
  23.0 0.5 compare_select_fusion.2.refs_0_
  23.5 4.7 %all-to-all-done = bf16[4,2,20480]{2,1,0:T(2,128)(2,1)S(1)} async-done(((bf16[4,2,20480]{2,1,0:T(2,128)(2,1)}), bf16[4,2,20480]{2,1,0:T(2,128)(2,1)S(1)}, u32[]{:S(2)}, u32[]{:S(2)}) %all-to-all-start) | async-done | bytes 327712 | tf_op jit(solution)/shard_map/all_to_all | solution.py:101
  28.2 0.4 reshape.213
  28.6 0.1 bitcast_bitcast_fusion
  28.8 0.8 %copy.11 = bf16[1,40,4,16,1,64]{1,5,3,2,4,0:T(8,128)(2,1)S(1)} copy(bf16[1,40,4,16,1,64]{5,3,1,2,4,0:T(8,128)(2,1)S(1)} %bitcast_bitcast_fusion) | data formatting | bytes 655360 | tf_op jit(solution)/shard_map/all_to_all | solution.py:101
  29.5 1.3 %copy.12 = bf16[32,40,2,64]{3,2,1,0:T(2,128)(2,1)S(1)} copy(bf16[32,40,2,64]{1,0,2,3:T(8,128)(2,1)S(1)} %bitcast.30) | data formatting | bytes 655360 | tf_op jit(solution)/shard_map/transpose | solution.py:106
  30.9 0.3 reshape.210
  31.1 0.3 reshape_reshape.3.refs_4_
  31.4 3.5 %collective-permute-start = (bf16[16,80,128]{2,1,0:T(8,128)(2,1)S(1)}, bf16[16,80,128]{2,1,0:T(8,128)(2,1)S(1)}, u32[]{:S(2)}, u32[]{:S(2)}) collective-permute-start(bf16[16,80,128]{2,1,0:T(8,128)(2,1)S(1)} %reshape_reshape.3.refs_4_), channel_id=1, source_target_pairs={{0,2},{1,3},{2,4},{3,5},{4,6},{5,7},{8,10},{9,11},{10,12},{11,13},... | collective-permute-start | bytes 983048 | tf_op jit(solution)/shard_map/ppermute | solution.py:18
  35.0 1.3 %collective-permute-start.1 = (bf16[16,80,128]{2,1,0:T(8,128)(2,1)S(1)}, bf16[16,80,128]{2,1,0:T(8,128)(2,1)S(1)}, u32[]{:S(2)}, u32[]{:S(2)}) collective-permute-start(bf16[16,80,128]{2,1,0:T(8,128)(2,1)S(1)} %reshape_reshape.3.refs_4_), channel_id=1, source_target_pairs={{0,1},{1,2},{2,3},{3,4},{4,5},{5,6},{6,7},{8,9},{9,10},{10,11},{11... | collective-permute-start | bytes 983048 | tf_op jit(solution)/shard_map/ppermute | solution.py:18
  36.3 1.3 %collective-permute-start.2 = (bf16[16,80,128]{2,1,0:T(8,128)(2,1)S(1)}, bf16[16,80,128]{2,1,0:T(8,128)(2,1)S(1)}, u32[]{:S(2)}, u32[]{:S(2)}) collective-permute-start(bf16[16,80,128]{2,1,0:T(8,128)(2,1)S(1)} %reshape_reshape.3.refs_4_), channel_id=1, source_target_pairs={{1,0},{2,1},{3,2},{4,3},{5,4},{6,5},{7,6},{9,8},{10,9},{11,10},{12... | collective-permute-start | bytes 983048 | tf_op jit(solution)/shard_map/ppermute | solution.py:18
  37.6 1.3 %collective-permute-start.3 = (bf16[16,80,128]{2,1,0:T(8,128)(2,1)S(1)}, bf16[16,80,128]{2,1,0:T(8,128)(2,1)S(1)}, u32[]{:S(2)}, u32[]{:S(2)}) collective-permute-start(bf16[16,80,128]{2,1,0:T(8,128)(2,1)S(1)} %reshape_reshape.3.refs_4_), channel_id=1, source_target_pairs={{2,0},{3,1},{4,2},{5,3},{6,4},{7,5},{10,8},{11,9},{12,10},{13,11},... | collective-permute-start | bytes 983048 | tf_op jit(solution)/shard_map/ppermute | solution.py:18
  38.9 0.2 slice_negate_fusion
  39.0 1.0 %maximum_maximum_fusion.refs_1_ = bf16[32,80,128]{2,1,0:T(8,128)(2,1)} fusion(bf16[32,40,64]{2,1,0:T(8,128)(2,1)S(1)} %get-tuple-element.6, bf16[32,40,64]{2,1,0:T(8,128)(2,1)S(1)} %get-tuple-element.5, bf16[32,40,128]{2,1,0:T(8,128)(2,1)S(1)} %reshape.210), kind=kLoop, calls=%fused_computation.6 | loop fusion | flops 1966080 | bytes 1310720 | tf_op jit(solution)/shard_map/concatenate | solution.py:117
  40.1 2.3 %collective-permute-done.refs_2_ = bf16[16,80,128]{2,1,0:T(8,128)(2,1)S(1)} collective-permute-done((bf16[16,80,128]{2,1,0:T(8,128)(2,1)S(1)}, bf16[16,80,128]{2,1,0:T(8,128)(2,1)S(1)}, u32[]{:S(2)}, u32[]{:S(2)}) %collective-permute-start) | collective-permute-done | bytes 327712 | tf_op jit(solution)/shard_map/ppermute | solution.py:18
  42.4 11.8 %collective-permute-done.3.refs_6_ = bf16[16,80,128]{2,1,0:T(8,128)(2,1)S(1)} collective-permute-done((bf16[16,80,128]{2,1,0:T(8,128)(2,1)S(1)}, bf16[16,80,128]{2,1,0:T(8,128)(2,1)S(1)}, u32[]{:S(2)}, u32[]{:S(2)}) %collective-permute-start.3) | collective-permute-done | bytes 327712 | tf_op jit(solution)/shard_map/ppermute | solution.py:18
  54.2 0.7 %copy-done.4 = bf16[16,80,128]{2,1,0:T(8,128)(2,1)} copy-done((bf16[16,80,128]{2,1,0:T(8,128)(2,1)}, bf16[16,80,128]{2,1,0:T(8,128)(2,1)S(1)}, u32[]{:S(2)}) %copy-start.4) | copy-done | bytes 327704
  54.9 6.4 %shard_map.37 = f32[5,40,2560]{2,1,0:T(8,128)} custom-call(s32[5]{0:T(128)} %compare_select_fusion.2.refs_0_, bf16[32,80,128]{2,1,0:T(8,128)(2,1)} %maximum_maximum_fusion.refs_1_, bf16[16,80,128]{2,1,0:T(8,128)(2,1)} %copy-done.1, bf16[16,80,128]{2,1,0:T(8,128)(2,1)} %copy-done.2, bf16[16,80,128]{2,1,0:T(8,128)(2,1)} %copy-done, ...), custom_call_target="tpu_custom_call" | custom-call | tf_op jit(solution)/shard_map/pallas_call | solution.py:88
  (19 shorter events, 0.1 us)
Async XLA Ops:
  0.6 2.4 %slice-start = ((s8[10485760]{0:T(1024)(128)(4,1)}), s8[4194304]{0:T(1024)(128)(4,1)S(1)}, s32[]{:S(2)}) async-start(s8[10485760]{0:T(1024)(128)(4,1)} %bitcast.32), calls=%async_computation.1 | async-start | bytes 8388608
  0.6 3.5 %slice-start.1 = ((s8[10485760]{0:T(1024)(128)(4,1)}), s8[4194304]{0:T(1024)(128)(4,1)S(1)}, s32[]{:S(2)}) async-start(s8[10485760]{0:T(1024)(128)(4,1)} %bitcast.32), calls=%async_computation.2 | async-start | bytes 8388608
  1.8 3.1 %slice-start.2 = ((s8[10485760]{0:T(1024)(128)(4,1)}), s8[2097152]{0:T(1024)(128)(4,1)S(1)}, s32[]{:S(2)}) async-start(s8[10485760]{0:T(1024)(128)(4,1)} %bitcast.32), calls=%async_computation.3 | async-start | bytes 4194304
  15.0 8.0 %copy-start.5 = (s32[1,5]{1,0:T(1,128)S(1)}, s32[1,5]{1,0:T(1,128)}, u32[]{:S(2)}) copy-start(s32[1,5]{1,0:T(1,128)} %param.4) | copy-start | bytes 64
  17.0 11.2 %all-to-all-start = ((bf16[4,2,20480]{2,1,0:T(2,128)(2,1)}), bf16[4,2,20480]{2,1,0:T(2,128)(2,1)S(1)}, u32[]{:S(2)}, u32[]{:S(2)}) async-start(bf16[4,2,20480]{2,1,0:T(2,128)(2,1)} %reshape.212), calls=%async_computation | async-start | bytes 655360 | tf_op jit(solution)/shard_map/all_to_all | solution.py:101
  31.4 22.7 %copy-start = (bf16[16,80,128]{2,1,0:T(8,128)(2,1)}, bf16[16,80,128]{2,1,0:T(8,128)(2,1)S(1)}, u32[]{:S(2)}) copy-start(bf16[16,80,128]{2,1,0:T(8,128)(2,1)S(1)} %reshape_reshape.3.refs_4_) | copy-start | bytes 983044
  31.4 10.9 %collective-permute-start = (bf16[16,80,128]{2,1,0:T(8,128)(2,1)S(1)}, bf16[16,80,128]{2,1,0:T(8,128)(2,1)S(1)}, u32[]{:S(2)}, u32[]{:S(2)}) collective-permute-start(bf16[16,80,128]{2,1,0:T(8,128)(2,1)S(1)} %reshape_reshape.3.refs_4_), channel_id=1, source_target_pairs={{0,2},{1,3},{2,4},{3,5},{4,6},{5,7},{8,10},{9,11},{10,12},{11,13},... | collective-permute-start | bytes 983048 | tf_op jit(solution)/shard_map/ppermute | solution.py:18
  35.0 7.4 %collective-permute-start.1 = (bf16[16,80,128]{2,1,0:T(8,128)(2,1)S(1)}, bf16[16,80,128]{2,1,0:T(8,128)(2,1)S(1)}, u32[]{:S(2)}, u32[]{:S(2)}) collective-permute-start(bf16[16,80,128]{2,1,0:T(8,128)(2,1)S(1)} %reshape_reshape.3.refs_4_), channel_id=1, source_target_pairs={{0,1},{1,2},{2,3},{3,4},{4,5},{5,6},{6,7},{8,9},{9,10},{10,11},{11... | collective-permute-start | bytes 983048 | tf_op jit(solution)/shard_map/ppermute | solution.py:18
  36.3 6.1 %collective-permute-start.2 = (bf16[16,80,128]{2,1,0:T(8,128)(2,1)S(1)}, bf16[16,80,128]{2,1,0:T(8,128)(2,1)S(1)}, u32[]{:S(2)}, u32[]{:S(2)}) collective-permute-start(bf16[16,80,128]{2,1,0:T(8,128)(2,1)S(1)} %reshape_reshape.3.refs_4_), channel_id=1, source_target_pairs={{1,0},{2,1},{3,2},{4,3},{5,4},{6,5},{7,6},{9,8},{10,9},{11,10},{12... | collective-permute-start | bytes 983048 | tf_op jit(solution)/shard_map/ppermute | solution.py:18
  37.6 16.6 %collective-permute-start.3 = (bf16[16,80,128]{2,1,0:T(8,128)(2,1)S(1)}, bf16[16,80,128]{2,1,0:T(8,128)(2,1)S(1)}, u32[]{:S(2)}, u32[]{:S(2)}) collective-permute-start(bf16[16,80,128]{2,1,0:T(8,128)(2,1)S(1)} %reshape_reshape.3.refs_4_), channel_id=1, source_target_pairs={{2,0},{3,1},{4,2},{5,3},{6,4},{7,5},{10,8},{11,9},{12,10},{13,11},... | collective-permute-start | bytes 983048 | tf_op jit(solution)/shard_map/ppermute | solution.py:18
  42.4 11.8 %copy-start.1 = (bf16[16,80,128]{2,1,0:T(8,128)(2,1)}, bf16[16,80,128]{2,1,0:T(8,128)(2,1)S(1)}, u32[]{:S(2)}) copy-start(bf16[16,80,128]{2,1,0:T(8,128)(2,1)S(1)} %collective-permute-done.refs_2_) | copy-start | bytes 983044
  42.4 11.8 %copy-start.2 = (bf16[16,80,128]{2,1,0:T(8,128)(2,1)}, bf16[16,80,128]{2,1,0:T(8,128)(2,1)S(1)}, u32[]{:S(2)}) copy-start(bf16[16,80,128]{2,1,0:T(8,128)(2,1)S(1)} %collective-permute-done.1.refs_3_) | copy-start | bytes 983044
  42.4 11.8 %copy-start.3 = (bf16[16,80,128]{2,1,0:T(8,128)(2,1)}, bf16[16,80,128]{2,1,0:T(8,128)(2,1)S(1)}, u32[]{:S(2)}) copy-start(bf16[16,80,128]{2,1,0:T(8,128)(2,1)S(1)} %collective-permute-done.2.refs_5_) | copy-start | bytes 983044
  54.2 0.7 %copy-start.4 = (bf16[16,80,128]{2,1,0:T(8,128)(2,1)}, bf16[16,80,128]{2,1,0:T(8,128)(2,1)S(1)}, u32[]{:S(2)}) copy-start(bf16[16,80,128]{2,1,0:T(8,128)(2,1)S(1)} %collective-permute-done.3.refs_6_) | copy-start | bytes 983044

commit v5 on v4

--- a/solution.py
+++ b/solution.py
@@ -12,9 +12,9 @@
 BINS_PER_STEP = 8
 
 
-def passed_along(array, axis, by):
+def passed_along(array, axis, by, sources=lambda i: True):
     peers = lax.axis_size(axis)
-    pairs = [(i, i + by) for i in range(peers) if 0 <= i + by < peers]
+    pairs = [(i, i + by) for i in range(peers) if 0 <= i + by < peers and sources(i)]
     return lax.ppermute(array, axis, pairs)
 
 
@@ -107,11 +107,24 @@
         .reshape(nb, stations, 2 * windows)
     )
     paired = spec.reshape(nb // 2, 2 * stations, 2 * windows)
-    ys = []
-    for offset in range(-R, R + 1):
-        ys.append(paired if offset == 0 else passed_along(paired, "sta", -offset))
+    even = lambda i: i % 2 == 0
+    odd = lambda i: i % 2 == 1
+    left1 = passed_along(paired, "sta", 1)
+    right1 = passed_along(paired, "sta", -1)
+    ys = [
+        passed_along(paired, "sta", 2, even),
+        passed_along(left1, "sta", 1, even),
+        left1,
+        paired,
+        right1,
+        passed_along(paired, "sta", -2, odd),
+        passed_along(right1, "sta", -1, odd),
+    ]
     where_at = jnp.clip(partner_row - block_index + R, 0, 2 * R)
-    sel = jnp.where(live_slots, where_at, -1).astype(jnp.int32)
+    parity = block_index % 2
+    slot_ref = jnp.where(where_at == 0, parity, where_at + 1)
+    slot_ref = jnp.where(where_at == 2 * R, 2 * R + 2 - parity, slot_ref)
+    sel = jnp.where(live_slots, slot_ref, -1).astype(jnp.int32)
     x_re = spec[:, :, :windows]
     x_im = spec[:, :, windows:]
     lx = jnp.concatenate([spec, jnp.concatenate([-x_im, x_re], axis=2)], axis=1)

time: 61.6 us -> 55.4 us (0.90); the launches traced: 61.3 us -> 54.4 us
  waiting for transfers between devices: 18.7 us -> 0.97 us
  blocking collectives: 0 us -> 11.6 us
  local copies, waits for them, and re-layouts: 7.61 us -> 6.9 us
    ppermute x4 -> x6, waiting for transfers between devices: 14 us -> 0.97 us  [passed_along(): return lax.ppermute(array, axis, pairs)]
    all_to_all x0 -> x1, blocking collectives: none -> 11.6 us  [body(): lax.all_to_all(own_spec, 'tm', split_axis=3, concat_axis=2, tiled=True)]
    all_to_all x1 -> x0, starting transfers between devices: 5.35 us -> none  [body(): lax.all_to_all(own_spec, 'tm', split_axis=3, concat_axis=2, tiled=True)]
    ppermute x4 -> x6, starting transfers between devices: 7.39 us -> 12.3 us  [passed_along(): return lax.ppermute(array, axis, pairs)]
    all_to_all x1 -> x0, waiting for transfers between devices: 4.7 us -> none  [body(): lax.all_to_all(own_spec, 'tm', split_axis=3, concat_axis=2, tiled=True)]
    unnamed x20 -> x24, local copies, waits for them, and re-layouts: 4.3 us -> 3.6 us
  transfers between devices with their start and end apart: 5 -> 6, of which waited for: 3 -> 1; matrix products, arithmetic and copies ran while one was open for 3% -> 4% of each run, Pallas kernels for 0% -> 0%
where the time goes in v5:
time: 55.4 us; the launch traced here: 54.4 us
  starting transfers between devices  12.3 us (22%)
  blocking collectives  11.6 us (21%)
  matrix products  10.1 us (18%)
  local copies, waits for them, and re-layouts  6.9 us (12%)
  Pallas kernels  6.68 us (12%)
  other arithmetic  4.85 us (9%)
  waiting for transfers between devices  0.97 us (2%)
  between operations  0.97 us (2%)
    ppermute x6, starting transfers between devices, passed_along(): return lax.ppermute(array, axis, pairs)  12.3 us
    all_to_all x1, blocking collectives, body(): lax.all_to_all(own_spec, 'tm', split_axis=3, concat_axis=2, tiled=True)  11.6 us
    dot_general x1, matrix products, whiten(): jnp.einsum('swn,nk->swk', records, dft_table, precision=lax.Precision.HIGH)  10.1 us
    pallas_call x1, Pallas kernels, cross_block(): pl.pallas_call(kernel, grid_spec=grid_spec, out_shape=jax.ShapeDtypeStruc...  6.68 us
    unnamed x24, local copies, waits for them, and re-layouts  3.6 us
    transpose x1, local copies, waits for them, and re-layouts, body(): spec = regrouped.reshape(stations, windows, 2, nb).transpose(3, 0, 2, 1)....  1.31 us
    sub x1, other arithmetic, dft_columns(): cosine = c1 * c2 - s1 * s2  1.17 us
    select_n x1, other arithmetic, dft_columns(): table = jnp.where(part_of[None, None, :] == 0, cosine, minus_sine)  1.14 us
  transfers between devices with their start and end apart: 6, of which 1 were waited for; matrix products, arithmetic and copies ran while one was open for 4% of the time, Pallas kernels for 0%

profile of v5, /device:TPU:0, one launch (start us, length us, event | category | flops | bytes accessed | tf_op | source)
XLA Modules:
  0.0 54.4 jit_solution(11480996913788192872)
XLA Ops:
  0.0 0.6 %fusion.16 = (f32[64,256]{1,0:T(8,128)S(1)}, f32[64,256]{1,0:T(8,128)S(1)}, f32[64,256]{1,0:T(8,128)S(1)}, f32[64,256]{1,0:T(8,128)S(1)}) fusion(s32[256]{0:T(256)S(1)} %fusion.21, s32[64]{0:T(128)S(1)} %iota_multiply_fusion), kind=kLoop, calls=%fused_computation.31 | loop fusion | flops 458752 | bytes 263424 | tf_op jit(solution)/shard_map/cos | solution.py:32
  0.6 0.0 slice-start
  0.6 1.2 %multiply_subtract_fusion = (f32[64,64,256]{2,1,0:T(8,128)S(1)}, f32[64,64,256]{2,1,0:T(8,128)S(1)}) fusion(f32[64,256]{1,0:T(8,128)S(1)} %get-tuple-element.11, f32[64,256]{1,0:T(8,128)S(1)} %get-tuple-element.10, f32[64,256]{1,0:T(8,128)S(1)} %get-tuple-element.12, f32[64,256]{1,0:T(8,128)S(1)} %get-tuple-element.9), kind=kLoop, calls=%fused_computation.5 | loop fusion | flops 7340032 | bytes 8650752 | tf_op jit(solution)/shard_map/sub | solution.py:36
  1.8 0.0 slice-start.2
  1.8 1.1 %bitcast_select_fusion = f32[4096,256]{1,0:T(8,128)S(1)} fusion(f32[64,64,256]{2,1,0:T(8,128)S(1)} %get-tuple-element.8, f32[64,64,256]{2,1,0:T(8,128)S(1)} %get-tuple-element.7, pred[256]{0:T(512)(128)(4,1)S(1)} %fusion.24), kind=kLoop, calls=%fused_computation.3 | loop fusion | flops 1048576 | bytes 12583168 | tf_op jit(solution)/shard_map/jit(_where)/select_n | solution.py:38
  2.9 1.1 %slice-done.1 = s8[4194304]{0:T(1024)(128)(4,1)S(1)} async-done(((s8[10485760]{0:T(1024)(128)(4,1)}), s8[4194304]{0:T(1024)(128)(4,1)S(1)}, s32[]{:S(2)}) %slice-start.1) | async-done | bytes 4194328
  4.0 0.8 %slice-done.2 = s8[2097152]{0:T(1024)(128)(4,1)S(1)} async-done(((s8[10485760]{0:T(1024)(128)(4,1)}), s8[2097152]{0:T(1024)(128)(4,1)S(1)}, s32[]{:S(2)}) %slice-start.2) | async-done | bytes 2097176
  4.9 10.1 %multiply_reduce_fusion = (f32[40,16]{0,1:T(8,128)S(1)}, f32[256,40,16]{0,1,2:T(8,128)S(1)}) fusion(f32[40,16,4096]{2,1,0:T(8,128)S(1)} %bitcast.35, f32[4096,256]{1,0:T(8,128)S(1)} %bitcast_select_fusion), kind=kOutput, calls=%fused_computation.8 | convolution fusion | flops 4026859008 | bytes 15337984 | tf_op jit(solution)/shard_map/swn,nk->swk/dot_general | solution.py:44
  15.0 0.2 fusion.3
  15.2 0.3 reshape.214
  15.5 0.3 copy.19
  15.8 0.0 copy-start.7
  15.8 0.5 reshape.222
  16.2 11.6 %all_to_all.15 = bf16[4,2,20480]{2,1,0:T(2,128)(2,1)S(1)} all-to-all(bf16[4,2,20480]{2,1,0:T(2,128)(2,1)S(1)} %reshape.222), channel_id=1, replica_groups=mesh['tm'=4,'sta'=8] {'tm'}, dimensions={0} | all-to-all | bytes 655360 | tf_op jit(solution)/shard_map/all_to_all | solution.py:101
  27.8 0.4 reshape.223
  28.2 0.1 bitcast_bitcast_fusion
  28.4 0.8 %copy.11 = bf16[1,40,4,16,1,64]{1,5,3,2,4,0:T(8,128)(2,1)S(1)} copy(bf16[1,40,4,16,1,64]{5,3,1,2,4,0:T(8,128)(2,1)S(1)} %bitcast_bitcast_fusion) | data formatting | bytes 655360 | tf_op jit(solution)/shard_map/all_to_all | solution.py:101
  29.1 1.3 %copy.12 = bf16[32,40,2,64]{3,2,1,0:T(2,128)(2,1)S(1)} copy(bf16[32,40,2,64]{1,0,2,3:T(8,128)(2,1)S(1)} %bitcast.32) | data formatting | bytes 655360 | tf_op jit(solution)/shard_map/transpose | solution.py:106
  30.5 0.3 reshape_reshape.3.refs_5_
  30.8 1.3 %collective-permute-start.1 = (bf16[16,80,128]{2,1,0:T(8,128)(2,1)S(1)}, bf16[16,80,128]{2,1,0:T(8,128)(2,1)S(1)}, u32[]{:S(2)}, u32[]{:S(2)}) collective-permute-start(bf16[16,80,128]{2,1,0:T(8,128)(2,1)S(1)} %reshape_reshape.3.refs_5_), channel_id=1, source_target_pairs={{0,1},{1,2},{2,3},{3,4},{4,5},{5,6},{6,7},{8,9},{9,10},{10,11},{11... | collective-permute-start | bytes 983048 | tf_op jit(solution)/shard_map/ppermute | solution.py:18
  32.1 1.3 %collective-permute-start.3 = (bf16[16,80,128]{2,1,0:T(8,128)(2,1)S(1)}, bf16[16,80,128]{2,1,0:T(8,128)(2,1)S(1)}, u32[]{:S(2)}, u32[]{:S(2)}) collective-permute-start(bf16[16,80,128]{2,1,0:T(8,128)(2,1)S(1)} %reshape_reshape.3.refs_5_), channel_id=1, source_target_pairs={{1,0},{2,1},{3,2},{4,3},{5,4},{6,5},{7,6},{9,8},{10,9},{11,10},{12... | collective-permute-start | bytes 983048 | tf_op jit(solution)/shard_map/ppermute | solution.py:18
  34.0 0.6 %compare_select_fusion.4.refs_0_ = s32[5]{0:T(128)} fusion(s32[1,5]{1,0:T(1,128)S(1)} %copy-done.7, s32[]{:T(128)S(6)} %sub.29, s32[]{:T(128)S(6)} %select_n.81, s32[]{:T(128)S(6)} %axis_index.12, s32[]{:T(128)} %bitcast.31), kind=kLoop, calls=%fused_computation.44 | loop fusion | flops 50 | bytes 56 | tf_op jit(solution)/shard_map/jit(_where)/select_n | solution.py:127
  34.6 0.3 reshape.216
  34.9 6.5 %collective-permute-start = (bf16[16,80,128]{2,1,0:T(8,128)(2,1)S(1)}, bf16[16,80,128]{2,1,0:T(8,128)(2,1)S(1)}, u32[]{:S(2)}, u32[]{:S(2)}) collective-permute-start(bf16[16,80,128]{2,1,0:T(8,128)(2,1)S(1)} %reshape_reshape.3.refs_5_), channel_id=1, source_target_pairs={{0,2},{2,4},{4,6},{8,10},{10,12},{12,14},{16,18},{18,20},{20,22},{... | collective-permute-start | bytes 983048 | tf_op jit(solution)/shard_map/ppermute | solution.py:18
  41.4 0.7 %collective-permute-start.4 = (bf16[16,80,128]{2,1,0:T(8,128)(2,1)S(1)}, bf16[16,80,128]{2,1,0:T(8,128)(2,1)S(1)}, u32[]{:S(2)}, u32[]{:S(2)}) collective-permute-start(bf16[16,80,128]{2,1,0:T(8,128)(2,1)S(1)} %reshape_reshape.3.refs_5_), channel_id=1, source_target_pairs={{3,1},{5,3},{7,5},{11,9},{13,11},{15,13},{19,17},{21,19},{23,21},{... | collective-permute-start | bytes 983048 | tf_op jit(solution)/shard_map/ppermute | solution.py:18
  42.1 1.3 %collective-permute-start.2 = (bf16[16,80,128]{2,1,0:T(8,128)(2,1)S(1)}, bf16[16,80,128]{2,1,0:T(8,128)(2,1)S(1)}, u32[]{:S(2)}, u32[]{:S(2)}) collective-permute-start(bf16[16,80,128]{2,1,0:T(8,128)(2,1)S(1)} %collective-permute-done.1.refs_4_), channel_id=1, source_target_pairs={{0,1},{2,3},{4,5},{6,7},{8,9},{10,11},{12,13},{14,15},{16,17},{18,... | collective-permute-start | bytes 983048 | tf_op jit(solution)/shard_map/ppermute | solution.py:18
  43.4 1.3 %collective-permute-start.5 = (bf16[16,80,128]{2,1,0:T(8,128)(2,1)S(1)}, bf16[16,80,128]{2,1,0:T(8,128)(2,1)S(1)}, u32[]{:S(2)}, u32[]{:S(2)}) collective-permute-start(bf16[16,80,128]{2,1,0:T(8,128)(2,1)S(1)} %collective-permute-done.3.refs_6_), channel_id=1, source_target_pairs={{1,0},{3,2},{5,4},{7,6},{9,8},{11,10},{13,12},{15,14},{17,16},{19,... | collective-permute-start | bytes 983048 | tf_op jit(solution)/shard_map/ppermute | solution.py:18
  44.7 0.2 slice_negate_fusion
  44.9 1.1 %maximum_maximum_fusion.refs_1_ = bf16[32,80,128]{2,1,0:T(8,128)(2,1)} fusion(bf16[32,40,64]{2,1,0:T(8,128)(2,1)S(1)} %get-tuple-element.6, bf16[32,40,64]{2,1,0:T(8,128)(2,1)S(1)} %get-tuple-element.5, bf16[32,40,128]{2,1,0:T(8,128)(2,1)S(1)} %reshape.216), kind=kLoop, calls=%fused_computation.6 | loop fusion | flops 1966080 | bytes 1310720 | tf_op jit(solution)/shard_map/concatenate | solution.py:130
  46.0 1.0 %collective-permute-done.5.refs_8_ = bf16[16,80,128]{2,1,0:T(8,128)(2,1)S(1)} collective-permute-done((bf16[16,80,128]{2,1,0:T(8,128)(2,1)S(1)}, bf16[16,80,128]{2,1,0:T(8,128)(2,1)S(1)}, u32[]{:S(2)}, u32[]{:S(2)}) %collective-permute-start.5) | collective-permute-done | bytes 327712 | tf_op jit(solution)/shard_map/ppermute | solution.py:18
  47.0 0.7 %copy-done.6 = bf16[16,80,128]{2,1,0:T(8,128)(2,1)} copy-done((bf16[16,80,128]{2,1,0:T(8,128)(2,1)}, bf16[16,80,128]{2,1,0:T(8,128)(2,1)S(1)}, u32[]{:S(2)}) %copy-start.6) | copy-done | bytes 327704
  47.7 6.7 %shard_map.37 = f32[5,40,2560]{2,1,0:T(8,128)} custom-call(s32[5]{0:T(128)} %compare_select_fusion.4.refs_0_, bf16[32,80,128]{2,1,0:T(8,128)(2,1)} %maximum_maximum_fusion.refs_1_, bf16[16,80,128]{2,1,0:T(8,128)(2,1)} %copy-done.3, bf16[16,80,128]{2,1,0:T(8,128)(2,1)} %copy-done.5, bf16[16,80,128]{2,1,0:T(8,128)(2,1)} %copy-done.1, ...), custom_call_target="tpu_custom_call" | custom-call | tf_op jit(solution)/shard_map/pallas_call | solution.py:88
  (26 shorter events, 0.1 us)
Async XLA Ops:
  0.6 2.4 %slice-start = ((s8[10485760]{0:T(1024)(128)(4,1)}), s8[4194304]{0:T(1024)(128)(4,1)S(1)}, s32[]{:S(2)}) async-start(s8[10485760]{0:T(1024)(128)(4,1)} %bitcast.34), calls=%async_computation.1 | async-start | bytes 8388608
  0.6 3.5 %slice-start.1 = ((s8[10485760]{0:T(1024)(128)(4,1)}), s8[4194304]{0:T(1024)(128)(4,1)S(1)}, s32[]{:S(2)}) async-start(s8[10485760]{0:T(1024)(128)(4,1)} %bitcast.34), calls=%async_computation.2 | async-start | bytes 8388608
  1.8 3.1 %slice-start.2 = ((s8[10485760]{0:T(1024)(128)(4,1)}), s8[2097152]{0:T(1024)(128)(4,1)S(1)}, s32[]{:S(2)}) async-start(s8[10485760]{0:T(1024)(128)(4,1)} %bitcast.34), calls=%async_computation.3 | async-start | bytes 4194304
  15.8 18.3 %copy-start.7 = (s32[1,5]{1,0:T(1,128)S(1)}, s32[1,5]{1,0:T(1,128)}, u32[]{:S(2)}) copy-start(s32[1,5]{1,0:T(1,128)} %param.4) | copy-start | bytes 64
  30.8 16.2 %copy-start = (bf16[16,80,128]{2,1,0:T(8,128)(2,1)}, bf16[16,80,128]{2,1,0:T(8,128)(2,1)S(1)}, u32[]{:S(2)}) copy-start(bf16[16,80,128]{2,1,0:T(8,128)(2,1)S(1)} %reshape_reshape.3.refs_5_) | copy-start | bytes 983044
  30.8 11.3 %collective-permute-start.1 = (bf16[16,80,128]{2,1,0:T(8,128)(2,1)S(1)}, bf16[16,80,128]{2,1,0:T(8,128)(2,1)S(1)}, u32[]{:S(2)}, u32[]{:S(2)}) collective-permute-start(bf16[16,80,128]{2,1,0:T(8,128)(2,1)S(1)} %reshape_reshape.3.refs_5_), channel_id=1, source_target_pairs={{0,1},{1,2},{2,3},{3,4},{4,5},{5,6},{6,7},{8,9},{9,10},{10,11},{11... | collective-permute-start | bytes 983048 | tf_op jit(solution)/shard_map/ppermute | solution.py:18
  32.1 11.3 %collective-permute-start.3 = (bf16[16,80,128]{2,1,0:T(8,128)(2,1)S(1)}, bf16[16,80,128]{2,1,0:T(8,128)(2,1)S(1)}, u32[]{:S(2)}, u32[]{:S(2)}) collective-permute-start(bf16[16,80,128]{2,1,0:T(8,128)(2,1)S(1)} %reshape_reshape.3.refs_5_), channel_id=1, source_target_pairs={{1,0},{2,1},{3,2},{4,3},{5,4},{6,5},{7,6},{9,8},{10,9},{11,10},{12... | collective-permute-start | bytes 983048 | tf_op jit(solution)/shard_map/ppermute | solution.py:18
  34.9 11.0 %collective-permute-start = (bf16[16,80,128]{2,1,0:T(8,128)(2,1)S(1)}, bf16[16,80,128]{2,1,0:T(8,128)(2,1)S(1)}, u32[]{:S(2)}, u32[]{:S(2)}) collective-permute-start(bf16[16,80,128]{2,1,0:T(8,128)(2,1)S(1)} %reshape_reshape.3.refs_5_), channel_id=1, source_target_pairs={{0,2},{2,4},{4,6},{8,10},{10,12},{12,14},{16,18},{18,20},{20,22},{... | collective-permute-start | bytes 983048 | tf_op jit(solution)/shard_map/ppermute | solution.py:18
  41.4 4.6 %collective-permute-start.4 = (bf16[16,80,128]{2,1,0:T(8,128)(2,1)S(1)}, bf16[16,80,128]{2,1,0:T(8,128)(2,1)S(1)}, u32[]{:S(2)}, u32[]{:S(2)}) collective-permute-start(bf16[16,80,128]{2,1,0:T(8,128)(2,1)S(1)} %reshape_reshape.3.refs_5_), channel_id=1, source_target_pairs={{3,1},{5,3},{7,5},{11,9},{13,11},{15,13},{19,17},{21,19},{23,21},{... | collective-permute-start | bytes 983048 | tf_op jit(solution)/shard_map/ppermute | solution.py:18
  42.1 4.9 %copy-start.1 = (bf16[16,80,128]{2,1,0:T(8,128)(2,1)}, bf16[16,80,128]{2,1,0:T(8,128)(2,1)S(1)}, u32[]{:S(2)}) copy-start(bf16[16,80,128]{2,1,0:T(8,128)(2,1)S(1)} %collective-permute-done.1.refs_4_) | copy-start | bytes 983044
  42.1 3.9 %collective-permute-start.2 = (bf16[16,80,128]{2,1,0:T(8,128)(2,1)S(1)}, bf16[16,80,128]{2,1,0:T(8,128)(2,1)S(1)}, u32[]{:S(2)}, u32[]{:S(2)}) collective-permute-start(bf16[16,80,128]{2,1,0:T(8,128)(2,1)S(1)} %collective-permute-done.1.refs_4_), channel_id=1, source_target_pairs={{0,1},{2,3},{4,5},{6,7},{8,9},{10,11},{12,13},{14,15},{16,17},{18,... | collective-permute-start | bytes 983048 | tf_op jit(solution)/shard_map/ppermute | solution.py:18
  43.4 3.5 %copy-start.2 = (bf16[16,80,128]{2,1,0:T(8,128)(2,1)}, bf16[16,80,128]{2,1,0:T(8,128)(2,1)S(1)}, u32[]{:S(2)}) copy-start(bf16[16,80,128]{2,1,0:T(8,128)(2,1)S(1)} %collective-permute-done.3.refs_6_) | copy-start | bytes 983044
  43.4 3.5 %collective-permute-start.5 = (bf16[16,80,128]{2,1,0:T(8,128)(2,1)S(1)}, bf16[16,80,128]{2,1,0:T(8,128)(2,1)S(1)}, u32[]{:S(2)}, u32[]{:S(2)}) collective-permute-start(bf16[16,80,128]{2,1,0:T(8,128)(2,1)S(1)} %collective-permute-done.3.refs_6_), channel_id=1, source_target_pairs={{1,0},{3,2},{5,4},{7,6},{9,8},{11,10},{13,12},{15,14},{17,16},{19,... | collective-permute-start | bytes 983048 | tf_op jit(solution)/shard_map/ppermute | solution.py:18
  46.0 1.0 %copy-start.3 = (bf16[16,80,128]{2,1,0:T(8,128)(2,1)}, bf16[16,80,128]{2,1,0:T(8,128)(2,1)S(1)}, u32[]{:S(2)}) copy-start(bf16[16,80,128]{2,1,0:T(8,128)(2,1)S(1)} %collective-permute-done.refs_2_) | copy-start | bytes 983044
  46.0 1.0 %copy-start.4 = (bf16[16,80,128]{2,1,0:T(8,128)(2,1)}, bf16[16,80,128]{2,1,0:T(8,128)(2,1)S(1)}, u32[]{:S(2)}) copy-start(bf16[16,80,128]{2,1,0:T(8,128)(2,1)S(1)} %collective-permute-done.4.refs_7_) | copy-start | bytes 983044
  46.0 1.0 %copy-start.5 = (bf16[16,80,128]{2,1,0:T(8,128)(2,1)}, bf16[16,80,128]{2,1,0:T(8,128)(2,1)S(1)}, u32[]{:S(2)}) copy-start(bf16[16,80,128]{2,1,0:T(8,128)(2,1)S(1)} %collective-permute-done.2.refs_3_) | copy-start | bytes 983044
  47.0 0.7 %copy-start.6 = (bf16[16,80,128]{2,1,0:T(8,128)(2,1)}, bf16[16,80,128]{2,1,0:T(8,128)(2,1)S(1)}, u32[]{:S(2)}) copy-start(bf16[16,80,128]{2,1,0:T(8,128)(2,1)S(1)} %collective-permute-done.5.refs_8_) | copy-start | bytes 983044

commit v6 on v5

--- a/solution.py
+++ b/solution.py
@@ -47,25 +47,29 @@
     return white.reshape(1, records.shape[0], records.shape[1], groups, 2 * (BINS // groups))
 
 
-def cross_kernel(scale, sel_ref, lx_ref, *refs):
-    *y_refs, o_ref = refs
+def cross_kernel(sel_ref, lx_ref, *refs):
+    *y_refs, o_ref, pick_ref = refs
     bins, two_s, _ = lx_ref.shape
     s = two_s // 2
     slots = o_ref.shape[0]
+    for p in range(slots):
+        rows = slice(p * two_s, (p + 1) * two_s)
+        for o, y_ref in enumerate(y_refs):
+            @pl.when(sel_ref[p] == o)
+            def _():
+                pick_ref[:, rows, :] = y_ref[...]
+
+        @pl.when(sel_ref[p] < 0)
+        def _():
+            pick_ref[:, rows, :] = jnp.zeros(y_refs[0].shape, y_refs[0].dtype)
+
     for j in range(bins // 2):
-        picked = []
-        for p in range(slots):
-            y = jnp.zeros(y_refs[0].shape[1:], y_refs[0].dtype)
-            for o, y_ref in enumerate(y_refs):
-                y = jnp.where(sel_ref[p] == o, y_ref[j], y)
-            picked.append(y)
-        ycat = jnp.concatenate(picked, axis=0)
+        ycat = pick_ref[j]
         for h in range(2):
             b = 2 * j + h
             r = lax.dot_general(
                 lx_ref[b], ycat, (((1,), (1,)), ((), ())), preferred_element_type=jnp.float32
             )
-            r = r * scale
             for p in range(slots):
                 src = (2 * p + h) * s
                 for x in range(2):
@@ -77,16 +81,16 @@
     nb, two_s, k = lx.shape
     s = two_s // 2
     step = BINS_PER_STEP
-    kernel = lambda *refs: cross_kernel(1.0 / windows, *refs)
     y_spec = pl.BlockSpec((step // 2, two_s, k), lambda g, sel: (g, 0, 0))
     grid_spec = pltpu.PrefetchScalarGridSpec(
         num_scalar_prefetch=1,
         grid=(nb // step,),
         in_specs=[pl.BlockSpec((step, two_s, k), lambda g, sel: (g, 0, 0))] + [y_spec] * len(ys),
         out_specs=pl.BlockSpec((slots, s, step * two_s), lambda g, sel: (0, 0, g)),
+        scratch_shapes=[pltpu.VMEM((step // 2, slots * two_s, k), lx.dtype)],
     )
     return pl.pallas_call(
-        kernel,
+        cross_kernel,
         grid_spec=grid_spec,
         out_shape=jax.ShapeDtypeStruct((slots, s, nb * two_s), jnp.float32),
     )(sel, lx, *ys)
@@ -128,6 +132,7 @@
     x_re = spec[:, :, :windows]
     x_im = spec[:, :, windows:]
     lx = jnp.concatenate([spec, jnp.concatenate([-x_im, x_re], axis=2)], axis=1)
+    lx = lx * jnp.asarray(1.0 / windows, lx.dtype)
     result = cross_block(sel, lx, ys, windows, slots)
     return result[None]
 

time: 55.4 us -> 56 us (1.011)
    mul x0 -> x1, other arithmetic: none -> 1.13 us  [body(): lx = lx * jnp.asarray(1.0 / windows, lx.dtype)]
    concatenate x1 -> x0, other arithmetic: 1.05 us -> none  [body(): lx = jnp.concatenate([spec, jnp.concatenate([-x_im, x_re], axis=2)], axis=1)]
where the time goes in v6:
time: 56 us; the launch traced here: 54.9 us
  starting transfers between devices  12.3 us (22%)
  blocking collectives  11.6 us (21%)
  matrix products  10.1 us (18%)
  Pallas kernels  7.21 us (13%)
  local copies, waits for them, and re-layouts  6.91 us (12%)
  other arithmetic  4.92 us (9%)
  between operations  0.96 us (2%)
  waiting for transfers between devices  0.9 us (2%)
    ppermute x6, starting transfers between devices, passed_along(): return lax.ppermute(array, axis, pairs)  12.3 us
    all_to_all x1, blocking collectives, body(): lax.all_to_all(own_spec, 'tm', split_axis=3, concat_axis=2, tiled=True)  11.6 us
    dot_general x1, matrix products, whiten(): jnp.einsum('swn,nk->swk', records, dft_table, precision=lax.Precision.HIGH)  10.1 us
    pallas_call x1, Pallas kernels, cross_block(): pl.pallas_call(cross_kernel, grid_spec=grid_spec, out_shape=jax.ShapeDtyp...  7.21 us
    unnamed x24, local copies, waits for them, and re-layouts  3.6 us
    transpose x1, local copies, waits for them, and re-layouts, body(): spec = regrouped.reshape(stations, windows, 2, nb).transpose(3, 0, 2, 1)....  1.31 us
    sub x1, other arithmetic, dft_columns(): cosine = c1 * c2 - s1 * s2  1.17 us
    select_n x1, other arithmetic, dft_columns(): table = jnp.where(part_of[None, None, :] == 0, cosine, minus_sine)  1.14 us
  transfers between devices with their start and end apart: 6, of which 1 were waited for; matrix products, arithmetic and copies ran while one was open for 4% of the time, Pallas kernels for 0%

profile of v6, /device:TPU:0, one launch (start us, length us, event | category | flops | bytes accessed | tf_op | source)
XLA Modules:
  0.0 54.9 jit_solution(5182873267869753244)
XLA Ops:
  0.0 0.6 %fusion.16 = (f32[64,256]{1,0:T(8,128)S(1)}, f32[64,256]{1,0:T(8,128)S(1)}, f32[64,256]{1,0:T(8,128)S(1)}, f32[64,256]{1,0:T(8,128)S(1)}) fusion(s32[256]{0:T(256)S(1)} %fusion.21, s32[64]{0:T(128)S(1)} %iota_multiply_fusion), kind=kLoop, calls=%fused_computation.31 | loop fusion | flops 458752 | bytes 263424 | tf_op jit(solution)/shard_map/cos | solution.py:32
  0.6 0.0 slice-start
  0.6 1.2 %multiply_subtract_fusion = (f32[64,64,256]{2,1,0:T(8,128)S(1)}, f32[64,64,256]{2,1,0:T(8,128)S(1)}) fusion(f32[64,256]{1,0:T(8,128)S(1)} %get-tuple-element.11, f32[64,256]{1,0:T(8,128)S(1)} %get-tuple-element.10, f32[64,256]{1,0:T(8,128)S(1)} %get-tuple-element.12, f32[64,256]{1,0:T(8,128)S(1)} %get-tuple-element.9), kind=kLoop, calls=%fused_computation.5 | loop fusion | flops 7340032 | bytes 8650752 | tf_op jit(solution)/shard_map/sub | solution.py:36
  1.8 0.0 slice-start.2
  1.8 1.1 %bitcast_select_fusion = f32[4096,256]{1,0:T(8,128)S(1)} fusion(f32[64,64,256]{2,1,0:T(8,128)S(1)} %get-tuple-element.8, f32[64,64,256]{2,1,0:T(8,128)S(1)} %get-tuple-element.7, pred[256]{0:T(512)(128)(4,1)S(1)} %fusion.24), kind=kLoop, calls=%fused_computation.3 | loop fusion | flops 1048576 | bytes 12583168 | tf_op jit(solution)/shard_map/jit(_where)/select_n | solution.py:38
  2.9 1.1 %slice-done.1 = s8[4194304]{0:T(1024)(128)(4,1)S(1)} async-done(((s8[10485760]{0:T(1024)(128)(4,1)}), s8[4194304]{0:T(1024)(128)(4,1)S(1)}, s32[]{:S(2)}) %slice-start.1) | async-done | bytes 4194328
  4.0 0.8 %slice-done.2 = s8[2097152]{0:T(1024)(128)(4,1)S(1)} async-done(((s8[10485760]{0:T(1024)(128)(4,1)}), s8[2097152]{0:T(1024)(128)(4,1)S(1)}, s32[]{:S(2)}) %slice-start.2) | async-done | bytes 2097176
  4.9 10.1 %multiply_reduce_fusion = (f32[40,16]{0,1:T(8,128)S(1)}, f32[256,40,16]{0,1,2:T(8,128)S(1)}) fusion(f32[40,16,4096]{2,1,0:T(8,128)S(1)} %bitcast.35, f32[4096,256]{1,0:T(8,128)S(1)} %bitcast_select_fusion), kind=kOutput, calls=%fused_computation.8 | convolution fusion | flops 4026859008 | bytes 15337984 | tf_op jit(solution)/shard_map/swn,nk->swk/dot_general | solution.py:44
  15.0 0.2 fusion.3
  15.2 0.3 reshape.214
  15.5 0.3 copy.19
  15.8 0.5 reshape.222
  16.2 11.6 %all_to_all.15 = bf16[4,2,20480]{2,1,0:T(2,128)(2,1)S(1)} all-to-all(bf16[4,2,20480]{2,1,0:T(2,128)(2,1)S(1)} %reshape.222), channel_id=1, replica_groups=mesh['tm'=4,'sta'=8] {'tm'}, dimensions={0} | all-to-all | bytes 655360 | tf_op jit(solution)/shard_map/all_to_all | solution.py:105
  27.8 0.4 reshape.223
  28.2 0.1 bitcast_bitcast_fusion
  28.4 0.8 %copy.11 = bf16[1,40,4,16,1,64]{1,5,3,2,4,0:T(8,128)(2,1)S(1)} copy(bf16[1,40,4,16,1,64]{5,3,1,2,4,0:T(8,128)(2,1)S(1)} %bitcast_bitcast_fusion) | data formatting | bytes 655360 | tf_op jit(solution)/shard_map/all_to_all | solution.py:105
  29.1 1.3 %copy.12 = bf16[32,40,2,64]{3,2,1,0:T(2,128)(2,1)S(1)} copy(bf16[32,40,2,64]{1,0,2,3:T(8,128)(2,1)S(1)} %bitcast.32) | data formatting | bytes 655360 | tf_op jit(solution)/shard_map/transpose | solution.py:110
  30.5 0.3 reshape_reshape.3.refs_3_
  30.8 1.3 %collective-permute-start.1 = (bf16[16,80,128]{2,1,0:T(8,128)(2,1)S(1)}, bf16[16,80,128]{2,1,0:T(8,128)(2,1)S(1)}, u32[]{:S(2)}, u32[]{:S(2)}) collective-permute-start(bf16[16,80,128]{2,1,0:T(8,128)(2,1)S(1)} %reshape_reshape.3.refs_3_), channel_id=1, source_target_pairs={{0,1},{1,2},{2,3},{3,4},{4,5},{5,6},{6,7},{8,9},{9,10},{10,11},{11... | collective-permute-start | bytes 983048 | tf_op jit(solution)/shard_map/ppermute | solution.py:18
  32.1 1.3 %collective-permute-start.3 = (bf16[16,80,128]{2,1,0:T(8,128)(2,1)S(1)}, bf16[16,80,128]{2,1,0:T(8,128)(2,1)S(1)}, u32[]{:S(2)}, u32[]{:S(2)}) collective-permute-start(bf16[16,80,128]{2,1,0:T(8,128)(2,1)S(1)} %reshape_reshape.3.refs_3_), channel_id=1, source_target_pairs={{1,0},{2,1},{3,2},{4,3},{5,4},{6,5},{7,6},{9,8},{10,9},{11,10},{12... | collective-permute-start | bytes 983048 | tf_op jit(solution)/shard_map/ppermute | solution.py:18
  34.0 0.6 %compare_select_fusion.4.sel_ref = s32[5]{0:T(128)} fusion(s32[1,5]{1,0:T(1,128)S(1)} %copy-done.7, s32[]{:T(128)S(6)} %sub.29, s32[]{:T(128)S(6)} %select_n.81, s32[]{:T(128)S(6)} %axis_index.12, s32[]{:T(128)} %bitcast.31), kind=kLoop, calls=%fused_computation.44 | loop fusion | flops 50 | bytes 56 | tf_op jit(solution)/shard_map/jit(_where)/select_n | solution.py:131
  34.6 0.3 reshape.216
  34.9 6.5 %collective-permute-start = (bf16[16,80,128]{2,1,0:T(8,128)(2,1)S(1)}, bf16[16,80,128]{2,1,0:T(8,128)(2,1)S(1)}, u32[]{:S(2)}, u32[]{:S(2)}) collective-permute-start(bf16[16,80,128]{2,1,0:T(8,128)(2,1)S(1)} %reshape_reshape.3.refs_3_), channel_id=1, source_target_pairs={{0,2},{2,4},{4,6},{8,10},{10,12},{12,14},{16,18},{18,20},{20,22},{... | collective-permute-start | bytes 983048 | tf_op jit(solution)/shard_map/ppermute | solution.py:18
  41.4 0.7 %collective-permute-start.4 = (bf16[16,80,128]{2,1,0:T(8,128)(2,1)S(1)}, bf16[16,80,128]{2,1,0:T(8,128)(2,1)S(1)}, u32[]{:S(2)}, u32[]{:S(2)}) collective-permute-start(bf16[16,80,128]{2,1,0:T(8,128)(2,1)S(1)} %reshape_reshape.3.refs_3_), channel_id=1, source_target_pairs={{3,1},{5,3},{7,5},{11,9},{13,11},{15,13},{19,17},{21,19},{23,21},{... | collective-permute-start | bytes 983048 | tf_op jit(solution)/shard_map/ppermute | solution.py:18
  42.1 1.3 %collective-permute-start.2 = (bf16[16,80,128]{2,1,0:T(8,128)(2,1)S(1)}, bf16[16,80,128]{2,1,0:T(8,128)(2,1)S(1)}, u32[]{:S(2)}, u32[]{:S(2)}) collective-permute-start(bf16[16,80,128]{2,1,0:T(8,128)(2,1)S(1)} %collective-permute-done.1.refs_2_), channel_id=1, source_target_pairs={{0,1},{2,3},{4,5},{6,7},{8,9},{10,11},{12,13},{14,15},{16,17},{18,... | collective-permute-start | bytes 983048 | tf_op jit(solution)/shard_map/ppermute | solution.py:18
  43.4 1.3 %collective-permute-start.5 = (bf16[16,80,128]{2,1,0:T(8,128)(2,1)S(1)}, bf16[16,80,128]{2,1,0:T(8,128)(2,1)S(1)}, u32[]{:S(2)}, u32[]{:S(2)}) collective-permute-start(bf16[16,80,128]{2,1,0:T(8,128)(2,1)S(1)} %collective-permute-done.3.refs_4_), channel_id=1, source_target_pairs={{1,0},{3,2},{5,4},{7,6},{9,8},{11,10},{13,12},{15,14},{17,16},{19,... | collective-permute-start | bytes 983048 | tf_op jit(solution)/shard_map/ppermute | solution.py:18
  44.7 0.2 slice_negate_fusion
  44.9 1.1 %maximum_multiply_fusion.lx_ref = bf16[32,80,128]{2,1,0:T(8,128)(2,1)} fusion(bf16[32,40,64]{2,1,0:T(8,128)(2,1)S(1)} %get-tuple-element.6, bf16[32,40,64]{2,1,0:T(8,128)(2,1)S(1)} %get-tuple-element.5, bf16[32,40,128]{2,1,0:T(8,128)(2,1)S(1)} %reshape.216), kind=kLoop, calls=%fused_computation.6 | loop fusion | flops 2621440 | bytes 1310720 | tf_op jit(solution)/shard_map/mul | solution.py:135
  46.1 0.9 %collective-permute-done.5.refs_6_ = bf16[16,80,128]{2,1,0:T(8,128)(2,1)S(1)} collective-permute-done((bf16[16,80,128]{2,1,0:T(8,128)(2,1)S(1)}, bf16[16,80,128]{2,1,0:T(8,128)(2,1)S(1)}, u32[]{:S(2)}, u32[]{:S(2)}) %collective-permute-start.5) | collective-permute-done | bytes 327712 | tf_op jit(solution)/shard_map/ppermute | solution.py:18
  47.0 0.0 copy-done.5
  47.0 0.7 %copy-done.6 = bf16[16,80,128]{2,1,0:T(8,128)(2,1)} copy-done((bf16[16,80,128]{2,1,0:T(8,128)(2,1)}, bf16[16,80,128]{2,1,0:T(8,128)(2,1)S(1)}, u32[]{:S(2)}) %copy-start.6) | copy-done | bytes 327704
  47.7 7.2 %shard_map.37 = f32[5,40,2560]{2,1,0:T(8,128)} custom-call(s32[5]{0:T(128)} %compare_select_fusion.4.sel_ref, bf16[32,80,128]{2,1,0:T(8,128)(2,1)} %maximum_multiply_fusion.lx_ref, bf16[16,80,128]{2,1,0:T(8,128)(2,1)} %copy-done.3, bf16[16,80,128]{2,1,0:T(8,128)(2,1)} %copy-done.5, bf16[16,80,128]{2,1,0:T(8,128)(2,1)} %copy-done.1, ...), custom_call_target="tpu_custom_call" | custom-call | tf_op jit(solution)/shard_map/pallas_call | solution.py:92
  (26 shorter events, 0.1 us)
Async XLA Ops:
  0.6 2.4 %slice-start = ((s8[10485760]{0:T(1024)(128)(4,1)}), s8[4194304]{0:T(1024)(128)(4,1)S(1)}, s32[]{:S(2)}) async-start(s8[10485760]{0:T(1024)(128)(4,1)} %bitcast.34), calls=%async_computation.1 | async-start | bytes 8388608
  0.6 3.5 %slice-start.1 = ((s8[10485760]{0:T(1024)(128)(4,1)}), s8[4194304]{0:T(1024)(128)(4,1)S(1)}, s32[]{:S(2)}) async-start(s8[10485760]{0:T(1024)(128)(4,1)} %bitcast.34), calls=%async_computation.2 | async-start | bytes 8388608
  1.8 3.1 %slice-start.2 = ((s8[10485760]{0:T(1024)(128)(4,1)}), s8[2097152]{0:T(1024)(128)(4,1)S(1)}, s32[]{:S(2)}) async-start(s8[10485760]{0:T(1024)(128)(4,1)} %bitcast.34), calls=%async_computation.3 | async-start | bytes 4194304
  15.8 18.3 %copy-start.7 = (s32[1,5]{1,0:T(1,128)S(1)}, s32[1,5]{1,0:T(1,128)}, u32[]{:S(2)}) copy-start(s32[1,5]{1,0:T(1,128)} %param.4) | copy-start | bytes 64
  30.8 16.2 %copy-start = (bf16[16,80,128]{2,1,0:T(8,128)(2,1)}, bf16[16,80,128]{2,1,0:T(8,128)(2,1)S(1)}, u32[]{:S(2)}) copy-start(bf16[16,80,128]{2,1,0:T(8,128)(2,1)S(1)} %reshape_reshape.3.refs_3_) | copy-start | bytes 983044
  30.8 11.3 %collective-permute-start.1 = (bf16[16,80,128]{2,1,0:T(8,128)(2,1)S(1)}, bf16[16,80,128]{2,1,0:T(8,128)(2,1)S(1)}, u32[]{:S(2)}, u32[]{:S(2)}) collective-permute-start(bf16[16,80,128]{2,1,0:T(8,128)(2,1)S(1)} %reshape_reshape.3.refs_3_), channel_id=1, source_target_pairs={{0,1},{1,2},{2,3},{3,4},{4,5},{5,6},{6,7},{8,9},{9,10},{10,11},{11... | collective-permute-start | bytes 983048 | tf_op jit(solution)/shard_map/ppermute | solution.py:18
  32.1 11.3 %collective-permute-start.3 = (bf16[16,80,128]{2,1,0:T(8,128)(2,1)S(1)}, bf16[16,80,128]{2,1,0:T(8,128)(2,1)S(1)}, u32[]{:S(2)}, u32[]{:S(2)}) collective-permute-start(bf16[16,80,128]{2,1,0:T(8,128)(2,1)S(1)} %reshape_reshape.3.refs_3_), channel_id=1, source_target_pairs={{1,0},{2,1},{3,2},{4,3},{5,4},{6,5},{7,6},{9,8},{10,9},{11,10},{12... | collective-permute-start | bytes 983048 | tf_op jit(solution)/shard_map/ppermute | solution.py:18
  34.9 11.1 %collective-permute-start = (bf16[16,80,128]{2,1,0:T(8,128)(2,1)S(1)}, bf16[16,80,128]{2,1,0:T(8,128)(2,1)S(1)}, u32[]{:S(2)}, u32[]{:S(2)}) collective-permute-start(bf16[16,80,128]{2,1,0:T(8,128)(2,1)S(1)} %reshape_reshape.3.refs_3_), channel_id=1, source_target_pairs={{0,2},{2,4},{4,6},{8,10},{10,12},{12,14},{16,18},{18,20},{20,22},{... | collective-permute-start | bytes 983048 | tf_op jit(solution)/shard_map/ppermute | solution.py:18
  41.4 4.7 %collective-permute-start.4 = (bf16[16,80,128]{2,1,0:T(8,128)(2,1)S(1)}, bf16[16,80,128]{2,1,0:T(8,128)(2,1)S(1)}, u32[]{:S(2)}, u32[]{:S(2)}) collective-permute-start(bf16[16,80,128]{2,1,0:T(8,128)(2,1)S(1)} %reshape_reshape.3.refs_3_), channel_id=1, source_target_pairs={{3,1},{5,3},{7,5},{11,9},{13,11},{15,13},{19,17},{21,19},{23,21},{... | collective-permute-start | bytes 983048 | tf_op jit(solution)/shard_map/ppermute | solution.py:18
  42.1 4.9 %copy-start.1 = (bf16[16,80,128]{2,1,0:T(8,128)(2,1)}, bf16[16,80,128]{2,1,0:T(8,128)(2,1)S(1)}, u32[]{:S(2)}) copy-start(bf16[16,80,128]{2,1,0:T(8,128)(2,1)S(1)} %collective-permute-done.1.refs_2_) | copy-start | bytes 983044
  42.1 4.0 %collective-permute-start.2 = (bf16[16,80,128]{2,1,0:T(8,128)(2,1)S(1)}, bf16[16,80,128]{2,1,0:T(8,128)(2,1)S(1)}, u32[]{:S(2)}, u32[]{:S(2)}) collective-permute-start(bf16[16,80,128]{2,1,0:T(8,128)(2,1)S(1)} %collective-permute-done.1.refs_2_), channel_id=1, source_target_pairs={{0,1},{2,3},{4,5},{6,7},{8,9},{10,11},{12,13},{14,15},{16,17},{18,... | collective-permute-start | bytes 983048 | tf_op jit(solution)/shard_map/ppermute | solution.py:18
  43.4 3.5 %copy-start.2 = (bf16[16,80,128]{2,1,0:T(8,128)(2,1)}, bf16[16,80,128]{2,1,0:T(8,128)(2,1)S(1)}, u32[]{:S(2)}) copy-start(bf16[16,80,128]{2,1,0:T(8,128)(2,1)S(1)} %collective-permute-done.3.refs_4_) | copy-start | bytes 983044
  43.4 3.5 %collective-permute-start.5 = (bf16[16,80,128]{2,1,0:T(8,128)(2,1)S(1)}, bf16[16,80,128]{2,1,0:T(8,128)(2,1)S(1)}, u32[]{:S(2)}, u32[]{:S(2)}) collective-permute-start(bf16[16,80,128]{2,1,0:T(8,128)(2,1)S(1)} %collective-permute-done.3.refs_4_), channel_id=1, source_target_pairs={{1,0},{3,2},{5,4},{7,6},{9,8},{11,10},{13,12},{15,14},{17,16},{19,... | collective-permute-start | bytes 983048 | tf_op jit(solution)/shard_map/ppermute | solution.py:18
  46.0 0.9 %copy-start.3 = (bf16[16,80,128]{2,1,0:T(8,128)(2,1)}, bf16[16,80,128]{2,1,0:T(8,128)(2,1)S(1)}, u32[]{:S(2)}) copy-start(bf16[16,80,128]{2,1,0:T(8,128)(2,1)S(1)} %collective-permute-done.refs_0_) | copy-start | bytes 983044
  46.0 0.9 %copy-start.4 = (bf16[16,80,128]{2,1,0:T(8,128)(2,1)}, bf16[16,80,128]{2,1,0:T(8,128)(2,1)S(1)}, u32[]{:S(2)}) copy-start(bf16[16,80,128]{2,1,0:T(8,128)(2,1)S(1)} %collective-permute-done.4.refs_5_) | copy-start | bytes 983044
  46.1 0.9 %copy-start.5 = (bf16[16,80,128]{2,1,0:T(8,128)(2,1)}, bf16[16,80,128]{2,1,0:T(8,128)(2,1)S(1)}, u32[]{:S(2)}) copy-start(bf16[16,80,128]{2,1,0:T(8,128)(2,1)S(1)} %collective-permute-done.2.refs_1_) | copy-start | bytes 983044
  47.0 0.7 %copy-start.6 = (bf16[16,80,128]{2,1,0:T(8,128)(2,1)}, bf16[16,80,128]{2,1,0:T(8,128)(2,1)S(1)}, u32[]{:S(2)}) copy-start(bf16[16,80,128]{2,1,0:T(8,128)(2,1)S(1)} %collective-permute-done.5.refs_6_) | copy-start | bytes 983044

commit v7 on v5

--- a/solution.py
+++ b/solution.py
@@ -18,7 +18,7 @@
     return lax.ppermute(array, axis, pairs)
 
 
-def dft_columns(samples, bins, groups):
+def dft_factors(samples, bins, groups):
     local = bins // groups
     column = jnp.arange(2 * bins, dtype=jnp.int32)
     group_of = column // (2 * local)
@@ -29,22 +29,66 @@
     unit = 2.0 * math.pi / samples
     outer = (jnp.arange(coarse, dtype=jnp.int32)[:, None] * fine * harmonic[None, :]) % samples
     inner = (jnp.arange(fine, dtype=jnp.int32)[:, None] * harmonic[None, :]) % samples
-    c1 = jnp.cos(outer.astype(jnp.float32) * unit)[:, None, :]
-    s1 = jnp.sin(outer.astype(jnp.float32) * unit)[:, None, :]
-    c2 = jnp.cos(inner.astype(jnp.float32) * unit)[None, :, :]
-    s2 = jnp.sin(inner.astype(jnp.float32) * unit)[None, :, :]
-    cosine = c1 * c2 - s1 * s2
-    minus_sine = -(s1 * c2 + c1 * s2)
-    table = jnp.where(part_of[None, None, :] == 0, cosine, minus_sine)
-    return table.reshape(samples, 2 * bins)
+    c1 = jnp.cos(outer.astype(jnp.float32) * unit)
+    s1 = jnp.sin(outer.astype(jnp.float32) * unit)
+    c2 = jnp.cos(inner.astype(jnp.float32) * unit)
+    s2 = jnp.sin(inner.astype(jnp.float32) * unit)
+    is_cos = part_of[None, :] == 0
+    p1 = jnp.where(is_cos, c1, -s1)
+    q1 = jnp.where(is_cos, -s1, -c1)
+    return p1, q1, c2, s2
+
+
+def split_bf16(v):
+    hi = v.astype(jnp.bfloat16)
+    lo = (v - hi.astype(jnp.float32)).astype(jnp.bfloat16)
+    return hi, lo
+
+
+def dft_kernel(p1_ref, q1_ref, c2_ref, s2_ref, x_ref, o_ref, acc_ref):
+    k = pl.program_id(0)
+
+    @pl.when(k == 0)
+    def _():
+        acc_ref[...] = jnp.zeros(acc_ref.shape, acc_ref.dtype)
+
+    c2 = c2_ref[...]
+    s2 = s2_ref[...]
+    rows = [p1_ref[a:a + 1, :] * c2 + q1_ref[a:a + 1, :] * s2 for a in range(p1_ref.shape[0])]
+    t_hi, t_lo = split_bf16(jnp.concatenate(rows, axis=0))
+    x_hi, x_lo = split_bf16(x_ref[...])
+    dot = lambda a, b: jnp.dot(a, b, preferred_element_type=jnp.float32)
+    acc_ref[...] += dot(x_hi, t_hi) + dot(x_hi, t_lo) + dot(x_lo, t_hi)
+
+    @pl.when(k == pl.num_programs(0) - 1)
+    def _():
+        spectra = acc_ref[...]
+        mean_power = jnp.mean(spectra * spectra, axis=1, keepdims=True)
+        o_ref[...] = (spectra / jnp.sqrt(mean_power + 1e-06)).astype(o_ref.dtype)
 
 
 def whiten(records, groups):
-    dft_table = dft_columns(records.shape[2], BINS, groups)
-    spectra = jnp.einsum("swn,nk->swk", records, dft_table, precision=lax.Precision.HIGH)
-    mean_power = jnp.mean(spectra * spectra, axis=2, keepdims=True)
-    white = (spectra / jnp.sqrt(mean_power + 1e-06)).astype(jnp.bfloat16)
-    return white.reshape(1, records.shape[0], records.shape[1], groups, 2 * (BINS // groups))
+    stations, windows, samples = records.shape
+    p1, q1, c2, s2 = dft_factors(samples, BINS, groups)
+    fine, width = c2.shape
+    coarse_step = 8
+    rows = stations * windows
+    x = records.reshape(rows, samples)
+    white = pl.pallas_call(
+        dft_kernel,
+        grid=(samples // (fine * coarse_step),),
+        in_specs=[
+            pl.BlockSpec((coarse_step, width), lambda k: (k, 0)),
+            pl.BlockSpec((coarse_step, width), lambda k: (k, 0)),
+            pl.BlockSpec((fine, width), lambda k: (0, 0)),
+            pl.BlockSpec((fine, width), lambda k: (0, 0)),
+            pl.BlockSpec((rows, fine * coarse_step), lambda k: (0, k)),
+        ],
+        out_specs=pl.BlockSpec((rows, width), lambda k: (0, 0)),
+        out_shape=jax.ShapeDtypeStruct((rows, width), jnp.bfloat16),
+        scratch_shapes=[pltpu.VMEM((rows, width), jnp.float32)],
+    )(p1, q1, c2, s2, x)
+    return white.reshape(1, stations, windows, groups, width // groups)
 
 
 def cross_kernel(scale, sel_ref, lx_ref, *refs):

time: 55.4 us -> 52.7 us (0.951)
  Pallas kernels: 6.68 us -> 17.1 us
  matrix products: 10.1 us -> 0 us
  other arithmetic: 4.85 us -> 2.97 us
  waiting for transfers between devices: 0.97 us -> 0.02 us
  starting transfers between devices: 12.3 us -> 12.9 us
    pallas_call x0 -> x1, Pallas kernels: none -> 10.4 us  [whiten(): pl.pallas_call(dft_kernel, grid=(samples // (fine * coarse_step),), in_sp...]
    dot_general x1 -> x0, matrix products: 10.1 us -> none  [whiten(): jnp.einsum('swn,nk->swk', records, dft_table, precision=lax.Precision.HIGH)]
    sub x1 -> x0, other arithmetic: 1.17 us -> none  [dft_columns(): cosine = c1 * c2 - s1 * s2]
    unnamed x24 -> x18, local copies, waits for them, and re-layouts: 3.6 us -> 2.56 us
    ppermute x6, waiting for transfers between devices: 0.97 us -> 0.02 us  [passed_along(): return lax.ppermute(array, axis, pairs)]
    reshape x2, local copies, waits for them, and re-layouts: 0.54 us -> 1.4 us  [whiten(): return white.reshape(1, stations, windows, groups, width // groups)]
    cos x1 -> x0, other arithmetic: 0.55 us -> none  [dft_columns(): c1 = jnp.cos(outer.astype(jnp.float32) * unit)[:, None, :]]
  transfers between devices with their start and end apart: 6 -> 6, of which waited for: 1 -> 0; matrix products, arithmetic and copies ran while one was open for 4% -> 4% of each run, Pallas kernels for 0% -> 0%
where the time goes in v7:
time: 52.7 us; the launch traced here: 52.1 us
  Pallas kernels  17.1 us (32%)
  starting transfers between devices  12.9 us (24%)
  blocking collectives  11.5 us (22%)
  local copies, waits for them, and re-layouts  6.73 us (13%)
  other arithmetic  2.97 us (6%)
  between operations  0.9 us (2%)
    ppermute x6, starting transfers between devices, passed_along(): return lax.ppermute(array, axis, pairs)  12.9 us
    all_to_all x1, blocking collectives, body(): lax.all_to_all(own_spec, 'tm', split_axis=3, concat_axis=2, tiled=True)  11.5 us
    pallas_call x1, Pallas kernels, whiten(): pl.pallas_call(dft_kernel, grid=(samples // (fine * coarse_step),), in_sp...  10.4 us
    pallas_call x1, Pallas kernels, cross_block(): pl.pallas_call(kernel, grid_spec=grid_spec, out_shape=jax.ShapeDtypeStruc...  6.68 us
    unnamed x18, local copies, waits for them, and re-layouts  2.56 us
    reshape x2, local copies, waits for them, and re-layouts, whiten(): return white.reshape(1, stations, windows, groups, width // groups)  1.4 us
    transpose x1, local copies, waits for them, and re-layouts, body(): spec = regrouped.reshape(stations, windows, 2, nb).transpose(3, 0, 2, 1)....  1.31 us
    select_n x1, other arithmetic, dft_factors(): q1 = jnp.where(is_cos, -s1, -c1)  1.26 us
  transfers between devices with their start and end apart: 6, of which 0 were waited for; matrix products, arithmetic and copies ran while one was open for 4% of the time, Pallas kernels for 0%

profile of v7, /device:TPU:0, one launch (start us, length us, event | category | flops | bytes accessed | tf_op | source)
XLA Modules:
  0.0 52.1 jit_solution(6573791411118837671)
XLA Ops:
  0.0 1.3 %negate_select_fusion.3 = (f32[64,256]{1,0:T(8,128)}, f32[64,256]{1,0:T(8,128)}, f32[64,256]{1,0:T(8,128)}, f32[64,256]{1,0:T(8,128)}) fusion(s32[256]{0:T(256)S(1)} %fusion.17, s32[64]{0:T(128)S(1)} %iota_multiply_fusion, pred[256]{0:T(512)(128)(4,1)S(1)} %fusion.20), kind=kLoop, calls=%fused_computation.18 | loop fusion | flops 524288 | bytes 263680 | tf_op jit(solution)/shard_map/jit(_where)/select_n | solution.py:38
  1.3 10.4 %shard_map.37 = bf16[640,256]{1,0:T(8,128)(2,1)} custom-call(f32[64,256]{1,0:T(8,128)} %get-tuple-element.8.p1_ref, f32[64,256]{1,0:T(8,128)} %get-tuple-element.7.q1_ref, f32[64,256]{1,0:T(8,128)} %get-tuple-element.10.c2_ref, f32[64,256]{1,0:T(8,128)} %get-tuple-element.9.s2_ref, f32[640,4096]{1,0:T(8,128)} %bitcast.20), custom_call_target="tpu_custom_call" | custom-call | tf_op jit(solution)/shard_map/pallas_call | solution.py:77
  11.7 1.3 %reshape.79 = bf16[1,40,16,4,64]{4,3,2,1,0:T(4,128)(2,1)S(1)} reshape(bf16[640,256]{1,0:T(8,128)(2,1)} %shard_map.37) | data formatting | bytes 655360 | tf_op jit(solution)/shard_map/reshape | solution.py:91
  13.0 0.1 copy.12
  13.1 0.5 reshape.86
  13.6 11.5 %all_to_all.15 = bf16[4,2,20480]{2,1,0:T(2,128)(2,1)S(1)} all-to-all(bf16[4,2,20480]{2,1,0:T(2,128)(2,1)S(1)} %reshape.86), channel_id=1, replica_groups=mesh['tm'=4,'sta'=8] {'tm'}, dimensions={0} | all-to-all | bytes 655360 | tf_op jit(solution)/shard_map/all_to_all | solution.py:145
  25.2 0.4 reshape.87
  25.6 0.1 bitcast_bitcast_fusion
  25.7 0.8 %copy.8 = bf16[1,40,4,16,1,64]{1,5,3,2,4,0:T(8,128)(2,1)S(1)} copy(bf16[1,40,4,16,1,64]{5,3,1,2,4,0:T(8,128)(2,1)S(1)} %bitcast_bitcast_fusion) | data formatting | bytes 655360 | tf_op jit(solution)/shard_map/all_to_all | solution.py:145
  26.5 0.0 copy-start.7
  26.5 1.3 %copy.9 = bf16[32,40,2,64]{3,2,1,0:T(2,128)(2,1)S(1)} copy(bf16[32,40,2,64]{1,0,2,3:T(8,128)(2,1)S(1)} %bitcast.21) | data formatting | bytes 655360 | tf_op jit(solution)/shard_map/transpose | solution.py:150
  27.8 0.3 reshape_reshape.3.refs_5_
  28.1 1.3 %collective-permute-start.3 = (bf16[16,80,128]{2,1,0:T(8,128)(2,1)S(1)}, bf16[16,80,128]{2,1,0:T(8,128)(2,1)S(1)}, u32[]{:S(2)}, u32[]{:S(2)}) collective-permute-start(bf16[16,80,128]{2,1,0:T(8,128)(2,1)S(1)} %reshape_reshape.3.refs_5_), channel_id=1, source_target_pairs={{1,0},{2,1},{3,2},{4,3},{5,4},{6,5},{7,6},{9,8},{10,9},{11,10},{12... | collective-permute-start | bytes 983048 | tf_op jit(solution)/shard_map/ppermute | solution.py:18
  29.4 3.1 %collective-permute-start.1 = (bf16[16,80,128]{2,1,0:T(8,128)(2,1)S(1)}, bf16[16,80,128]{2,1,0:T(8,128)(2,1)S(1)}, u32[]{:S(2)}, u32[]{:S(2)}) collective-permute-start(bf16[16,80,128]{2,1,0:T(8,128)(2,1)S(1)} %reshape_reshape.3.refs_5_), channel_id=1, source_target_pairs={{0,1},{1,2},{2,3},{3,4},{4,5},{5,6},{6,7},{8,9},{9,10},{10,11},{11... | collective-permute-start | bytes 983048 | tf_op jit(solution)/shard_map/ppermute | solution.py:18
  33.2 0.5 compare_select_fusion.4.refs_0_
  33.6 0.3 reshape.81
  33.9 0.7 %collective-permute-start.4 = (bf16[16,80,128]{2,1,0:T(8,128)(2,1)S(1)}, bf16[16,80,128]{2,1,0:T(8,128)(2,1)S(1)}, u32[]{:S(2)}, u32[]{:S(2)}) collective-permute-start(bf16[16,80,128]{2,1,0:T(8,128)(2,1)S(1)} %reshape_reshape.3.refs_5_), channel_id=1, source_target_pairs={{3,1},{5,3},{7,5},{11,9},{13,11},{15,13},{19,17},{21,19},{23,21},{... | collective-permute-start | bytes 983048 | tf_op jit(solution)/shard_map/ppermute | solution.py:18
  34.6 3.5 %collective-permute-start = (bf16[16,80,128]{2,1,0:T(8,128)(2,1)S(1)}, bf16[16,80,128]{2,1,0:T(8,128)(2,1)S(1)}, u32[]{:S(2)}, u32[]{:S(2)}) collective-permute-start(bf16[16,80,128]{2,1,0:T(8,128)(2,1)S(1)} %reshape_reshape.3.refs_5_), channel_id=1, source_target_pairs={{0,2},{2,4},{4,6},{8,10},{10,12},{12,14},{16,18},{18,20},{20,22},{... | collective-permute-start | bytes 983048 | tf_op jit(solution)/shard_map/ppermute | solution.py:18
  38.1 0.0 collective-permute-done.3.refs_6_
  38.1 1.3 %collective-permute-start.5 = (bf16[16,80,128]{2,1,0:T(8,128)(2,1)S(1)}, bf16[16,80,128]{2,1,0:T(8,128)(2,1)S(1)}, u32[]{:S(2)}, u32[]{:S(2)}) collective-permute-start(bf16[16,80,128]{2,1,0:T(8,128)(2,1)S(1)} %collective-permute-done.3.refs_6_), channel_id=1, source_target_pairs={{1,0},{3,2},{5,4},{7,6},{9,8},{11,10},{13,12},{15,14},{17,16},{19,... | collective-permute-start | bytes 983048 | tf_op jit(solution)/shard_map/ppermute | solution.py:18
  39.4 0.0 collective-permute-done.1.refs_4_
  39.5 3.1 %collective-permute-start.2 = (bf16[16,80,128]{2,1,0:T(8,128)(2,1)S(1)}, bf16[16,80,128]{2,1,0:T(8,128)(2,1)S(1)}, u32[]{:S(2)}, u32[]{:S(2)}) collective-permute-start(bf16[16,80,128]{2,1,0:T(8,128)(2,1)S(1)} %collective-permute-done.1.refs_4_), channel_id=1, source_target_pairs={{0,1},{2,3},{4,5},{6,7},{8,9},{10,11},{12,13},{14,15},{16,17},{18,... | collective-permute-start | bytes 983048 | tf_op jit(solution)/shard_map/ppermute | solution.py:18
  42.5 0.2 slice_negate_fusion
  42.7 1.0 %maximum_maximum_fusion.refs_1_ = bf16[32,80,128]{2,1,0:T(8,128)(2,1)} fusion(bf16[32,40,64]{2,1,0:T(8,128)(2,1)S(1)} %get-tuple-element.6, bf16[32,40,64]{2,1,0:T(8,128)(2,1)S(1)} %get-tuple-element.5, bf16[32,40,128]{2,1,0:T(8,128)(2,1)S(1)} %reshape.81), kind=kLoop, calls=%fused_computation | loop fusion | flops 1966080 | bytes 1310720 | tf_op jit(solution)/shard_map/concatenate | solution.py:174
  43.8 0.0 collective-permute-done.4.refs_7_
  43.8 0.0 collective-permute-done.5.refs_8_
  43.8 0.0 collective-permute-done.2.refs_3_
  43.8 0.7 %copy-done.3 = bf16[16,80,128]{2,1,0:T(8,128)(2,1)} copy-done((bf16[16,80,128]{2,1,0:T(8,128)(2,1)}, bf16[16,80,128]{2,1,0:T(8,128)(2,1)S(1)}, u32[]{:S(2)}) %copy-start.3) | copy-done | bytes 327704
  44.5 0.1 copy-done.4
  44.6 0.1 copy-done.5
  44.7 0.7 %copy-done.6 = bf16[16,80,128]{2,1,0:T(8,128)(2,1)} copy-done((bf16[16,80,128]{2,1,0:T(8,128)(2,1)}, bf16[16,80,128]{2,1,0:T(8,128)(2,1)S(1)}, u32[]{:S(2)}) %copy-start.6) | copy-done | bytes 327704
  45.5 6.7 %shard_map.38 = f32[5,40,2560]{2,1,0:T(8,128)} custom-call(s32[5]{0:T(128)} %compare_select_fusion.4.refs_0_, bf16[32,80,128]{2,1,0:T(8,128)(2,1)} %maximum_maximum_fusion.refs_1_, bf16[16,80,128]{2,1,0:T(8,128)(2,1)} %copy-done.4, bf16[16,80,128]{2,1,0:T(8,128)(2,1)} %copy-done.6, bf16[16,80,128]{2,1,0:T(8,128)(2,1)} %copy-done.2, ...), custom_call_target="tpu_custom_call" | custom-call | tf_op jit(solution)/shard_map/pallas_call | solution.py:132
  (15 shorter events, 0.0 us)
Async XLA Ops:
  26.5 6.6 %copy-start.7 = (s32[1,5]{1,0:T(1,128)S(1)}, s32[1,5]{1,0:T(1,128)}, u32[]{:S(2)}) copy-start(s32[1,5]{1,0:T(1,128)} %param.4) | copy-start | bytes 64
  28.1 15.6 %copy-start = (bf16[16,80,128]{2,1,0:T(8,128)(2,1)}, bf16[16,80,128]{2,1,0:T(8,128)(2,1)S(1)}, u32[]{:S(2)}) copy-start(bf16[16,80,128]{2,1,0:T(8,128)(2,1)S(1)} %reshape_reshape.3.refs_5_) | copy-start | bytes 983044
  28.1 10.0 %collective-permute-start.3 = (bf16[16,80,128]{2,1,0:T(8,128)(2,1)S(1)}, bf16[16,80,128]{2,1,0:T(8,128)(2,1)S(1)}, u32[]{:S(2)}, u32[]{:S(2)}) collective-permute-start(bf16[16,80,128]{2,1,0:T(8,128)(2,1)S(1)} %reshape_reshape.3.refs_5_), channel_id=1, source_target_pairs={{1,0},{2,1},{3,2},{4,3},{5,4},{6,5},{7,6},{9,8},{10,9},{11,10},{12... | collective-permute-start | bytes 983048 | tf_op jit(solution)/shard_map/ppermute | solution.py:18
  29.4 10.0 %collective-permute-start.1 = (bf16[16,80,128]{2,1,0:T(8,128)(2,1)S(1)}, bf16[16,80,128]{2,1,0:T(8,128)(2,1)S(1)}, u32[]{:S(2)}, u32[]{:S(2)}) collective-permute-start(bf16[16,80,128]{2,1,0:T(8,128)(2,1)S(1)} %reshape_reshape.3.refs_5_), channel_id=1, source_target_pairs={{0,1},{1,2},{2,3},{3,4},{4,5},{5,6},{6,7},{8,9},{9,10},{10,11},{11... | collective-permute-start | bytes 983048 | tf_op jit(solution)/shard_map/ppermute | solution.py:18
  33.9 9.8 %collective-permute-start.4 = (bf16[16,80,128]{2,1,0:T(8,128)(2,1)S(1)}, bf16[16,80,128]{2,1,0:T(8,128)(2,1)S(1)}, u32[]{:S(2)}, u32[]{:S(2)}) collective-permute-start(bf16[16,80,128]{2,1,0:T(8,128)(2,1)S(1)} %reshape_reshape.3.refs_5_), channel_id=1, source_target_pairs={{3,1},{5,3},{7,5},{11,9},{13,11},{15,13},{19,17},{21,19},{23,21},{... | collective-permute-start | bytes 983048 | tf_op jit(solution)/shard_map/ppermute | solution.py:18
  34.6 9.1 %collective-permute-start = (bf16[16,80,128]{2,1,0:T(8,128)(2,1)S(1)}, bf16[16,80,128]{2,1,0:T(8,128)(2,1)S(1)}, u32[]{:S(2)}, u32[]{:S(2)}) collective-permute-start(bf16[16,80,128]{2,1,0:T(8,128)(2,1)S(1)} %reshape_reshape.3.refs_5_), channel_id=1, source_target_pairs={{0,2},{2,4},{4,6},{8,10},{10,12},{12,14},{16,18},{18,20},{20,22},{... | collective-permute-start | bytes 983048 | tf_op jit(solution)/shard_map/ppermute | solution.py:18
  38.1 5.6 %copy-start.1 = (bf16[16,80,128]{2,1,0:T(8,128)(2,1)}, bf16[16,80,128]{2,1,0:T(8,128)(2,1)S(1)}, u32[]{:S(2)}) copy-start(bf16[16,80,128]{2,1,0:T(8,128)(2,1)S(1)} %collective-permute-done.3.refs_6_) | copy-start | bytes 983044
  38.1 5.6 %collective-permute-start.5 = (bf16[16,80,128]{2,1,0:T(8,128)(2,1)S(1)}, bf16[16,80,128]{2,1,0:T(8,128)(2,1)S(1)}, u32[]{:S(2)}, u32[]{:S(2)}) collective-permute-start(bf16[16,80,128]{2,1,0:T(8,128)(2,1)S(1)} %collective-permute-done.3.refs_6_), channel_id=1, source_target_pairs={{1,0},{3,2},{5,4},{7,6},{9,8},{11,10},{13,12},{15,14},{17,16},{19,... | collective-permute-start | bytes 983048 | tf_op jit(solution)/shard_map/ppermute | solution.py:18
  39.5 4.3 %copy-start.2 = (bf16[16,80,128]{2,1,0:T(8,128)(2,1)}, bf16[16,80,128]{2,1,0:T(8,128)(2,1)S(1)}, u32[]{:S(2)}) copy-start(bf16[16,80,128]{2,1,0:T(8,128)(2,1)S(1)} %collective-permute-done.1.refs_4_) | copy-start | bytes 983044
  39.5 4.3 %collective-permute-start.2 = (bf16[16,80,128]{2,1,0:T(8,128)(2,1)S(1)}, bf16[16,80,128]{2,1,0:T(8,128)(2,1)S(1)}, u32[]{:S(2)}, u32[]{:S(2)}) collective-permute-start(bf16[16,80,128]{2,1,0:T(8,128)(2,1)S(1)} %collective-permute-done.1.refs_4_), channel_id=1, source_target_pairs={{0,1},{2,3},{4,5},{6,7},{8,9},{10,11},{12,13},{14,15},{16,17},{18,... | collective-permute-start | bytes 983048 | tf_op jit(solution)/shard_map/ppermute | solution.py:18
  43.8 0.7 %copy-start.3 = (bf16[16,80,128]{2,1,0:T(8,128)(2,1)}, bf16[16,80,128]{2,1,0:T(8,128)(2,1)S(1)}, u32[]{:S(2)}) copy-start(bf16[16,80,128]{2,1,0:T(8,128)(2,1)S(1)} %collective-permute-done.4.refs_7_) | copy-start | bytes 983044
  43.8 0.8 %copy-start.4 = (bf16[16,80,128]{2,1,0:T(8,128)(2,1)}, bf16[16,80,128]{2,1,0:T(8,128)(2,1)S(1)}, u32[]{:S(2)}) copy-start(bf16[16,80,128]{2,1,0:T(8,128)(2,1)S(1)} %collective-permute-done.refs_2_) | copy-start | bytes 983044
  43.8 0.9 %copy-start.5 = (bf16[16,80,128]{2,1,0:T(8,128)(2,1)}, bf16[16,80,128]{2,1,0:T(8,128)(2,1)S(1)}, u32[]{:S(2)}) copy-start(bf16[16,80,128]{2,1,0:T(8,128)(2,1)S(1)} %collective-permute-done.5.refs_8_) | copy-start | bytes 983044
  44.7 0.7 %copy-start.6 = (bf16[16,80,128]{2,1,0:T(8,128)(2,1)}, bf16[16,80,128]{2,1,0:T(8,128)(2,1)S(1)}, u32[]{:S(2)}) copy-start(bf16[16,80,128]{2,1,0:T(8,128)(2,1)S(1)} %collective-permute-done.2.refs_3_) | copy-start | bytes 983044

commit v8 on v7

--- a/solution.py
+++ b/solution.py
@@ -151,23 +151,21 @@
         .reshape(nb, stations, 2 * windows)
     )
     paired = spec.reshape(nb // 2, 2 * stations, 2 * windows)
-    even = lambda i: i % 2 == 0
-    odd = lambda i: i % 2 == 1
+    peers = lax.axis_size("sta")
+    parity = block_index % 2
     left1 = passed_along(paired, "sta", 1)
     right1 = passed_along(paired, "sta", -1)
-    ys = [
-        passed_along(paired, "sta", 2, even),
-        passed_along(left1, "sta", 1, even),
-        left1,
-        paired,
-        right1,
-        passed_along(paired, "sta", -2, odd),
-        passed_along(right1, "sta", -1, odd),
-    ]
+    far = lax.ppermute(
+        paired, "sta", [(i, i + 2 - 4 * (i % 2)) for i in range(peers) if 0 <= i + 2 - 4 * (i % 2) < peers]
+    )
+    relay = jnp.where(parity == 0, left1, right1)
+    forwarded = lax.ppermute(
+        relay, "sta", [(i, i + 1 - 2 * (i % 2)) for i in range(peers) if 0 <= i + 1 - 2 * (i % 2) < peers]
+    )
+    ys = [far, forwarded, left1, paired, right1]
     where_at = jnp.clip(partner_row - block_index + R, 0, 2 * R)
-    parity = block_index % 2
     slot_ref = jnp.where(where_at == 0, parity, where_at + 1)
-    slot_ref = jnp.where(where_at == 2 * R, 2 * R + 2 - parity, slot_ref)
+    slot_ref = jnp.where(where_at == 2 * R, 1 - parity, slot_ref)
     sel = jnp.where(live_slots, slot_ref, -1).astype(jnp.int32)
     x_re = spec[:, :, :windows]
     x_im = spec[:, :, windows:]

time: 52.7 us -> 50.9 us (0.966)
  starting transfers between devices: 12.9 us -> 8.01 us
  waiting for transfers between devices: 0.02 us -> 3.08 us
    ppermute x6 -> x2, starting transfers between devices: 12.9 us -> 4.34 us  [passed_along(): return lax.ppermute(array, axis, pairs)]
    ppermute x0 -> x2, starting transfers between devices: none -> 3.66 us  [the longest x1 3.49 us: body(): lax.ppermute(paired, 'sta', [(i, i + 2 - 4 * (i % 2)) for i in range(peer...]
    ppermute x0 -> x2, waiting for transfers between devices: none -> 3.08 us  [the longest x1 3.08 us: body(): lax.ppermute(paired, 'sta', [(i, i + 2 - 4 * (i % 2)) for i in range(peer...]
    unnamed x18 -> x14, local copies, waits for them, and re-layouts: 2.56 us -> 2.36 us
  transfers between devices with their start and end apart: 6 -> 4, of which waited for: 0 -> 1; matrix products, arithmetic and copies ran while one was open for 4% -> 4% of each run, Pallas kernels for 0% -> 0%
where the time goes in v8:
time: 50.9 us; the launch traced here: 49.9 us
  Pallas kernels  16.8 us (33%)
  blocking collectives  11.6 us (23%)
  starting transfers between devices  8.01 us (16%)
  local copies, waits for them, and re-layouts  6.53 us (13%)
  other arithmetic  3.09 us (6%)
  waiting for transfers between devices  3.08 us (6%)
  between operations  0.84 us (2%)
    all_to_all x1, blocking collectives, body(): lax.all_to_all(own_spec, 'tm', split_axis=3, concat_axis=2, tiled=True)  11.6 us
    pallas_call x1, Pallas kernels, whiten(): pl.pallas_call(dft_kernel, grid=(samples // (fine * coarse_step),), in_sp...  10.4 us
    pallas_call x1, Pallas kernels, cross_block(): pl.pallas_call(kernel, grid_spec=grid_spec, out_shape=jax.ShapeDtypeStruc...  6.39 us
    ppermute x2, starting transfers between devices, passed_along(): return lax.ppermute(array, axis, pairs)  4.34 us
    ppermute x1, starting transfers between devices, body(): lax.ppermute(paired, 'sta', [(i, i + 2 - 4 * (i % 2)) for i in range(peer...  3.49 us
    ppermute x1, waiting for transfers between devices, body(): lax.ppermute(paired, 'sta', [(i, i + 2 - 4 * (i % 2)) for i in range(peer...  3.08 us
    unnamed x14, local copies, waits for them, and re-layouts  2.36 us
    reshape x2, local copies, waits for them, and re-layouts, whiten(): return white.reshape(1, stations, windows, groups, width // groups)  1.4 us
  transfers between devices with their start and end apart: 4, of which 1 were waited for; matrix products, arithmetic and copies ran while one was open for 4% of the time, Pallas kernels for 0%

profile of v8, /device:TPU:0, one launch (start us, length us, event | category | flops | bytes accessed | tf_op | source)
XLA Modules:
  0.0 49.9 jit_solution(10256576257646636773)
XLA Ops:
  0.0 1.3 %negate_select_fusion.3 = (f32[64,256]{1,0:T(8,128)}, f32[64,256]{1,0:T(8,128)}, f32[64,256]{1,0:T(8,128)}, f32[64,256]{1,0:T(8,128)}) fusion(s32[256]{0:T(256)S(1)} %fusion.17, s32[64]{0:T(128)S(1)} %iota_multiply_fusion, pred[256]{0:T(512)(128)(4,1)S(1)} %fusion.20), kind=kLoop, calls=%fused_computation.19 | loop fusion | flops 524288 | bytes 263680 | tf_op jit(solution)/shard_map/jit(_where)/select_n | solution.py:38
  1.3 10.4 %shard_map.37 = bf16[640,256]{1,0:T(8,128)(2,1)} custom-call(f32[64,256]{1,0:T(8,128)} %get-tuple-element.8.p1_ref, f32[64,256]{1,0:T(8,128)} %get-tuple-element.7.q1_ref, f32[64,256]{1,0:T(8,128)} %get-tuple-element.10.c2_ref, f32[64,256]{1,0:T(8,128)} %get-tuple-element.9.s2_ref, f32[640,4096]{1,0:T(8,128)} %bitcast.20), custom_call_target="tpu_custom_call" | custom-call | tf_op jit(solution)/shard_map/pallas_call | solution.py:77
  11.7 1.3 %reshape.79 = bf16[1,40,16,4,64]{4,3,2,1,0:T(4,128)(2,1)S(1)} reshape(bf16[640,256]{1,0:T(8,128)(2,1)} %shard_map.37) | data formatting | bytes 655360 | tf_op jit(solution)/shard_map/reshape | solution.py:91
  13.0 0.1 copy.12
  13.1 0.5 reshape.86
  13.6 11.6 %all_to_all.15 = bf16[4,2,20480]{2,1,0:T(2,128)(2,1)S(1)} all-to-all(bf16[4,2,20480]{2,1,0:T(2,128)(2,1)S(1)} %reshape.86), channel_id=1, replica_groups=mesh['tm'=4,'sta'=8] {'tm'}, dimensions={0} | all-to-all | bytes 655360 | tf_op jit(solution)/shard_map/all_to_all | solution.py:145
  25.2 0.4 reshape.87
  25.6 0.1 bitcast_bitcast_fusion
  25.7 0.8 %copy.8 = bf16[1,40,4,16,1,64]{1,5,3,2,4,0:T(8,128)(2,1)S(1)} copy(bf16[1,40,4,16,1,64]{5,3,1,2,4,0:T(8,128)(2,1)S(1)} %bitcast_bitcast_fusion) | data formatting | bytes 655360 | tf_op jit(solution)/shard_map/all_to_all | solution.py:145
  26.5 0.0 copy-start.5
  26.5 1.3 %copy.9 = bf16[32,40,2,64]{3,2,1,0:T(2,128)(2,1)S(1)} copy(bf16[32,40,2,64]{1,0,2,3:T(8,128)(2,1)S(1)} %bitcast.21) | data formatting | bytes 655360 | tf_op jit(solution)/shard_map/transpose | solution.py:150
  27.8 0.3 reshape_reshape.3.refs_5_
  28.1 0.0 copy-start.2
  28.1 1.3 %collective-permute-start.2 = (bf16[16,80,128]{2,1,0:T(8,128)(2,1)S(1)}, bf16[16,80,128]{2,1,0:T(8,128)(2,1)S(1)}, u32[]{:S(2)}, u32[]{:S(2)}) collective-permute-start(bf16[16,80,128]{2,1,0:T(8,128)(2,1)S(1)} %reshape_reshape.3.refs_5_), channel_id=1, source_target_pairs={{1,0},{2,1},{3,2},{4,3},{5,4},{6,5},{7,6},{9,8},{10,9},{11,10},{12... | collective-permute-start | bytes 983048 | tf_op jit(solution)/shard_map/ppermute | solution.py:18
  29.4 3.1 %collective-permute-start.1 = (bf16[16,80,128]{2,1,0:T(8,128)(2,1)S(1)}, bf16[16,80,128]{2,1,0:T(8,128)(2,1)S(1)}, u32[]{:S(2)}, u32[]{:S(2)}) collective-permute-start(bf16[16,80,128]{2,1,0:T(8,128)(2,1)S(1)} %reshape_reshape.3.refs_5_), channel_id=1, source_target_pairs={{0,1},{1,2},{2,3},{3,4},{4,5},{5,6},{6,7},{8,9},{9,10},{10,11},{11... | collective-permute-start | bytes 983048 | tf_op jit(solution)/shard_map/ppermute | solution.py:18
  33.1 0.0 copy-done.5
  33.2 0.6 %compare_select_fusion.4.refs_0_ = s32[5]{0:T(128)} fusion(s32[1,5]{1,0:T(1,128)S(1)} %copy-done.5, s32[]{:T(128)S(6)} %sub.30, s32[]{:T(128)S(6)} %select_n.97, s32[]{:T(128)S(6)} %axis_index.12, s32[]{:T(128)} %bitcast.19), kind=kLoop, calls=%fused_computation.37 | loop fusion | flops 50 | bytes 56 | tf_op jit(solution)/shard_map/jit(_where)/select_n | solution.py:169
  33.7 0.3 reshape.81
  34.0 3.5 %collective-permute-start = (bf16[16,80,128]{2,1,0:T(8,128)(2,1)S(1)}, bf16[16,80,128]{2,1,0:T(8,128)(2,1)S(1)}, u32[]{:S(2)}, u32[]{:S(2)}) collective-permute-start(bf16[16,80,128]{2,1,0:T(8,128)(2,1)S(1)} %reshape_reshape.3.refs_5_), channel_id=1, source_target_pairs={{0,2},{2,4},{3,1},{4,6},{5,3},{7,5},{8,10},{10,12},{11,9},{12,14},... | collective-permute-start | bytes 983048 | tf_op jit(solution)/shard_map/ppermute | solution.py:158
  37.5 0.0 collective-permute-done.2.refs_6_
  37.5 0.0 copy-start
  37.5 0.0 collective-permute-done.1.refs_4_
  37.5 0.0 copy-start.1
  37.6 0.2 collective-permute-start.3
  37.8 0.2 slice_negate_fusion
  38.0 1.0 %maximum_maximum_fusion.refs_1_ = bf16[32,80,128]{2,1,0:T(8,128)(2,1)} fusion(bf16[32,40,64]{2,1,0:T(8,128)(2,1)S(1)} %get-tuple-element.6, bf16[32,40,64]{2,1,0:T(8,128)(2,1)S(1)} %get-tuple-element.5, bf16[32,40,128]{2,1,0:T(8,128)(2,1)S(1)} %reshape.81), kind=kLoop, calls=%fused_computation | loop fusion | flops 1966080 | bytes 1310720 | tf_op jit(solution)/shard_map/concatenate | solution.py:172
  39.0 0.0 copy-done.1
  39.0 3.1 %collective-permute-done.refs_2_ = bf16[16,80,128]{2,1,0:T(8,128)(2,1)S(1)} collective-permute-done((bf16[16,80,128]{2,1,0:T(8,128)(2,1)S(1)}, bf16[16,80,128]{2,1,0:T(8,128)(2,1)S(1)}, u32[]{:S(2)}, u32[]{:S(2)}) %collective-permute-start) | collective-permute-done | bytes 327712 | tf_op jit(solution)/shard_map/ppermute | solution.py:158
  42.1 0.0 collective-permute-done.3.refs_3_
  42.1 0.7 %copy-done.3 = bf16[16,80,128]{2,1,0:T(8,128)(2,1)} copy-done((bf16[16,80,128]{2,1,0:T(8,128)(2,1)}, bf16[16,80,128]{2,1,0:T(8,128)(2,1)S(1)}, u32[]{:S(2)}) %copy-start.3) | copy-done | bytes 327704
  42.8 0.7 %copy-done.4 = bf16[16,80,128]{2,1,0:T(8,128)(2,1)} copy-done((bf16[16,80,128]{2,1,0:T(8,128)(2,1)}, bf16[16,80,128]{2,1,0:T(8,128)(2,1)S(1)}, u32[]{:S(2)}) %copy-start.4) | copy-done | bytes 327704
  43.5 6.4 %shard_map.38 = f32[5,40,2560]{2,1,0:T(8,128)} custom-call(s32[5]{0:T(128)} %compare_select_fusion.4.refs_0_, bf16[32,80,128]{2,1,0:T(8,128)(2,1)} %maximum_maximum_fusion.refs_1_, bf16[16,80,128]{2,1,0:T(8,128)(2,1)} %copy-done.3, bf16[16,80,128]{2,1,0:T(8,128)(2,1)} %copy-done.4, bf16[16,80,128]{2,1,0:T(8,128)(2,1)} %copy-done.1, ...), custom_call_target="tpu_custom_call" | custom-call | tf_op jit(solution)/shard_map/pallas_call | solution.py:132
  (8 shorter events, 0.1 us)
Async XLA Ops:
  26.5 6.6 %copy-start.5 = (s32[1,5]{1,0:T(1,128)S(1)}, s32[1,5]{1,0:T(1,128)}, u32[]{:S(2)}) copy-start(s32[1,5]{1,0:T(1,128)} %param.4) | copy-start | bytes 64
  28.1 9.8 %copy-start.2 = (bf16[16,80,128]{2,1,0:T(8,128)(2,1)}, bf16[16,80,128]{2,1,0:T(8,128)(2,1)S(1)}, u32[]{:S(2)}) copy-start(bf16[16,80,128]{2,1,0:T(8,128)(2,1)S(1)} %reshape_reshape.3.refs_5_) | copy-start | bytes 983044
  28.1 9.4 %collective-permute-start.2 = (bf16[16,80,128]{2,1,0:T(8,128)(2,1)S(1)}, bf16[16,80,128]{2,1,0:T(8,128)(2,1)S(1)}, u32[]{:S(2)}, u32[]{:S(2)}) collective-permute-start(bf16[16,80,128]{2,1,0:T(8,128)(2,1)S(1)} %reshape_reshape.3.refs_5_), channel_id=1, source_target_pairs={{1,0},{2,1},{3,2},{4,3},{5,4},{6,5},{7,6},{9,8},{10,9},{11,10},{12... | collective-permute-start | bytes 983048 | tf_op jit(solution)/shard_map/ppermute | solution.py:18
  29.4 8.1 %collective-permute-start.1 = (bf16[16,80,128]{2,1,0:T(8,128)(2,1)S(1)}, bf16[16,80,128]{2,1,0:T(8,128)(2,1)S(1)}, u32[]{:S(2)}, u32[]{:S(2)}) collective-permute-start(bf16[16,80,128]{2,1,0:T(8,128)(2,1)S(1)} %reshape_reshape.3.refs_5_), channel_id=1, source_target_pairs={{0,1},{1,2},{2,3},{3,4},{4,5},{5,6},{6,7},{8,9},{9,10},{10,11},{11... | collective-permute-start | bytes 983048 | tf_op jit(solution)/shard_map/ppermute | solution.py:18
  34.0 8.1 %collective-permute-start = (bf16[16,80,128]{2,1,0:T(8,128)(2,1)S(1)}, bf16[16,80,128]{2,1,0:T(8,128)(2,1)S(1)}, u32[]{:S(2)}, u32[]{:S(2)}) collective-permute-start(bf16[16,80,128]{2,1,0:T(8,128)(2,1)S(1)} %reshape_reshape.3.refs_5_), channel_id=1, source_target_pairs={{0,2},{2,4},{3,1},{4,6},{5,3},{7,5},{8,10},{10,12},{11,9},{12,14},... | collective-permute-start | bytes 983048 | tf_op jit(solution)/shard_map/ppermute | solution.py:158
  37.5 1.5 %copy-start = (bf16[16,80,128]{2,1,0:T(8,128)(2,1)}, bf16[16,80,128]{2,1,0:T(8,128)(2,1)S(1)}, u32[]{:S(2)}) copy-start(bf16[16,80,128]{2,1,0:T(8,128)(2,1)S(1)} %collective-permute-done.2.refs_6_) | copy-start | bytes 983044
  37.5 1.4 %copy-start.1 = (bf16[16,80,128]{2,1,0:T(8,128)(2,1)}, bf16[16,80,128]{2,1,0:T(8,128)(2,1)S(1)}, u32[]{:S(2)}) copy-start(bf16[16,80,128]{2,1,0:T(8,128)(2,1)S(1)} %collective-permute-done.1.refs_4_) | copy-start | bytes 983044
  37.6 4.5 %collective-permute-start.3 = (bf16[16,80,128]{2,1,0:T(8,128)(2,1)S(1)}, bf16[16,80,128]{2,1,0:T(8,128)(2,1)S(1)}, u32[]{:S(2)}, u32[]{:S(2)}) collective-permute-start(bf16[16,80,128]{2,1,0:T(8,128)(2,1)S(1)} %broadcast_select_fusion), channel_id=1, source_target_pairs={{0,1},{1,0},{2,3},{3,2},{4,5},{5,4},{6,7},{7,6},{8,9},{9,8},{10,11... | collective-permute-start | bytes 983048 | tf_op jit(solution)/shard_map/ppermute | solution.py:162
  42.1 0.7 %copy-start.3 = (bf16[16,80,128]{2,1,0:T(8,128)(2,1)}, bf16[16,80,128]{2,1,0:T(8,128)(2,1)S(1)}, u32[]{:S(2)}) copy-start(bf16[16,80,128]{2,1,0:T(8,128)(2,1)S(1)} %collective-permute-done.refs_2_) | copy-start | bytes 983044
  42.8 0.7 %copy-start.4 = (bf16[16,80,128]{2,1,0:T(8,128)(2,1)}, bf16[16,80,128]{2,1,0:T(8,128)(2,1)S(1)}, u32[]{:S(2)}) copy-start(bf16[16,80,128]{2,1,0:T(8,128)(2,1)S(1)} %collective-permute-done.3.refs_3_) | copy-start | bytes 983044

commit v9 on v8

--- a/solution.py
+++ b/solution.py
@@ -64,7 +64,8 @@
     def _():
         spectra = acc_ref[...]
         mean_power = jnp.mean(spectra * spectra, axis=1, keepdims=True)
-        o_ref[...] = (spectra / jnp.sqrt(mean_power + 1e-06)).astype(o_ref.dtype)
+        white = spectra / jnp.sqrt(mean_power + 1e-06)
+        o_ref[...] = white.T.astype(o_ref.dtype)
 
 
 def whiten(records, groups):
@@ -84,11 +85,11 @@
             pl.BlockSpec((fine, width), lambda k: (0, 0)),
             pl.BlockSpec((rows, fine * coarse_step), lambda k: (0, k)),
         ],
-        out_specs=pl.BlockSpec((rows, width), lambda k: (0, 0)),
-        out_shape=jax.ShapeDtypeStruct((rows, width), jnp.bfloat16),
+        out_specs=pl.BlockSpec((width, rows), lambda k: (0, 0)),
+        out_shape=jax.ShapeDtypeStruct((width, rows), jnp.bfloat16),
         scratch_shapes=[pltpu.VMEM((rows, width), jnp.float32)],
     )(p1, q1, c2, s2, x)
-    return white.reshape(1, stations, windows, groups, width // groups)
+    return white.reshape(groups, width // groups, rows)
 
 
 def cross_kernel(scale, sel_ref, lx_ref, *refs):
@@ -142,12 +143,15 @@
     partner_row = partners[0]
     slots = partner_row.shape[0]
     live_slots = jnp.arange(slots, dtype=jnp.int32) < counts[0]
-    regrouped = lax.all_to_all(own_spec, "tm", split_axis=3, concat_axis=2, tiled=True)
-    stations, windows, width = regrouped.shape[1], regrouped.shape[2], regrouped.shape[4]
-    nb = width // 2
+    regrouped = lax.all_to_all(own_spec, "tm", split_axis=0, concat_axis=0, tiled=True)
+    groups = regrouped.shape[0]
+    nb = regrouped.shape[1] // 2
+    stations = records.shape[0]
+    local_windows = records.shape[1]
+    windows = groups * local_windows
     spec = (
-        regrouped.reshape(stations, windows, 2, nb)
-        .transpose(3, 0, 2, 1)
+        regrouped.reshape(groups, 2, nb, stations, local_windows)
+        .transpose(2, 3, 1, 0, 4)
         .reshape(nb, stations, 2 * windows)
     )
     paired = spec.reshape(nb // 2, 2 * stations, 2 * windows)

time: 50.9 us -> 52 us (1.022)
  local copies, waits for them, and re-layouts: 6.53 us -> 7.77 us
    transpose x1 -> x2, local copies, waits for them, and re-layouts: 1.31 us -> 4.17 us  [body(): spec = regrouped.reshape(groups, 2, nb, stations, local_windows).transpos...]
    unnamed x14 -> x12, local copies, waits for them, and re-layouts: 2.36 us -> 1.46 us
    reshape x3 -> x2, local copies, waits for them, and re-layouts: 1.68 us -> 0.85 us  [the longest x1 0.49 us: body(): regrouped.reshape(groups, 2, nb, stations, local_windows)]
    another operation x1 -> x2, local copies, waits for them, and re-layouts: 0.28 us -> 0.96 us  [body(): paired = spec.reshape(nb // 2, 2 * stations, 2 * windows)]
    all_to_all x2 -> x1, local copies, waits for them, and re-layouts: 0.9 us -> 0.33 us  [body(): lax.all_to_all(own_spec, 'tm', split_axis=0, concat_axis=0, tiled=True)]
  transfers between devices with their start and end apart: 4 -> 4, of which waited for: 1 -> 1; matrix products, arithmetic and copies ran while one was open for 4% -> 9% of each run, Pallas kernels for 0% -> 0%
where the time goes in v9:
time: 52 us; the launch traced here: 51.1 us
  Pallas kernels  16.9 us (32%)
  blocking collectives  11.8 us (23%)
  starting transfers between devices  7.9 us (15%)
  local copies, waits for them, and re-layouts  7.77 us (15%)
  other arithmetic  3.09 us (6%)
  waiting for transfers between devices  2.81 us (5%)
  between operations  0.82 us (2%)
    all_to_all x1, blocking collectives, body(): lax.all_to_all(own_spec, 'tm', split_axis=0, concat_axis=0, tiled=True)  11.8 us
    pallas_call x1, Pallas kernels, whiten(): pl.pallas_call(dft_kernel, grid=(samples // (fine * coarse_step),), in_sp...  10.5 us
    pallas_call x1, Pallas kernels, cross_block(): pl.pallas_call(kernel, grid_spec=grid_spec, out_shape=jax.ShapeDtypeStruc...  6.39 us
    ppermute x2, starting transfers between devices, passed_along(): return lax.ppermute(array, axis, pairs)  4.34 us
    transpose x2, local copies, waits for them, and re-layouts, body(): spec = regrouped.reshape(groups, 2, nb, stations, local_windows).transpos...  4.17 us
    ppermute x1, starting transfers between devices, body(): lax.ppermute(paired, 'sta', [(i, i + 2 - 4 * (i % 2)) for i in range(peer...  3.49 us
    ppermute x1, waiting for transfers between devices, body(): lax.ppermute(paired, 'sta', [(i, i + 2 - 4 * (i % 2)) for i in range(peer...  2.81 us
    unnamed x12, local copies, waits for them, and re-layouts  1.46 us
  transfers between devices with their start and end apart: 4, of which 1 were waited for; matrix products, arithmetic and copies ran while one was open for 9% of the time, Pallas kernels for 0%

profile of v9, /device:TPU:0, one launch (start us, length us, event | category | flops | bytes accessed | tf_op | source)
XLA Modules:
  0.0 51.1 jit_solution(12616580349858379173)
XLA Ops:
  0.0 1.3 %negate_select_fusion.3 = (f32[64,256]{1,0:T(8,128)}, f32[64,256]{1,0:T(8,128)}, f32[64,256]{1,0:T(8,128)}, f32[64,256]{1,0:T(8,128)}) fusion(s32[256]{0:T(256)S(1)} %fusion.17, s32[64]{0:T(128)S(1)} %iota_multiply_fusion, pred[256]{0:T(512)(128)(4,1)S(1)} %fusion.20), kind=kLoop, calls=%fused_computation.19 | loop fusion | flops 524288 | bytes 263680 | tf_op jit(solution)/shard_map/jit(_where)/select_n | solution.py:38
  1.3 10.5 %shard_map.37 = bf16[256,640]{1,0:T(8,128)(2,1)} custom-call(f32[64,256]{1,0:T(8,128)} %get-tuple-element.8.p1_ref, f32[64,256]{1,0:T(8,128)} %get-tuple-element.7.q1_ref, f32[64,256]{1,0:T(8,128)} %get-tuple-element.10.c2_ref, f32[64,256]{1,0:T(8,128)} %get-tuple-element.9.s2_ref, f32[640,4096]{1,0:T(8,128)} %bitcast.19), custom_call_target="tpu_custom_call" | custom-call | tf_op jit(solution)/shard_map/pallas_call | solution.py:78
  11.8 11.8 %all_to_all.5 = bf16[4,64,640]{2,1,0:T(8,128)(2,1)S(1)} all-to-all(bf16[4,64,640]{2,1,0:T(8,128)(2,1)} %bitcast.21), channel_id=1, replica_groups=mesh['tm'=4,'sta'=8] {'tm'}, dimensions={0} | all-to-all | bytes 655360 | tf_op jit(solution)/shard_map/all_to_all | solution.py:146
  23.6 0.3 copy.14
  23.9 0.5 reshape.79
  24.4 1.6 %copy.19 = bf16[32,40,2,4,16]{1,0,4,3,2:T(8,128)(2,1)S(1)} copy(bf16[32,40,2,4,16]{0,2,4,1,3:T(2,128)(2,1)S(1)} %bitcast.17) | data formatting | bytes 655360 | tf_op jit(solution)/shard_map/transpose | solution.py:154
  26.0 0.0 copy-start.5
  26.0 0.5 reshape_reshape.3
  26.5 0.5 copy.20.refs_5_
  27.0 0.0 copy-start.2
  27.0 1.3 %collective-permute-start.2 = (bf16[16,80,128]{2,1,0:T(8,128)(2,1)S(1)}, bf16[16,80,128]{2,1,0:T(8,128)(2,1)S(1)}, u32[]{:S(2)}, u32[]{:S(2)}) collective-permute-start(bf16[16,80,128]{2,1,0:T(8,128)(2,1)S(1)} %copy.20.refs_5_), channel_id=1, source_target_pairs={{1,0},{2,1},{3,2},{4,3},{5,4},{6,5},{7,6},{9,8},{10,9},{11,10},{12... | collective-permute-start | bytes 983048 | tf_op jit(solution)/shard_map/ppermute | solution.py:18
  28.3 3.1 %collective-permute-start.1 = (bf16[16,80,128]{2,1,0:T(8,128)(2,1)S(1)}, bf16[16,80,128]{2,1,0:T(8,128)(2,1)S(1)}, u32[]{:S(2)}, u32[]{:S(2)}) collective-permute-start(bf16[16,80,128]{2,1,0:T(8,128)(2,1)S(1)} %copy.20.refs_5_), channel_id=1, source_target_pairs={{0,1},{1,2},{2,3},{3,4},{4,5},{5,6},{6,7},{8,9},{9,10},{10,11},{11... | collective-permute-start | bytes 983048 | tf_op jit(solution)/shard_map/ppermute | solution.py:18
  32.0 0.0 copy-done.5
  32.0 0.6 %compare_select_fusion.4.refs_0_ = s32[5]{0:T(128)} fusion(s32[1,5]{1,0:T(1,128)S(1)} %copy-done.5, s32[]{:T(128)S(6)} %sub.30, s32[]{:T(128)S(6)} %select_n.97, s32[]{:T(128)S(6)} %axis_index.12, s32[]{:T(128)} %bitcast.16), kind=kLoop, calls=%fused_computation.37 | loop fusion | flops 50 | bytes 56 | tf_op jit(solution)/shard_map/jit(_where)/select_n | solution.py:173
  32.6 2.5 %copy.15 = bf16[32,40,2,4,16]{1,4,3,2,0:T(8,128)(2,1)S(1)} copy(bf16[32,40,2,4,16]{0,2,4,1,3:T(2,128)(2,1)S(1)} %bitcast.18) | data formatting | bytes 655360 | tf_op jit(solution)/shard_map/transpose | solution.py:154
  35.2 3.5 %collective-permute-start = (bf16[16,80,128]{2,1,0:T(8,128)(2,1)S(1)}, bf16[16,80,128]{2,1,0:T(8,128)(2,1)S(1)}, u32[]{:S(2)}, u32[]{:S(2)}) collective-permute-start(bf16[16,80,128]{2,1,0:T(8,128)(2,1)S(1)} %copy.20.refs_5_), channel_id=1, source_target_pairs={{0,2},{2,4},{3,1},{4,6},{5,3},{7,5},{8,10},{10,12},{11,9},{12,14},... | collective-permute-start | bytes 983048 | tf_op jit(solution)/shard_map/ppermute | solution.py:162
  38.7 0.4 copy.18
  39.0 0.0 copy-done.2
  39.0 0.0 collective-permute-done.2.refs_6_
  39.1 0.0 copy-start
  39.1 0.0 collective-permute-done.1.refs_4_
  39.1 0.0 copy-start.1
  39.1 0.1 collective-permute-start.3
  39.2 0.2 slice_negate_fusion
  39.4 1.0 %maximum_maximum_fusion.refs_1_ = bf16[32,80,128]{2,1,0:T(8,128)(2,1)} fusion(bf16[32,40,64]{2,1,0:T(8,128)(2,1)S(1)} %get-tuple-element.6, bf16[32,40,64]{2,1,0:T(8,128)(2,1)S(1)} %get-tuple-element.5, bf16[32,40,128]{2,1,0:T(8,128)(2,1)S(1)} %copy.18), kind=kLoop, calls=%fused_computation | loop fusion | flops 1966080 | bytes 1310720 | tf_op jit(solution)/shard_map/concatenate | solution.py:176
  40.4 0.0 copy-done
  40.4 0.0 copy-done.1
  40.4 2.8 %collective-permute-done.refs_2_ = bf16[16,80,128]{2,1,0:T(8,128)(2,1)S(1)} collective-permute-done((bf16[16,80,128]{2,1,0:T(8,128)(2,1)S(1)}, bf16[16,80,128]{2,1,0:T(8,128)(2,1)S(1)}, u32[]{:S(2)}, u32[]{:S(2)}) %collective-permute-start) | collective-permute-done | bytes 327712 | tf_op jit(solution)/shard_map/ppermute | solution.py:162
  43.2 0.0 collective-permute-done.3.refs_3_
  43.2 0.7 %copy-done.3 = bf16[16,80,128]{2,1,0:T(8,128)(2,1)} copy-done((bf16[16,80,128]{2,1,0:T(8,128)(2,1)}, bf16[16,80,128]{2,1,0:T(8,128)(2,1)S(1)}, u32[]{:S(2)}) %copy-start.3) | copy-done | bytes 327704
  43.9 0.7 %copy-done.4 = bf16[16,80,128]{2,1,0:T(8,128)(2,1)} copy-done((bf16[16,80,128]{2,1,0:T(8,128)(2,1)}, bf16[16,80,128]{2,1,0:T(8,128)(2,1)S(1)}, u32[]{:S(2)}) %copy-start.4) | copy-done | bytes 327704
  44.7 6.4 %shard_map.38 = f32[5,40,2560]{2,1,0:T(8,128)} custom-call(s32[5]{0:T(128)} %compare_select_fusion.4.refs_0_, bf16[32,80,128]{2,1,0:T(8,128)(2,1)} %maximum_maximum_fusion.refs_1_, bf16[16,80,128]{2,1,0:T(8,128)(2,1)} %copy-done.3, bf16[16,80,128]{2,1,0:T(8,128)(2,1)} %copy-done.4, bf16[16,80,128]{2,1,0:T(8,128)(2,1)} %copy-done.1, ...), custom_call_target="tpu_custom_call" | custom-call | tf_op jit(solution)/shard_map/pallas_call | solution.py:133
  (6 shorter events, 0.1 us)
Async XLA Ops:
  26.0 6.0 %copy-start.5 = (s32[1,5]{1,0:T(1,128)S(1)}, s32[1,5]{1,0:T(1,128)}, u32[]{:S(2)}) copy-start(s32[1,5]{1,0:T(1,128)} %param.4) | copy-start | bytes 64
  27.0 12.0 %copy-start.2 = (bf16[16,80,128]{2,1,0:T(8,128)(2,1)}, bf16[16,80,128]{2,1,0:T(8,128)(2,1)S(1)}, u32[]{:S(2)}) copy-start(bf16[16,80,128]{2,1,0:T(8,128)(2,1)S(1)} %copy.20.refs_5_) | copy-start | bytes 983044
  27.0 12.0 %collective-permute-start.2 = (bf16[16,80,128]{2,1,0:T(8,128)(2,1)S(1)}, bf16[16,80,128]{2,1,0:T(8,128)(2,1)S(1)}, u32[]{:S(2)}, u32[]{:S(2)}) collective-permute-start(bf16[16,80,128]{2,1,0:T(8,128)(2,1)S(1)} %copy.20.refs_5_), channel_id=1, source_target_pairs={{1,0},{2,1},{3,2},{4,3},{5,4},{6,5},{7,6},{9,8},{10,9},{11,10},{12... | collective-permute-start | bytes 983048 | tf_op jit(solution)/shard_map/ppermute | solution.py:18
  28.3 10.8 %collective-permute-start.1 = (bf16[16,80,128]{2,1,0:T(8,128)(2,1)S(1)}, bf16[16,80,128]{2,1,0:T(8,128)(2,1)S(1)}, u32[]{:S(2)}, u32[]{:S(2)}) collective-permute-start(bf16[16,80,128]{2,1,0:T(8,128)(2,1)S(1)} %copy.20.refs_5_), channel_id=1, source_target_pairs={{0,1},{1,2},{2,3},{3,4},{4,5},{5,6},{6,7},{8,9},{9,10},{10,11},{11... | collective-permute-start | bytes 983048 | tf_op jit(solution)/shard_map/ppermute | solution.py:18
  35.2 8.1 %collective-permute-start = (bf16[16,80,128]{2,1,0:T(8,128)(2,1)S(1)}, bf16[16,80,128]{2,1,0:T(8,128)(2,1)S(1)}, u32[]{:S(2)}, u32[]{:S(2)}) collective-permute-start(bf16[16,80,128]{2,1,0:T(8,128)(2,1)S(1)} %copy.20.refs_5_), channel_id=1, source_target_pairs={{0,2},{2,4},{3,1},{4,6},{5,3},{7,5},{8,10},{10,12},{11,9},{12,14},... | collective-permute-start | bytes 983048 | tf_op jit(solution)/shard_map/ppermute | solution.py:162
  39.1 1.4 %copy-start = (bf16[16,80,128]{2,1,0:T(8,128)(2,1)}, bf16[16,80,128]{2,1,0:T(8,128)(2,1)S(1)}, u32[]{:S(2)}) copy-start(bf16[16,80,128]{2,1,0:T(8,128)(2,1)S(1)} %collective-permute-done.2.refs_6_) | copy-start | bytes 983044
  39.1 1.3 %copy-start.1 = (bf16[16,80,128]{2,1,0:T(8,128)(2,1)}, bf16[16,80,128]{2,1,0:T(8,128)(2,1)S(1)}, u32[]{:S(2)}) copy-start(bf16[16,80,128]{2,1,0:T(8,128)(2,1)S(1)} %collective-permute-done.1.refs_4_) | copy-start | bytes 983044
  39.1 4.1 %collective-permute-start.3 = (bf16[16,80,128]{2,1,0:T(8,128)(2,1)S(1)}, bf16[16,80,128]{2,1,0:T(8,128)(2,1)S(1)}, u32[]{:S(2)}, u32[]{:S(2)}) collective-permute-start(bf16[16,80,128]{2,1,0:T(8,128)(2,1)S(1)} %broadcast_select_fusion), channel_id=1, source_target_pairs={{0,1},{1,0},{2,3},{3,2},{4,5},{5,4},{6,7},{7,6},{8,9},{9,8},{10,11... | collective-permute-start | bytes 983048 | tf_op jit(solution)/shard_map/ppermute | solution.py:166
  43.2 0.7 %copy-start.3 = (bf16[16,80,128]{2,1,0:T(8,128)(2,1)}, bf16[16,80,128]{2,1,0:T(8,128)(2,1)S(1)}, u32[]{:S(2)}) copy-start(bf16[16,80,128]{2,1,0:T(8,128)(2,1)S(1)} %collective-permute-done.refs_2_) | copy-start | bytes 983044
  43.9 0.7 %copy-start.4 = (bf16[16,80,128]{2,1,0:T(8,128)(2,1)}, bf16[16,80,128]{2,1,0:T(8,128)(2,1)S(1)}, u32[]{:S(2)}) copy-start(bf16[16,80,128]{2,1,0:T(8,128)(2,1)S(1)} %collective-permute-done.3.refs_3_) | copy-start | bytes 983044

commit v10 on v8

--- a/solution.py
+++ b/solution.py
@@ -71,7 +71,7 @@
     stations, windows, samples = records.shape
     p1, q1, c2, s2 = dft_factors(samples, BINS, groups)
     fine, width = c2.shape
-    coarse_step = 8
+    coarse_step = 32
     rows = stations * windows
     x = records.reshape(rows, samples)
     white = pl.pallas_call(

time: 50.9 us -> 48.4 us (0.951)
  Pallas kernels: 16.8 us -> 14.4 us
    pallas_call x1, Pallas kernels: 10.4 us -> 8.06 us  [whiten(): pl.pallas_call(dft_kernel, grid=(samples // (fine * coarse_step),), in_sp...]
where the time goes in v10:
time: 48.4 us; the launch traced here: 47.6 us
  Pallas kernels  14.4 us (30%)
  blocking collectives  11.6 us (24%)
  starting transfers between devices  8 us (17%)
  local copies, waits for them, and re-layouts  6.53 us (13%)
  other arithmetic  3.09 us (6%)
  waiting for transfers between devices  3.08 us (6%)
  between operations  0.84 us (2%)
    all_to_all x1, blocking collectives, body(): lax.all_to_all(own_spec, 'tm', split_axis=3, concat_axis=2, tiled=True)  11.6 us
    pallas_call x1, Pallas kernels, whiten(): pl.pallas_call(dft_kernel, grid=(samples // (fine * coarse_step),), in_sp...  8.06 us
    pallas_call x1, Pallas kernels, cross_block(): pl.pallas_call(kernel, grid_spec=grid_spec, out_shape=jax.ShapeDtypeStruc...  6.39 us
    ppermute x2, starting transfers between devices, passed_along(): return lax.ppermute(array, axis, pairs)  4.34 us
    ppermute x1, starting transfers between devices, body(): lax.ppermute(paired, 'sta', [(i, i + 2 - 4 * (i % 2)) for i in range(peer...  3.48 us
    ppermute x1, waiting for transfers between devices, body(): lax.ppermute(paired, 'sta', [(i, i + 2 - 4 * (i % 2)) for i in range(peer...  3.08 us
    unnamed x14, local copies, waits for them, and re-layouts  2.36 us
    reshape x2, local copies, waits for them, and re-layouts, whiten(): return white.reshape(1, stations, windows, groups, width // groups)  1.4 us
  transfers between devices with their start and end apart: 4, of which 1 were waited for; matrix products, arithmetic and copies ran while one was open for 4% of the time, Pallas kernels for 0%

profile of v10, /device:TPU:0, one launch (start us, length us, event | category | flops | bytes accessed | tf_op | source)
XLA Modules:
  0.0 47.6 jit_solution(11674655858335422703)
XLA Ops:
  0.0 1.3 %negate_select_fusion.3 = (f32[64,256]{1,0:T(8,128)}, f32[64,256]{1,0:T(8,128)}, f32[64,256]{1,0:T(8,128)}, f32[64,256]{1,0:T(8,128)}) fusion(s32[256]{0:T(256)S(1)} %fusion.17, s32[64]{0:T(128)S(1)} %iota_multiply_fusion, pred[256]{0:T(512)(128)(4,1)S(1)} %fusion.20), kind=kLoop, calls=%fused_computation.19 | loop fusion | flops 524288 | bytes 263680 | tf_op jit(solution)/shard_map/jit(_where)/select_n | solution.py:38
  1.3 8.1 %shard_map.37 = bf16[640,256]{1,0:T(8,128)(2,1)} custom-call(f32[64,256]{1,0:T(8,128)} %get-tuple-element.8.p1_ref, f32[64,256]{1,0:T(8,128)} %get-tuple-element.7.q1_ref, f32[64,256]{1,0:T(8,128)} %get-tuple-element.10.c2_ref, f32[64,256]{1,0:T(8,128)} %get-tuple-element.9.s2_ref, f32[640,4096]{1,0:T(8,128)} %bitcast.20), custom_call_target="tpu_custom_call" | custom-call | tf_op jit(solution)/shard_map/pallas_call | solution.py:77
  9.4 1.3 %reshape.79 = bf16[1,40,16,4,64]{4,3,2,1,0:T(4,128)(2,1)S(1)} reshape(bf16[640,256]{1,0:T(8,128)(2,1)} %shard_map.37) | data formatting | bytes 655360 | tf_op jit(solution)/shard_map/reshape | solution.py:91
  10.7 0.1 copy.12
  10.8 0.5 %reshape.86 = bf16[4,2,20480]{2,1,0:T(2,128)(2,1)S(1)} reshape(bf16[4,1,40,16,64]{4,3,2,1,0:T(8,128)(2,1)S(1)} %bitcast.22) | data formatting | bytes 655360
  11.3 11.6 %all_to_all.15 = bf16[4,2,20480]{2,1,0:T(2,128)(2,1)S(1)} all-to-all(bf16[4,2,20480]{2,1,0:T(2,128)(2,1)S(1)} %reshape.86), channel_id=1, replica_groups=mesh['tm'=4,'sta'=8] {'tm'}, dimensions={0} | all-to-all | bytes 655360 | tf_op jit(solution)/shard_map/all_to_all | solution.py:145
  22.8 0.4 reshape.87
  23.2 0.1 bitcast_bitcast_fusion
  23.4 0.8 %copy.8 = bf16[1,40,4,16,1,64]{1,5,3,2,4,0:T(8,128)(2,1)S(1)} copy(bf16[1,40,4,16,1,64]{5,3,1,2,4,0:T(8,128)(2,1)S(1)} %bitcast_bitcast_fusion) | data formatting | bytes 655360 | tf_op jit(solution)/shard_map/all_to_all | solution.py:145
  24.2 0.0 copy-start.5
  24.2 1.3 %copy.9 = bf16[32,40,2,64]{3,2,1,0:T(2,128)(2,1)S(1)} copy(bf16[32,40,2,64]{1,0,2,3:T(8,128)(2,1)S(1)} %bitcast.21) | data formatting | bytes 655360 | tf_op jit(solution)/shard_map/transpose | solution.py:150
  25.5 0.3 reshape_reshape.3.refs_5_
  25.8 0.0 copy-start.2
  25.8 1.3 %collective-permute-start.2 = (bf16[16,80,128]{2,1,0:T(8,128)(2,1)S(1)}, bf16[16,80,128]{2,1,0:T(8,128)(2,1)S(1)}, u32[]{:S(2)}, u32[]{:S(2)}) collective-permute-start(bf16[16,80,128]{2,1,0:T(8,128)(2,1)S(1)} %reshape_reshape.3.refs_5_), channel_id=1, source_target_pairs={{1,0},{2,1},{3,2},{4,3},{5,4},{6,5},{7,6},{9,8},{10,9},{11,10},{12... | collective-permute-start | bytes 983048 | tf_op jit(solution)/shard_map/ppermute | solution.py:18
  27.1 3.1 %collective-permute-start.1 = (bf16[16,80,128]{2,1,0:T(8,128)(2,1)S(1)}, bf16[16,80,128]{2,1,0:T(8,128)(2,1)S(1)}, u32[]{:S(2)}, u32[]{:S(2)}) collective-permute-start(bf16[16,80,128]{2,1,0:T(8,128)(2,1)S(1)} %reshape_reshape.3.refs_5_), channel_id=1, source_target_pairs={{0,1},{1,2},{2,3},{3,4},{4,5},{5,6},{6,7},{8,9},{9,10},{10,11},{11... | collective-permute-start | bytes 983048 | tf_op jit(solution)/shard_map/ppermute | solution.py:18
  30.8 0.0 copy-done.5
  30.8 0.6 %compare_select_fusion.4.refs_0_ = s32[5]{0:T(128)} fusion(s32[1,5]{1,0:T(1,128)S(1)} %copy-done.5, s32[]{:T(128)S(6)} %sub.30, s32[]{:T(128)S(6)} %select_n.97, s32[]{:T(128)S(6)} %axis_index.12, s32[]{:T(128)} %bitcast.19), kind=kLoop, calls=%fused_computation.37 | loop fusion | flops 50 | bytes 56 | tf_op jit(solution)/shard_map/jit(_where)/select_n | solution.py:169
  31.4 0.3 reshape.81
  31.7 3.5 %collective-permute-start = (bf16[16,80,128]{2,1,0:T(8,128)(2,1)S(1)}, bf16[16,80,128]{2,1,0:T(8,128)(2,1)S(1)}, u32[]{:S(2)}, u32[]{:S(2)}) collective-permute-start(bf16[16,80,128]{2,1,0:T(8,128)(2,1)S(1)} %reshape_reshape.3.refs_5_), channel_id=1, source_target_pairs={{0,2},{2,4},{3,1},{4,6},{5,3},{7,5},{8,10},{10,12},{11,9},{12,14},... | collective-permute-start | bytes 983048 | tf_op jit(solution)/shard_map/ppermute | solution.py:158
  35.2 0.0 collective-permute-done.2.refs_6_
  35.2 0.0 copy-start
  35.2 0.0 collective-permute-done.1.refs_4_
  35.2 0.0 copy-start.1
  35.2 0.2 collective-permute-start.3
  35.4 0.2 slice_negate_fusion
  35.6 0.0 copy-done.2
  35.6 1.0 %maximum_maximum_fusion.refs_1_ = bf16[32,80,128]{2,1,0:T(8,128)(2,1)} fusion(bf16[32,40,64]{2,1,0:T(8,128)(2,1)S(1)} %get-tuple-element.6, bf16[32,40,64]{2,1,0:T(8,128)(2,1)S(1)} %get-tuple-element.5, bf16[32,40,128]{2,1,0:T(8,128)(2,1)S(1)} %reshape.81), kind=kLoop, calls=%fused_computation | loop fusion | flops 1966080 | bytes 1310720 | tf_op jit(solution)/shard_map/concatenate | solution.py:172
  36.6 3.1 %collective-permute-done.refs_2_ = bf16[16,80,128]{2,1,0:T(8,128)(2,1)S(1)} collective-permute-done((bf16[16,80,128]{2,1,0:T(8,128)(2,1)S(1)}, bf16[16,80,128]{2,1,0:T(8,128)(2,1)S(1)}, u32[]{:S(2)}, u32[]{:S(2)}) %collective-permute-start) | collective-permute-done | bytes 327712 | tf_op jit(solution)/shard_map/ppermute | solution.py:158
  39.7 0.0 collective-permute-done.3.refs_3_
  39.7 0.7 %copy-done.3 = bf16[16,80,128]{2,1,0:T(8,128)(2,1)} copy-done((bf16[16,80,128]{2,1,0:T(8,128)(2,1)}, bf16[16,80,128]{2,1,0:T(8,128)(2,1)S(1)}, u32[]{:S(2)}) %copy-start.3) | copy-done | bytes 327704
  40.4 0.7 %copy-done.4 = bf16[16,80,128]{2,1,0:T(8,128)(2,1)} copy-done((bf16[16,80,128]{2,1,0:T(8,128)(2,1)}, bf16[16,80,128]{2,1,0:T(8,128)(2,1)S(1)}, u32[]{:S(2)}) %copy-start.4) | copy-done | bytes 327704
  41.2 6.4 %shard_map.38 = f32[5,40,2560]{2,1,0:T(8,128)} custom-call(s32[5]{0:T(128)} %compare_select_fusion.4.refs_0_, bf16[32,80,128]{2,1,0:T(8,128)(2,1)} %maximum_maximum_fusion.refs_1_, bf16[16,80,128]{2,1,0:T(8,128)(2,1)} %copy-done.3, bf16[16,80,128]{2,1,0:T(8,128)(2,1)} %copy-done.4, bf16[16,80,128]{2,1,0:T(8,128)(2,1)} %copy-done.1, ...), custom_call_target="tpu_custom_call" | custom-call | tf_op jit(solution)/shard_map/pallas_call | solution.py:132
  (8 shorter events, 0.1 us)
Async XLA Ops:
  24.2 6.6 %copy-start.5 = (s32[1,5]{1,0:T(1,128)S(1)}, s32[1,5]{1,0:T(1,128)}, u32[]{:S(2)}) copy-start(s32[1,5]{1,0:T(1,128)} %param.4) | copy-start | bytes 64
  25.8 9.8 %copy-start.2 = (bf16[16,80,128]{2,1,0:T(8,128)(2,1)}, bf16[16,80,128]{2,1,0:T(8,128)(2,1)S(1)}, u32[]{:S(2)}) copy-start(bf16[16,80,128]{2,1,0:T(8,128)(2,1)S(1)} %reshape_reshape.3.refs_5_) | copy-start | bytes 983044
  25.8 9.4 %collective-permute-start.2 = (bf16[16,80,128]{2,1,0:T(8,128)(2,1)S(1)}, bf16[16,80,128]{2,1,0:T(8,128)(2,1)S(1)}, u32[]{:S(2)}, u32[]{:S(2)}) collective-permute-start(bf16[16,80,128]{2,1,0:T(8,128)(2,1)S(1)} %reshape_reshape.3.refs_5_), channel_id=1, source_target_pairs={{1,0},{2,1},{3,2},{4,3},{5,4},{6,5},{7,6},{9,8},{10,9},{11,10},{12... | collective-permute-start | bytes 983048 | tf_op jit(solution)/shard_map/ppermute | solution.py:18
  27.1 8.1 %collective-permute-start.1 = (bf16[16,80,128]{2,1,0:T(8,128)(2,1)S(1)}, bf16[16,80,128]{2,1,0:T(8,128)(2,1)S(1)}, u32[]{:S(2)}, u32[]{:S(2)}) collective-permute-start(bf16[16,80,128]{2,1,0:T(8,128)(2,1)S(1)} %reshape_reshape.3.refs_5_), channel_id=1, source_target_pairs={{0,1},{1,2},{2,3},{3,4},{4,5},{5,6},{6,7},{8,9},{9,10},{10,11},{11... | collective-permute-start | bytes 983048 | tf_op jit(solution)/shard_map/ppermute | solution.py:18
  31.7 8.0 %collective-permute-start = (bf16[16,80,128]{2,1,0:T(8,128)(2,1)S(1)}, bf16[16,80,128]{2,1,0:T(8,128)(2,1)S(1)}, u32[]{:S(2)}, u32[]{:S(2)}) collective-permute-start(bf16[16,80,128]{2,1,0:T(8,128)(2,1)S(1)} %reshape_reshape.3.refs_5_), channel_id=1, source_target_pairs={{0,2},{2,4},{3,1},{4,6},{5,3},{7,5},{8,10},{10,12},{11,9},{12,14},... | collective-permute-start | bytes 983048 | tf_op jit(solution)/shard_map/ppermute | solution.py:158
  35.2 1.5 %copy-start = (bf16[16,80,128]{2,1,0:T(8,128)(2,1)}, bf16[16,80,128]{2,1,0:T(8,128)(2,1)S(1)}, u32[]{:S(2)}) copy-start(bf16[16,80,128]{2,1,0:T(8,128)(2,1)S(1)} %collective-permute-done.2.refs_6_) | copy-start | bytes 983044
  35.2 1.4 %copy-start.1 = (bf16[16,80,128]{2,1,0:T(8,128)(2,1)}, bf16[16,80,128]{2,1,0:T(8,128)(2,1)S(1)}, u32[]{:S(2)}) copy-start(bf16[16,80,128]{2,1,0:T(8,128)(2,1)S(1)} %collective-permute-done.1.refs_4_) | copy-start | bytes 983044
  35.2 4.5 %collective-permute-start.3 = (bf16[16,80,128]{2,1,0:T(8,128)(2,1)S(1)}, bf16[16,80,128]{2,1,0:T(8,128)(2,1)S(1)}, u32[]{:S(2)}, u32[]{:S(2)}) collective-permute-start(bf16[16,80,128]{2,1,0:T(8,128)(2,1)S(1)} %broadcast_select_fusion), channel_id=1, source_target_pairs={{0,1},{1,0},{2,3},{3,2},{4,5},{5,4},{6,7},{7,6},{8,9},{9,8},{10,11... | collective-permute-start | bytes 983048 | tf_op jit(solution)/shard_map/ppermute | solution.py:162
  39.7 0.7 %copy-start.3 = (bf16[16,80,128]{2,1,0:T(8,128)(2,1)}, bf16[16,80,128]{2,1,0:T(8,128)(2,1)S(1)}, u32[]{:S(2)}) copy-start(bf16[16,80,128]{2,1,0:T(8,128)(2,1)S(1)} %collective-permute-done.refs_2_) | copy-start | bytes 983044
  40.4 0.7 %copy-start.4 = (bf16[16,80,128]{2,1,0:T(8,128)(2,1)}, bf16[16,80,128]{2,1,0:T(8,128)(2,1)S(1)}, u32[]{:S(2)}) copy-start(bf16[16,80,128]{2,1,0:T(8,128)(2,1)S(1)} %collective-permute-done.3.refs_3_) | copy-start | bytes 983044

commit v11 on v10

--- a/solution.py
+++ b/solution.py
@@ -1,6 +1,7 @@
 import math
 
 import jax
+import numpy as np
 import jax.numpy as jnp
 from jax import lax
 from jax.experimental import pallas as pl
@@ -20,23 +21,21 @@
 
 def dft_factors(samples, bins, groups):
     local = bins // groups
-    column = jnp.arange(2 * bins, dtype=jnp.int32)
+    column = np.arange(2 * bins)
     group_of = column // (2 * local)
     part_of = column // local % 2
     harmonic = group_of * local + column % local + 1
     fine = 1 << ((samples.bit_length() - 1) // 2)
     coarse = samples // fine
     unit = 2.0 * math.pi / samples
-    outer = (jnp.arange(coarse, dtype=jnp.int32)[:, None] * fine * harmonic[None, :]) % samples
-    inner = (jnp.arange(fine, dtype=jnp.int32)[:, None] * harmonic[None, :]) % samples
-    c1 = jnp.cos(outer.astype(jnp.float32) * unit)
-    s1 = jnp.sin(outer.astype(jnp.float32) * unit)
-    c2 = jnp.cos(inner.astype(jnp.float32) * unit)
-    s2 = jnp.sin(inner.astype(jnp.float32) * unit)
+    outer = (np.arange(coarse)[:, None] * fine * harmonic[None, :]) % samples * unit
+    inner = (np.arange(fine)[:, None] * harmonic[None, :]) % samples * unit
     is_cos = part_of[None, :] == 0
-    p1 = jnp.where(is_cos, c1, -s1)
-    q1 = jnp.where(is_cos, -s1, -c1)
-    return p1, q1, c2, s2
+    p1 = np.where(is_cos, np.cos(outer), -np.sin(outer))
+    q1 = np.where(is_cos, -np.sin(outer), -np.cos(outer))
+    c2 = np.cos(inner)
+    s2 = np.sin(inner)
+    return tuple(jnp.asarray(t.astype(np.float32)) for t in (p1, q1, c2, s2))
 
 
 def split_bf16(v):

time: 48.4 us -> 47.1 us (0.973)
  other arithmetic: 3.09 us -> 1.77 us
    select_n x1 -> x0, other arithmetic: 1.27 us -> none  [dft_factors(): q1 = jnp.where(is_cos, -s1, -c1)]
where the time goes in v11:
time: 47.1 us; the launch traced here: 46.2 us
  Pallas kernels  14.5 us (31%)
  blocking collectives  11.6 us (25%)
  starting transfers between devices  8.04 us (17%)
  local copies, waits for them, and re-layouts  6.54 us (14%)
  waiting for transfers between devices  3.04 us (6%)
  other arithmetic  1.77 us (4%)
  between operations  0.84 us (2%)
    all_to_all x1, blocking collectives, body(): lax.all_to_all(own_spec, 'tm', split_axis=3, concat_axis=2, tiled=True)  11.6 us
    pallas_call x1, Pallas kernels, whiten(): pl.pallas_call(dft_kernel, grid=(samples // (fine * coarse_step),), in_sp...  8.07 us
    pallas_call x1, Pallas kernels, cross_block(): pl.pallas_call(kernel, grid_spec=grid_spec, out_shape=jax.ShapeDtypeStruc...  6.39 us
    ppermute x2, starting transfers between devices, passed_along(): return lax.ppermute(array, axis, pairs)  4.34 us
    ppermute x1, starting transfers between devices, body(): lax.ppermute(paired, 'sta', [(i, i + 2 - 4 * (i % 2)) for i in range(peer...  3.49 us
    ppermute x1, waiting for transfers between devices, body(): lax.ppermute(paired, 'sta', [(i, i + 2 - 4 * (i % 2)) for i in range(peer...  3.03 us
    unnamed x14, local copies, waits for them, and re-layouts  2.37 us
    reshape x2, local copies, waits for them, and re-layouts, whiten(): return white.reshape(1, stations, windows, groups, width // groups)  1.4 us
  transfers between devices with their start and end apart: 4, of which 1 were waited for; matrix products, arithmetic and copies ran while one was open for 4% of the time, Pallas kernels for 0%

profile of v11, /device:TPU:0, one launch (start us, length us, event | category | flops | bytes accessed | tf_op | source)
XLA Modules:
  0.0 46.2 jit_solution(17583472313681195971)
XLA Ops:
  0.0 8.1 %shard_map.73 = bf16[640,256]{1,0:T(8,128)(2,1)} custom-call(f32[64,256]{1,0:T(8,128)} %constant.35.clone.p1_ref, f32[64,256]{1,0:T(8,128)} %constant.36.clone.q1_ref, f32[64,256]{1,0:T(8,128)} %constant.37.clone.c2_ref, f32[64,256]{1,0:T(8,128)} %constant.38.clone.s2_ref, f32[640,4096]{1,0:T(8,128)} %bitcast.20), custom_call_target="tpu_custom_call" | custom-call | tf_op jit(solution)/shard_map/pallas_call | solution.py:76
  8.1 1.3 %reshape.27 = bf16[1,40,16,4,64]{4,3,2,1,0:T(4,128)(2,1)S(1)} reshape(bf16[640,256]{1,0:T(8,128)(2,1)} %shard_map.73) | data formatting | bytes 655360 | tf_op jit(solution)/shard_map/reshape | solution.py:90
  9.4 0.1 copy.16
  9.5 0.5 %reshape.34 = bf16[4,2,20480]{2,1,0:T(2,128)(2,1)S(1)} reshape(bf16[4,1,40,16,64]{4,3,2,1,0:T(8,128)(2,1)S(1)} %bitcast.22) | data formatting | bytes 655360
  10.0 11.6 %all_to_all.15 = bf16[4,2,20480]{2,1,0:T(2,128)(2,1)S(1)} all-to-all(bf16[4,2,20480]{2,1,0:T(2,128)(2,1)S(1)} %reshape.34), channel_id=1, replica_groups=mesh['tm'=4,'sta'=8] {'tm'}, dimensions={0} | all-to-all | bytes 655360 | tf_op jit(solution)/shard_map/all_to_all | solution.py:144
  21.5 0.4 reshape.35
  22.0 0.1 bitcast_bitcast_fusion
  22.1 0.8 %copy.12 = bf16[1,40,4,16,1,64]{1,5,3,2,4,0:T(8,128)(2,1)S(1)} copy(bf16[1,40,4,16,1,64]{5,3,1,2,4,0:T(8,128)(2,1)S(1)} %bitcast_bitcast_fusion) | data formatting | bytes 655360 | tf_op jit(solution)/shard_map/all_to_all | solution.py:144
  22.9 0.0 copy-start.5
  22.9 1.3 %copy.13 = bf16[32,40,2,64]{3,2,1,0:T(2,128)(2,1)S(1)} copy(bf16[32,40,2,64]{1,0,2,3:T(8,128)(2,1)S(1)} %bitcast.21) | data formatting | bytes 655360 | tf_op jit(solution)/shard_map/transpose | solution.py:149
  24.2 0.3 reshape_reshape.3.refs_5_
  24.5 0.0 copy-start.2
  24.5 1.3 %collective-permute-start.2 = (bf16[16,80,128]{2,1,0:T(8,128)(2,1)S(1)}, bf16[16,80,128]{2,1,0:T(8,128)(2,1)S(1)}, u32[]{:S(2)}, u32[]{:S(2)}) collective-permute-start(bf16[16,80,128]{2,1,0:T(8,128)(2,1)S(1)} %reshape_reshape.3.refs_5_), channel_id=1, source_target_pairs={{1,0},{2,1},{3,2},{4,3},{5,4},{6,5},{7,6},{9,8},{10,9},{11,10},{12... | collective-permute-start | bytes 983048 | tf_op jit(solution)/shard_map/ppermute | solution.py:19
  25.8 3.1 %collective-permute-start.1 = (bf16[16,80,128]{2,1,0:T(8,128)(2,1)S(1)}, bf16[16,80,128]{2,1,0:T(8,128)(2,1)S(1)}, u32[]{:S(2)}, u32[]{:S(2)}) collective-permute-start(bf16[16,80,128]{2,1,0:T(8,128)(2,1)S(1)} %reshape_reshape.3.refs_5_), channel_id=1, source_target_pairs={{0,1},{1,2},{2,3},{3,4},{4,5},{5,6},{6,7},{8,9},{9,10},{10,11},{11... | collective-permute-start | bytes 983048 | tf_op jit(solution)/shard_map/ppermute | solution.py:19
  29.5 0.0 copy-done.5
  29.5 0.5 %compare_select_fusion.2.refs_0_ = s32[5]{0:T(128)} fusion(s32[1,5]{1,0:T(1,128)S(1)} %copy-done.5, s32[]{:T(128)S(6)} %sub.12, s32[]{:T(128)S(6)} %select_n.26, s32[]{:T(128)S(6)} %axis_index.12, s32[]{:T(128)} %bitcast.19), kind=kLoop, calls=%fused_computation.5 | loop fusion | flops 50 | bytes 56 | tf_op jit(solution)/shard_map/jit(_where)/select_n | solution.py:168
  30.1 0.3 reshape.29
  30.3 3.5 %collective-permute-start = (bf16[16,80,128]{2,1,0:T(8,128)(2,1)S(1)}, bf16[16,80,128]{2,1,0:T(8,128)(2,1)S(1)}, u32[]{:S(2)}, u32[]{:S(2)}) collective-permute-start(bf16[16,80,128]{2,1,0:T(8,128)(2,1)S(1)} %reshape_reshape.3.refs_5_), channel_id=1, source_target_pairs={{0,2},{2,4},{3,1},{4,6},{5,3},{7,5},{8,10},{10,12},{11,9},{12,14},... | collective-permute-start | bytes 983048 | tf_op jit(solution)/shard_map/ppermute | solution.py:157
  33.8 0.0 collective-permute-done.2.refs_6_
  33.8 0.0 copy-start
  33.9 0.0 collective-permute-done.1.refs_4_
  33.9 0.0 copy-start.1
  33.9 0.2 collective-permute-start.3
  34.1 0.2 slice_negate_fusion
  34.3 0.0 copy-done.2
  34.3 1.0 %maximum_maximum_fusion.refs_1_ = bf16[32,80,128]{2,1,0:T(8,128)(2,1)} fusion(bf16[32,40,64]{2,1,0:T(8,128)(2,1)S(1)} %get-tuple-element.6, bf16[32,40,64]{2,1,0:T(8,128)(2,1)S(1)} %get-tuple-element.5, bf16[32,40,128]{2,1,0:T(8,128)(2,1)S(1)} %reshape.29), kind=kLoop, calls=%fused_computation | loop fusion | flops 1966080 | bytes 1310720 | tf_op jit(solution)/shard_map/concatenate | solution.py:171
  35.4 0.0 copy-done
  35.4 3.0 %collective-permute-done.refs_2_ = bf16[16,80,128]{2,1,0:T(8,128)(2,1)S(1)} collective-permute-done((bf16[16,80,128]{2,1,0:T(8,128)(2,1)S(1)}, bf16[16,80,128]{2,1,0:T(8,128)(2,1)S(1)}, u32[]{:S(2)}, u32[]{:S(2)}) %collective-permute-start) | collective-permute-done | bytes 327712 | tf_op jit(solution)/shard_map/ppermute | solution.py:157
  38.4 0.0 collective-permute-done.3.refs_3_
  38.4 0.7 %copy-done.3 = bf16[16,80,128]{2,1,0:T(8,128)(2,1)} copy-done((bf16[16,80,128]{2,1,0:T(8,128)(2,1)}, bf16[16,80,128]{2,1,0:T(8,128)(2,1)S(1)}, u32[]{:S(2)}) %copy-start.3) | copy-done | bytes 327704
  39.1 0.7 %copy-done.4 = bf16[16,80,128]{2,1,0:T(8,128)(2,1)} copy-done((bf16[16,80,128]{2,1,0:T(8,128)(2,1)}, bf16[16,80,128]{2,1,0:T(8,128)(2,1)S(1)}, u32[]{:S(2)}) %copy-start.4) | copy-done | bytes 327704
  39.9 6.4 %shard_map.74 = f32[5,40,2560]{2,1,0:T(8,128)} custom-call(s32[5]{0:T(128)} %compare_select_fusion.2.refs_0_, bf16[32,80,128]{2,1,0:T(8,128)(2,1)} %maximum_maximum_fusion.refs_1_, bf16[16,80,128]{2,1,0:T(8,128)(2,1)} %copy-done.3, bf16[16,80,128]{2,1,0:T(8,128)(2,1)} %copy-done.4, bf16[16,80,128]{2,1,0:T(8,128)(2,1)} %copy-done.1, ...), custom_call_target="tpu_custom_call" | custom-call | tf_op jit(solution)/shard_map/pallas_call | solution.py:131
  (4 shorter events, 0.0 us)
Async XLA Ops:
  22.9 6.6 %copy-start.5 = (s32[1,5]{1,0:T(1,128)S(1)}, s32[1,5]{1,0:T(1,128)}, u32[]{:S(2)}) copy-start(s32[1,5]{1,0:T(1,128)} %param.8) | copy-start | bytes 64
  24.5 9.8 %copy-start.2 = (bf16[16,80,128]{2,1,0:T(8,128)(2,1)}, bf16[16,80,128]{2,1,0:T(8,128)(2,1)S(1)}, u32[]{:S(2)}) copy-start(bf16[16,80,128]{2,1,0:T(8,128)(2,1)S(1)} %reshape_reshape.3.refs_5_) | copy-start | bytes 983044
  24.5 9.3 %collective-permute-start.2 = (bf16[16,80,128]{2,1,0:T(8,128)(2,1)S(1)}, bf16[16,80,128]{2,1,0:T(8,128)(2,1)S(1)}, u32[]{:S(2)}, u32[]{:S(2)}) collective-permute-start(bf16[16,80,128]{2,1,0:T(8,128)(2,1)S(1)} %reshape_reshape.3.refs_5_), channel_id=1, source_target_pairs={{1,0},{2,1},{3,2},{4,3},{5,4},{6,5},{7,6},{9,8},{10,9},{11,10},{12... | collective-permute-start | bytes 983048 | tf_op jit(solution)/shard_map/ppermute | solution.py:19
  25.8 8.1 %collective-permute-start.1 = (bf16[16,80,128]{2,1,0:T(8,128)(2,1)S(1)}, bf16[16,80,128]{2,1,0:T(8,128)(2,1)S(1)}, u32[]{:S(2)}, u32[]{:S(2)}) collective-permute-start(bf16[16,80,128]{2,1,0:T(8,128)(2,1)S(1)} %reshape_reshape.3.refs_5_), channel_id=1, source_target_pairs={{0,1},{1,2},{2,3},{3,4},{4,5},{5,6},{6,7},{8,9},{9,10},{10,11},{11... | collective-permute-start | bytes 983048 | tf_op jit(solution)/shard_map/ppermute | solution.py:19
  30.3 8.0 %collective-permute-start = (bf16[16,80,128]{2,1,0:T(8,128)(2,1)S(1)}, bf16[16,80,128]{2,1,0:T(8,128)(2,1)S(1)}, u32[]{:S(2)}, u32[]{:S(2)}) collective-permute-start(bf16[16,80,128]{2,1,0:T(8,128)(2,1)S(1)} %reshape_reshape.3.refs_5_), channel_id=1, source_target_pairs={{0,2},{2,4},{3,1},{4,6},{5,3},{7,5},{8,10},{10,12},{11,9},{12,14},... | collective-permute-start | bytes 983048 | tf_op jit(solution)/shard_map/ppermute | solution.py:157
  33.8 1.5 %copy-start = (bf16[16,80,128]{2,1,0:T(8,128)(2,1)}, bf16[16,80,128]{2,1,0:T(8,128)(2,1)S(1)}, u32[]{:S(2)}) copy-start(bf16[16,80,128]{2,1,0:T(8,128)(2,1)S(1)} %collective-permute-done.2.refs_6_) | copy-start | bytes 983044
  33.9 1.5 %copy-start.1 = (bf16[16,80,128]{2,1,0:T(8,128)(2,1)}, bf16[16,80,128]{2,1,0:T(8,128)(2,1)S(1)}, u32[]{:S(2)}) copy-start(bf16[16,80,128]{2,1,0:T(8,128)(2,1)S(1)} %collective-permute-done.1.refs_4_) | copy-start | bytes 983044
  33.9 4.5 %collective-permute-start.3 = (bf16[16,80,128]{2,1,0:T(8,128)(2,1)S(1)}, bf16[16,80,128]{2,1,0:T(8,128)(2,1)S(1)}, u32[]{:S(2)}, u32[]{:S(2)}) collective-permute-start(bf16[16,80,128]{2,1,0:T(8,128)(2,1)S(1)} %broadcast_select_fusion), channel_id=1, source_target_pairs={{0,1},{1,0},{2,3},{3,2},{4,5},{5,4},{6,7},{7,6},{8,9},{9,8},{10,11... | collective-permute-start | bytes 983048 | tf_op jit(solution)/shard_map/ppermute | solution.py:161
  38.4 0.7 %copy-start.3 = (bf16[16,80,128]{2,1,0:T(8,128)(2,1)}, bf16[16,80,128]{2,1,0:T(8,128)(2,1)S(1)}, u32[]{:S(2)}) copy-start(bf16[16,80,128]{2,1,0:T(8,128)(2,1)S(1)} %collective-permute-done.refs_2_) | copy-start | bytes 983044
  39.1 0.7 %copy-start.4 = (bf16[16,80,128]{2,1,0:T(8,128)(2,1)}, bf16[16,80,128]{2,1,0:T(8,128)(2,1)S(1)}, u32[]{:S(2)}) copy-start(bf16[16,80,128]{2,1,0:T(8,128)(2,1)S(1)} %collective-permute-done.3.refs_3_) | copy-start | bytes 983044

commit v12 on v11

--- a/solution.py
+++ b/solution.py
@@ -136,12 +136,17 @@
 
 
 def body(records, partners, counts):
-    own_spec = whiten(records, lax.axis_size("tm"))
+    own_spec = whiten(records, lax.axis_size("tmy") * lax.axis_size("tmx"))
     block_index = lax.axis_index("sta")
     partner_row = partners[0]
     slots = partner_row.shape[0]
     live_slots = jnp.arange(slots, dtype=jnp.int32) < counts[0]
-    regrouped = lax.all_to_all(own_spec, "tm", split_axis=3, concat_axis=2, tiled=True)
+    _, stations0, windows0, groups0, width0 = own_spec.shape
+    ny = lax.axis_size("tmy")
+    split = own_spec.reshape(stations0, windows0, ny, groups0 // ny, width0)
+    split = lax.all_to_all(split, "tmx", split_axis=3, concat_axis=1, tiled=True)
+    split = lax.all_to_all(split, "tmy", split_axis=2, concat_axis=1, tiled=True)
+    regrouped = split.reshape(1, stations0, windows0 * groups0, 1, width0)
     stations, windows, width = regrouped.shape[1], regrouped.shape[2], regrouped.shape[4]
     nb = width // 2
     spec = (
@@ -174,6 +179,12 @@
 
 
 def solution(mesh):
-    in_specs = (P("sta", "tm", None), P("sta", None), P("sta"))
-    out_specs = P("sta", None, None, "tm")
-    return jax.shard_map(body, mesh=mesh, in_specs=in_specs, out_specs=out_specs, check_vma=False)
+    tm, sta = mesh.devices.shape
+    chips_x = 2 if tm % 2 == 0 else 1
+    split_mesh = jax.sharding.Mesh(
+        mesh.devices.reshape(tm // chips_x, chips_x, sta), ("tmy", "tmx", "sta")
+    )
+    tm_axes = ("tmy", "tmx")
+    in_specs = (P("sta", tm_axes, None), P("sta", None), P("sta"))
+    out_specs = P("sta", None, None, tm_axes)
+    return jax.shard_map(body, mesh=split_mesh, in_specs=in_specs, out_specs=out_specs, check_vma=False)

time: 47.1 us -> 54.9 us (1.17)
  blocking collectives: 11.6 us -> 18.1 us
  local copies, waits for them, and re-layouts: 6.54 us -> 7.81 us
    all_to_all x1 -> x2, blocking collectives: 11.6 us -> 18.1 us  [the longest x1 9.88 us: body(): lax.all_to_all(split, 'tmx', split_axis=3, concat_axis=1, tiled=True)]
    another operation x0 -> x2, local copies, waits for them, and re-layouts: none -> 1.41 us  [body(): split = own_spec.reshape(stations0, windows0, ny, groups0 // ny, width0)]
    reshape x2 -> x0, local copies, waits for them, and re-layouts: 1.4 us -> none  [whiten(): return white.reshape(1, stations, windows, groups, width // groups)]
    unnamed x14 -> x17, local copies, waits for them, and re-layouts: 2.37 us -> 3.38 us
    all_to_all x2 -> x3, local copies, waits for them, and re-layouts: 0.9 us -> 1.15 us  [the longest x2 0.97 us: body(): lax.all_to_all(split, 'tmy', split_axis=2, concat_axis=1, tiled=True)]
where the time goes in v12:
time: 54.9 us; the launch traced here: 54.1 us
  blocking collectives  18.1 us (33%)
  Pallas kernels  14.5 us (26%)
  starting transfers between devices  8.04 us (15%)
  local copies, waits for them, and re-layouts  7.81 us (14%)
  waiting for transfers between devices  3.04 us (6%)
  other arithmetic  1.77 us (3%)
  between operations  0.87 us (2%)
    all_to_all x1, blocking collectives, body(): lax.all_to_all(split, 'tmx', split_axis=3, concat_axis=1, tiled=True)  9.88 us
    all_to_all x1, blocking collectives, body(): lax.all_to_all(split, 'tmy', split_axis=2, concat_axis=1, tiled=True)  8.22 us
    pallas_call x1, Pallas kernels, whiten(): pl.pallas_call(dft_kernel, grid=(samples // (fine * coarse_step),), in_sp...  8.07 us
    pallas_call x1, Pallas kernels, cross_block(): pl.pallas_call(kernel, grid_spec=grid_spec, out_shape=jax.ShapeDtypeStruc...  6.39 us
    ppermute x2, starting transfers between devices, passed_along(): return lax.ppermute(array, axis, pairs)  4.34 us
    ppermute x1, starting transfers between devices, body(): lax.ppermute(paired, 'sta', [(i, i + 2 - 4 * (i % 2)) for i in range(peer...  3.49 us
    unnamed x17, local copies, waits for them, and re-layouts  3.38 us
    ppermute x1, waiting for transfers between devices, body(): lax.ppermute(paired, 'sta', [(i, i + 2 - 4 * (i % 2)) for i in range(peer...  3.03 us
  transfers between devices with their start and end apart: 4, of which 1 were waited for; matrix products, arithmetic and copies ran while one was open for 4% of the time, Pallas kernels for 0%

profile of v12, /device:TPU:0, one launch (start us, length us, event | category | flops | bytes accessed | tf_op | source)
XLA Modules:
  0.0 54.1 jit_solution(15470766232799499285)
XLA Ops:
  0.0 8.1 %shard_map.73 = bf16[640,256]{1,0:T(8,128)(2,1)} custom-call(f32[64,256]{1,0:T(8,128)} %constant.35.clone.p1_ref, f32[64,256]{1,0:T(8,128)} %constant.36.clone.q1_ref, f32[64,256]{1,0:T(8,128)} %constant.37.clone.c2_ref, f32[64,256]{1,0:T(8,128)} %constant.38.clone.s2_ref, f32[640,4096]{1,0:T(8,128)} %bitcast.31), custom_call_target="tpu_custom_call" | custom-call | tf_op jit(solution)/shard_map/pallas_call | solution.py:76
  8.1 1.3 %reshape_reshape.9 = bf16[40,16,2,2,64]{4,3,2,1,0:T(2,128)(2,1)S(1)} reshape(bf16[640,256]{1,0:T(8,128)(2,1)} %shard_map.73) | data formatting | bytes 655360 | tf_op jit(solution)/shard_map/reshape;reshape | solution.py:146
  9.4 0.1 copy.22
  9.5 0.5 reshape.26
  10.0 9.9 %all_to_all.33 = bf16[2,2,40960]{2,1,0:T(2,128)(2,1)S(1)} all-to-all(bf16[2,2,40960]{2,1,0:T(2,128)(2,1)S(1)} %reshape.26), channel_id=1, replica_groups=mesh['tmy'=2,'tmx'=2,'sta'=8] {'tmx'}, dimensions={0} | all-to-all | bytes 655360 | tf_op jit(solution)/shard_map/all_to_all | solution.py:147
  19.9 0.4 reshape.27
  20.3 0.2 copy.13
  20.5 0.1 copy_bitcast_fusion.1
  20.6 0.5 reshape.28
  21.1 8.2 %all_to_all.34 = bf16[2,2,40960]{2,1,0:T(2,128)(2,1)S(1)} all-to-all(bf16[2,2,40960]{2,1,0:T(2,128)(2,1)S(1)} %reshape.28), channel_id=1, replica_groups=mesh['tmy'=2,'tmx'=2,'sta'=8] {'tmy'}, dimensions={0} | all-to-all | bytes 655360 | tf_op jit(solution)/shard_map/all_to_all | solution.py:148
  29.3 0.4 reshape.29
  29.7 0.1 copy_bitcast_fusion
  29.8 0.9 %copy.16 = bf16[40,2,32,1,1,64]{0,5,2,1,4,3:T(8,128)(2,1)S(1)} copy(bf16[40,2,32,1,1,64]{5,2,4,3,1,0:T(8,128)(2,1)S(1)} %copy_bitcast_fusion) | data formatting | bytes 655360 | tf_op jit(solution)/shard_map/all_to_all | solution.py:148
  30.7 0.0 copy-start.5
  30.7 1.3 %copy.17 = bf16[32,40,2,64]{3,2,1,0:T(2,128)(2,1)S(1)} copy(bf16[32,40,2,64]{1,0,2,3:T(8,128)(2,1)S(1)} %bitcast.32) | data formatting | bytes 655360 | tf_op jit(solution)/shard_map/transpose | solution.py:154
  32.0 0.3 reshape_reshape.11.refs_5_
  32.3 1.3 %collective-permute-start.2 = (bf16[16,80,128]{2,1,0:T(8,128)(2,1)S(1)}, bf16[16,80,128]{2,1,0:T(8,128)(2,1)S(1)}, u32[]{:S(2)}, u32[]{:S(2)}) collective-permute-start(bf16[16,80,128]{2,1,0:T(8,128)(2,1)S(1)} %reshape_reshape.11.refs_5_), channel_id=1, source_target_pairs={{1,0},{2,1},{3,2},{4,3},{5,4},{6,5},{7,6},{9,8},{10,9},{11,10},{12... | collective-permute-start | bytes 983048 | tf_op jit(solution)/shard_map/ppermute | solution.py:19
  33.6 3.1 %collective-permute-start.1 = (bf16[16,80,128]{2,1,0:T(8,128)(2,1)S(1)}, bf16[16,80,128]{2,1,0:T(8,128)(2,1)S(1)}, u32[]{:S(2)}, u32[]{:S(2)}) collective-permute-start(bf16[16,80,128]{2,1,0:T(8,128)(2,1)S(1)} %reshape_reshape.11.refs_5_), channel_id=1, source_target_pairs={{0,1},{1,2},{2,3},{3,4},{4,5},{5,6},{6,7},{8,9},{9,10},{10,11},{11... | collective-permute-start | bytes 983048 | tf_op jit(solution)/shard_map/ppermute | solution.py:19
  37.4 0.5 compare_select_fusion.2.refs_0_
  37.9 0.3 reshape.21
  38.2 3.5 %collective-permute-start = (bf16[16,80,128]{2,1,0:T(8,128)(2,1)S(1)}, bf16[16,80,128]{2,1,0:T(8,128)(2,1)S(1)}, u32[]{:S(2)}, u32[]{:S(2)}) collective-permute-start(bf16[16,80,128]{2,1,0:T(8,128)(2,1)S(1)} %reshape_reshape.11.refs_5_), channel_id=1, source_target_pairs={{0,2},{2,4},{3,1},{4,6},{5,3},{7,5},{8,10},{10,12},{11,9},{12,14},... | collective-permute-start | bytes 983048 | tf_op jit(solution)/shard_map/ppermute | solution.py:162
  41.7 0.0 collective-permute-done.2.refs_6_
  41.7 0.0 collective-permute-done.1.refs_4_
  41.8 0.2 collective-permute-start.3
  42.0 0.2 slice_negate_fusion
  42.1 1.0 %maximum_maximum_fusion.refs_1_ = bf16[32,80,128]{2,1,0:T(8,128)(2,1)} fusion(bf16[32,40,64]{2,1,0:T(8,128)(2,1)S(1)} %get-tuple-element.6, bf16[32,40,64]{2,1,0:T(8,128)(2,1)S(1)} %get-tuple-element.5, bf16[32,40,128]{2,1,0:T(8,128)(2,1)S(1)} %reshape.21), kind=kLoop, calls=%fused_computation | loop fusion | flops 1966080 | bytes 1310720 | tf_op jit(solution)/shard_map/concatenate | solution.py:176
  43.2 0.0 copy-done.1
  43.2 3.0 %collective-permute-done.refs_2_ = bf16[16,80,128]{2,1,0:T(8,128)(2,1)S(1)} collective-permute-done((bf16[16,80,128]{2,1,0:T(8,128)(2,1)S(1)}, bf16[16,80,128]{2,1,0:T(8,128)(2,1)S(1)}, u32[]{:S(2)}, u32[]{:S(2)}) %collective-permute-start) | collective-permute-done | bytes 327712 | tf_op jit(solution)/shard_map/ppermute | solution.py:162
  46.2 0.0 collective-permute-done.3.refs_3_
  46.2 0.7 %copy-done.3 = bf16[16,80,128]{2,1,0:T(8,128)(2,1)} copy-done((bf16[16,80,128]{2,1,0:T(8,128)(2,1)}, bf16[16,80,128]{2,1,0:T(8,128)(2,1)S(1)}, u32[]{:S(2)}) %copy-start.3) | copy-done | bytes 327704
  47.0 0.7 %copy-done.4 = bf16[16,80,128]{2,1,0:T(8,128)(2,1)} copy-done((bf16[16,80,128]{2,1,0:T(8,128)(2,1)}, bf16[16,80,128]{2,1,0:T(8,128)(2,1)S(1)}, u32[]{:S(2)}) %copy-start.4) | copy-done | bytes 327704
  47.7 6.4 %shard_map.74 = f32[5,40,2560]{2,1,0:T(8,128)} custom-call(s32[5]{0:T(128)} %compare_select_fusion.2.refs_0_, bf16[32,80,128]{2,1,0:T(8,128)(2,1)} %maximum_maximum_fusion.refs_1_, bf16[16,80,128]{2,1,0:T(8,128)(2,1)} %copy-done.3, bf16[16,80,128]{2,1,0:T(8,128)(2,1)} %copy-done.4, bf16[16,80,128]{2,1,0:T(8,128)(2,1)} %copy-done.1, ...), custom_call_target="tpu_custom_call" | custom-call | tf_op jit(solution)/shard_map/pallas_call | solution.py:131
  (9 shorter events, 0.1 us)
Async XLA Ops:
  30.7 6.6 %copy-start.5 = (s32[1,5]{1,0:T(1,128)S(1)}, s32[1,5]{1,0:T(1,128)}, u32[]{:S(2)}) copy-start(s32[1,5]{1,0:T(1,128)} %param.8) | copy-start | bytes 64
  32.3 9.8 %copy-start.2 = (bf16[16,80,128]{2,1,0:T(8,128)(2,1)}, bf16[16,80,128]{2,1,0:T(8,128)(2,1)S(1)}, u32[]{:S(2)}) copy-start(bf16[16,80,128]{2,1,0:T(8,128)(2,1)S(1)} %reshape_reshape.11.refs_5_) | copy-start | bytes 983044
  32.3 9.3 %collective-permute-start.2 = (bf16[16,80,128]{2,1,0:T(8,128)(2,1)S(1)}, bf16[16,80,128]{2,1,0:T(8,128)(2,1)S(1)}, u32[]{:S(2)}, u32[]{:S(2)}) collective-permute-start(bf16[16,80,128]{2,1,0:T(8,128)(2,1)S(1)} %reshape_reshape.11.refs_5_), channel_id=1, source_target_pairs={{1,0},{2,1},{3,2},{4,3},{5,4},{6,5},{7,6},{9,8},{10,9},{11,10},{12... | collective-permute-start | bytes 983048 | tf_op jit(solution)/shard_map/ppermute | solution.py:19
  33.6 8.1 %collective-permute-start.1 = (bf16[16,80,128]{2,1,0:T(8,128)(2,1)S(1)}, bf16[16,80,128]{2,1,0:T(8,128)(2,1)S(1)}, u32[]{:S(2)}, u32[]{:S(2)}) collective-permute-start(bf16[16,80,128]{2,1,0:T(8,128)(2,1)S(1)} %reshape_reshape.11.refs_5_), channel_id=1, source_target_pairs={{0,1},{1,2},{2,3},{3,4},{4,5},{5,6},{6,7},{8,9},{9,10},{10,11},{11... | collective-permute-start | bytes 983048 | tf_op jit(solution)/shard_map/ppermute | solution.py:19
  38.2 8.0 %collective-permute-start = (bf16[16,80,128]{2,1,0:T(8,128)(2,1)S(1)}, bf16[16,80,128]{2,1,0:T(8,128)(2,1)S(1)}, u32[]{:S(2)}, u32[]{:S(2)}) collective-permute-start(bf16[16,80,128]{2,1,0:T(8,128)(2,1)S(1)} %reshape_reshape.11.refs_5_), channel_id=1, source_target_pairs={{0,2},{2,4},{3,1},{4,6},{5,3},{7,5},{8,10},{10,12},{11,9},{12,14},... | collective-permute-start | bytes 983048 | tf_op jit(solution)/shard_map/ppermute | solution.py:162
  41.7 1.5 %copy-start = (bf16[16,80,128]{2,1,0:T(8,128)(2,1)}, bf16[16,80,128]{2,1,0:T(8,128)(2,1)S(1)}, u32[]{:S(2)}) copy-start(bf16[16,80,128]{2,1,0:T(8,128)(2,1)S(1)} %collective-permute-done.2.refs_6_) | copy-start | bytes 983044
  41.7 1.5 %copy-start.1 = (bf16[16,80,128]{2,1,0:T(8,128)(2,1)}, bf16[16,80,128]{2,1,0:T(8,128)(2,1)S(1)}, u32[]{:S(2)}) copy-start(bf16[16,80,128]{2,1,0:T(8,128)(2,1)S(1)} %collective-permute-done.1.refs_4_) | copy-start | bytes 983044
  41.8 4.5 %collective-permute-start.3 = (bf16[16,80,128]{2,1,0:T(8,128)(2,1)S(1)}, bf16[16,80,128]{2,1,0:T(8,128)(2,1)S(1)}, u32[]{:S(2)}, u32[]{:S(2)}) collective-permute-start(bf16[16,80,128]{2,1,0:T(8,128)(2,1)S(1)} %broadcast_select_fusion), channel_id=1, source_target_pairs={{0,1},{1,0},{2,3},{3,2},{4,5},{5,4},{6,7},{7,6},{8,9},{9,8},{10,11... | collective-permute-start | bytes 983048 | tf_op jit(solution)/shard_map/ppermute | solution.py:166
  46.2 0.7 %copy-start.3 = (bf16[16,80,128]{2,1,0:T(8,128)(2,1)}, bf16[16,80,128]{2,1,0:T(8,128)(2,1)S(1)}, u32[]{:S(2)}) copy-start(bf16[16,80,128]{2,1,0:T(8,128)(2,1)S(1)} %collective-permute-done.refs_2_) | copy-start | bytes 983044
  47.0 0.7 %copy-start.4 = (bf16[16,80,128]{2,1,0:T(8,128)(2,1)}, bf16[16,80,128]{2,1,0:T(8,128)(2,1)S(1)}, u32[]{:S(2)}) copy-start(bf16[16,80,128]{2,1,0:T(8,128)(2,1)S(1)} %collective-permute-done.3.refs_3_) | copy-start | bytes 983044

commit v13 on v11

--- a/solution.py
+++ b/solution.py
@@ -90,17 +90,25 @@
     return white.reshape(1, stations, windows, groups, width // groups)
 
 
-def cross_kernel(scale, sel_ref, lx_ref, *refs):
+def cross_kernel(scale, partner_ref, count_ref, lx_ref, *refs):
     *y_refs, o_ref = refs
     bins, two_s, _ = lx_ref.shape
     s = two_s // 2
     slots = o_ref.shape[0]
+    block_index = lax.axis_index("sta")
+    parity = block_index % 2
+    sel = []
+    for p in range(slots):
+        where_at = jnp.clip(partner_ref[p] - block_index + R, 0, 2 * R)
+        slot = jnp.where(where_at == 0, parity, where_at + 1)
+        slot = jnp.where(where_at == 2 * R, 1 - parity, slot)
+        sel.append(jnp.where(p < count_ref[0], slot, -1))
     for j in range(bins // 2):
         picked = []
         for p in range(slots):
             y = jnp.zeros(y_refs[0].shape[1:], y_refs[0].dtype)
             for o, y_ref in enumerate(y_refs):
-                y = jnp.where(sel_ref[p] == o, y_ref[j], y)
+                y = jnp.where(sel[p] == o, y_ref[j], y)
             picked.append(y)
         ycat = jnp.concatenate(picked, axis=0)
         for h in range(2):
@@ -116,23 +124,23 @@
                     o_ref[p, :, col:col + s] = r[x * s:(x + 1) * s, src:src + s]
 
 
-def cross_block(sel, lx, ys, windows, slots):
+def cross_block(partner_row, count, lx, ys, windows, slots):
     nb, two_s, k = lx.shape
     s = two_s // 2
     step = BINS_PER_STEP
     kernel = lambda *refs: cross_kernel(1.0 / windows, *refs)
-    y_spec = pl.BlockSpec((step // 2, two_s, k), lambda g, sel: (g, 0, 0))
+    y_spec = pl.BlockSpec((step // 2, two_s, k), lambda g, *_: (g, 0, 0))
     grid_spec = pltpu.PrefetchScalarGridSpec(
-        num_scalar_prefetch=1,
+        num_scalar_prefetch=2,
         grid=(nb // step,),
-        in_specs=[pl.BlockSpec((step, two_s, k), lambda g, sel: (g, 0, 0))] + [y_spec] * len(ys),
-        out_specs=pl.BlockSpec((slots, s, step * two_s), lambda g, sel: (0, 0, g)),
+        in_specs=[pl.BlockSpec((step, two_s, k), lambda g, *_: (g, 0, 0))] + [y_spec] * len(ys),
+        out_specs=pl.BlockSpec((slots, s, step * two_s), lambda g, *_: (0, 0, g)),
     )
     return pl.pallas_call(
         kernel,
         grid_spec=grid_spec,
         out_shape=jax.ShapeDtypeStruct((slots, s, nb * two_s), jnp.float32),
-    )(sel, lx, *ys)
+    )(partner_row, count, lx, *ys)
 
 
 def body(records, partners, counts):
@@ -162,14 +170,10 @@
         relay, "sta", [(i, i + 1 - 2 * (i % 2)) for i in range(peers) if 0 <= i + 1 - 2 * (i % 2) < peers]
     )
     ys = [far, forwarded, left1, paired, right1]
-    where_at = jnp.clip(partner_row - block_index + R, 0, 2 * R)
-    slot_ref = jnp.where(where_at == 0, parity, where_at + 1)
-    slot_ref = jnp.where(where_at == 2 * R, 1 - parity, slot_ref)
-    sel = jnp.where(live_slots, slot_ref, -1).astype(jnp.int32)
     x_re = spec[:, :, :windows]
     x_im = spec[:, :, windows:]
     lx = jnp.concatenate([spec, jnp.concatenate([-x_im, x_re], axis=2)], axis=1)
-    result = cross_block(sel, lx, ys, windows, slots)
+    result = cross_block(partner_row, counts, lx, ys, windows, slots)
     return result[None]
 
 

time: 47.1 us -> 45.9 us (0.975)
  local copies, waits for them, and re-layouts: 6.54 us -> 5.92 us
  starting transfers between devices: 8.04 us -> 8.58 us
  other arithmetic: 1.77 us -> 1.23 us
  waiting for transfers between devices: 3.04 us -> 2.51 us
    unnamed x14 -> x12, local copies, waits for them, and re-layouts: 2.37 us -> 1.75 us
    ppermute x1, starting transfers between devices: 0.21 us -> 0.75 us  [body(): lax.ppermute(relay, 'sta', [(i, i + 1 - 2 * (i % 2)) for i in range(peers...]
    select_n x1 -> x0, other arithmetic: 0.53 us -> none  [body(): sel = jnp.where(live_slots, slot_ref, -1).astype(jnp.int32)]
    ppermute x1, waiting for transfers between devices: 3.03 us -> 2.5 us  [body(): lax.ppermute(paired, 'sta', [(i, i + 2 - 4 * (i % 2)) for i in range(peer...]
  transfers between devices with their start and end apart: 4 -> 4, of which waited for: 1 -> 1; matrix products, arithmetic and copies ran while one was open for 4% -> 3% of each run, Pallas kernels for 0% -> 0%
where the time goes in v13:
time: 45.9 us; the launch traced here: 45.1 us
  Pallas kernels  14.5 us (32%)
  blocking collectives  11.6 us (25%)
  starting transfers between devices  8.58 us (19%)
  local copies, waits for them, and re-layouts  5.92 us (13%)
  waiting for transfers between devices  2.51 us (5%)
  other arithmetic  1.23 us (3%)
  between operations  0.82 us (2%)
    all_to_all x1, blocking collectives, body(): lax.all_to_all(own_spec, 'tm', split_axis=3, concat_axis=2, tiled=True)  11.6 us
    pallas_call x1, Pallas kernels, whiten(): pl.pallas_call(dft_kernel, grid=(samples // (fine * coarse_step),), in_sp...  8.07 us
    pallas_call x1, Pallas kernels, cross_block(): pl.pallas_call(kernel, grid_spec=grid_spec, out_shape=jax.ShapeDtypeStruc...  6.39 us
    ppermute x2, starting transfers between devices, passed_along(): return lax.ppermute(array, axis, pairs)  4.34 us
    ppermute x1, starting transfers between devices, body(): lax.ppermute(paired, 'sta', [(i, i + 2 - 4 * (i % 2)) for i in range(peer...  3.49 us
    ppermute x1, waiting for transfers between devices, body(): lax.ppermute(paired, 'sta', [(i, i + 2 - 4 * (i % 2)) for i in range(peer...  2.5 us
    unnamed x12, local copies, waits for them, and re-layouts  1.75 us
    reshape x2, local copies, waits for them, and re-layouts, whiten(): return white.reshape(1, stations, windows, groups, width // groups)  1.4 us
  transfers between devices with their start and end apart: 4, of which 1 were waited for; matrix products, arithmetic and copies ran while one was open for 3% of the time, Pallas kernels for 0%

profile of v13, /device:TPU:0, one launch (start us, length us, event | category | flops | bytes accessed | tf_op | source)
XLA Modules:
  0.0 45.1 jit_solution(15411175230887065561)
XLA Ops:
  0.0 8.1 %shard_map.73 = bf16[640,256]{1,0:T(8,128)(2,1)} custom-call(f32[64,256]{1,0:T(8,128)} %constant.26.clone.p1_ref, f32[64,256]{1,0:T(8,128)} %constant.27.clone.q1_ref, f32[64,256]{1,0:T(8,128)} %constant.28.clone.c2_ref, f32[64,256]{1,0:T(8,128)} %constant.29.clone.s2_ref, f32[640,4096]{1,0:T(8,128)} %bitcast.15), custom_call_target="tpu_custom_call" | custom-call | tf_op jit(solution)/shard_map/pallas_call | solution.py:76
  8.1 1.3 %reshape.14 = bf16[1,40,16,4,64]{4,3,2,1,0:T(4,128)(2,1)S(1)} reshape(bf16[640,256]{1,0:T(8,128)(2,1)} %shard_map.73) | data formatting | bytes 655360 | tf_op jit(solution)/shard_map/reshape | solution.py:90
  9.4 0.1 copy.16
  9.5 0.5 %reshape.17 = bf16[4,2,20480]{2,1,0:T(2,128)(2,1)S(1)} reshape(bf16[4,1,40,16,64]{4,3,2,1,0:T(8,128)(2,1)S(1)} %bitcast.17) | data formatting | bytes 655360
  10.0 11.6 %all_to_all.15 = bf16[4,2,20480]{2,1,0:T(2,128)(2,1)S(1)} all-to-all(bf16[4,2,20480]{2,1,0:T(2,128)(2,1)S(1)} %reshape.17), channel_id=1, replica_groups=mesh['tm'=4,'sta'=8] {'tm'}, dimensions={0} | all-to-all | bytes 655360 | tf_op jit(solution)/shard_map/all_to_all | solution.py:152
  21.5 0.4 reshape.18
  22.0 0.1 bitcast_bitcast_fusion
  22.1 0.8 %copy.12 = bf16[1,40,4,16,1,64]{1,5,3,2,4,0:T(8,128)(2,1)S(1)} copy(bf16[1,40,4,16,1,64]{5,3,1,2,4,0:T(8,128)(2,1)S(1)} %bitcast_bitcast_fusion) | data formatting | bytes 655360 | tf_op jit(solution)/shard_map/all_to_all | solution.py:152
  22.9 1.3 %copy.13 = bf16[32,40,2,64]{3,2,1,0:T(2,128)(2,1)S(1)} copy(bf16[32,40,2,64]{1,0,2,3:T(8,128)(2,1)S(1)} %bitcast.16) | data formatting | bytes 655360 | tf_op jit(solution)/shard_map/transpose | solution.py:157
  24.2 0.3 reshape_reshape.3.refs_6_
  24.5 0.0 copy-start.2
  24.5 1.3 %collective-permute-start.2 = (bf16[16,80,128]{2,1,0:T(8,128)(2,1)S(1)}, bf16[16,80,128]{2,1,0:T(8,128)(2,1)S(1)}, u32[]{:S(2)}, u32[]{:S(2)}) collective-permute-start(bf16[16,80,128]{2,1,0:T(8,128)(2,1)S(1)} %reshape_reshape.3.refs_6_), channel_id=1, source_target_pairs={{1,0},{2,1},{3,2},{4,3},{5,4},{6,5},{7,6},{9,8},{10,9},{11,10},{12... | collective-permute-start | bytes 983048 | tf_op jit(solution)/shard_map/ppermute | solution.py:19
  25.8 3.1 %collective-permute-start.1 = (bf16[16,80,128]{2,1,0:T(8,128)(2,1)S(1)}, bf16[16,80,128]{2,1,0:T(8,128)(2,1)S(1)}, u32[]{:S(2)}, u32[]{:S(2)}) collective-permute-start(bf16[16,80,128]{2,1,0:T(8,128)(2,1)S(1)} %reshape_reshape.3.refs_6_), channel_id=1, source_target_pairs={{0,1},{1,2},{2,3},{3,4},{4,5},{5,6},{6,7},{8,9},{9,10},{10,11},{11... | collective-permute-start | bytes 983048 | tf_op jit(solution)/shard_map/ppermute | solution.py:19
  29.5 0.3 reshape.16
  29.8 3.5 %collective-permute-start = (bf16[16,80,128]{2,1,0:T(8,128)(2,1)S(1)}, bf16[16,80,128]{2,1,0:T(8,128)(2,1)S(1)}, u32[]{:S(2)}, u32[]{:S(2)}) collective-permute-start(bf16[16,80,128]{2,1,0:T(8,128)(2,1)S(1)} %reshape_reshape.3.refs_6_), channel_id=1, source_target_pairs={{0,2},{2,4},{3,1},{4,6},{5,3},{7,5},{8,10},{10,12},{11,9},{12,14},... | collective-permute-start | bytes 983048 | tf_op jit(solution)/shard_map/ppermute | solution.py:165
  33.3 0.0 collective-permute-done.2.refs_7_
  33.3 0.0 copy-start
  33.3 0.0 collective-permute-done.1.refs_5_
  33.3 0.0 copy-start.1
  33.4 0.8 %collective-permute-start.3 = (bf16[16,80,128]{2,1,0:T(8,128)(2,1)S(1)}, bf16[16,80,128]{2,1,0:T(8,128)(2,1)S(1)}, u32[]{:S(2)}, u32[]{:S(2)}) collective-permute-start(bf16[16,80,128]{2,1,0:T(8,128)(2,1)S(1)} %broadcast_select_fusion), channel_id=1, source_target_pairs={{0,1},{1,0},{2,3},{3,2},{4,5},{5,4},{6,7},{7,6},{8,9},{9,8},{10,11... | collective-permute-start | bytes 983048 | tf_op jit(solution)/shard_map/ppermute | solution.py:169
  34.1 0.2 slice_negate_fusion
  34.3 0.0 copy-done.2
  34.3 1.0 %maximum_maximum_fusion.refs_2_ = bf16[32,80,128]{2,1,0:T(8,128)(2,1)} fusion(bf16[32,40,64]{2,1,0:T(8,128)(2,1)S(1)} %get-tuple-element.6, bf16[32,40,64]{2,1,0:T(8,128)(2,1)S(1)} %get-tuple-element.5, bf16[32,40,128]{2,1,0:T(8,128)(2,1)S(1)} %reshape.16), kind=kLoop, calls=%fused_computation | loop fusion | flops 1966080 | bytes 1310720 | tf_op jit(solution)/shard_map/concatenate | solution.py:175
  35.3 0.0 copy-done
  35.3 0.0 copy-done.1
  35.3 2.5 %collective-permute-done.refs_3_ = bf16[16,80,128]{2,1,0:T(8,128)(2,1)S(1)} collective-permute-done((bf16[16,80,128]{2,1,0:T(8,128)(2,1)S(1)}, bf16[16,80,128]{2,1,0:T(8,128)(2,1)S(1)}, u32[]{:S(2)}, u32[]{:S(2)}) %collective-permute-start) | collective-permute-done | bytes 327712 | tf_op jit(solution)/shard_map/ppermute | solution.py:165
  37.8 0.0 copy-start.3
  37.8 0.0 collective-permute-done.3.refs_4_
  37.8 0.0 copy-start.4
  37.8 0.7 %copy-done.3 = bf16[16,80,128]{2,1,0:T(8,128)(2,1)} copy-done((bf16[16,80,128]{2,1,0:T(8,128)(2,1)}, bf16[16,80,128]{2,1,0:T(8,128)(2,1)S(1)}, u32[]{:S(2)}) %copy-start.3) | copy-done | bytes 327704
  38.6 0.1 copy-done.4
  38.7 6.4 %shard_map.74 = f32[5,40,2560]{2,1,0:T(8,128)} custom-call(s32[5]{0:T(128)} %bitcast.18, s32[1]{0:T(128)S(6)} %copy.17.refs_1_, bf16[32,80,128]{2,1,0:T(8,128)(2,1)} %maximum_maximum_fusion.refs_2_, bf16[16,80,128]{2,1,0:T(8,128)(2,1)} %copy-done.3, bf16[16,80,128]{2,1,0:T(8,128)(2,1)} %copy-done.4, bf16[16,80,128]{2,1,0:T(8,128)(2,1)} %copy-done.1, ...), custom_call_target="tpu_custom_call" | custom-call | tf_op jit(solution)/shard_map/pallas_call | solution.py:139
  (1 shorter events, 0.0 us)
Async XLA Ops:
  24.5 9.8 %copy-start.2 = (bf16[16,80,128]{2,1,0:T(8,128)(2,1)}, bf16[16,80,128]{2,1,0:T(8,128)(2,1)S(1)}, u32[]{:S(2)}) copy-start(bf16[16,80,128]{2,1,0:T(8,128)(2,1)S(1)} %reshape_reshape.3.refs_6_) | copy-start | bytes 983044
  24.5 8.8 %collective-permute-start.2 = (bf16[16,80,128]{2,1,0:T(8,128)(2,1)S(1)}, bf16[16,80,128]{2,1,0:T(8,128)(2,1)S(1)}, u32[]{:S(2)}, u32[]{:S(2)}) collective-permute-start(bf16[16,80,128]{2,1,0:T(8,128)(2,1)S(1)} %reshape_reshape.3.refs_6_), channel_id=1, source_target_pairs={{1,0},{2,1},{3,2},{4,3},{5,4},{6,5},{7,6},{9,8},{10,9},{11,10},{12... | collective-permute-start | bytes 983048 | tf_op jit(solution)/shard_map/ppermute | solution.py:19
  25.8 7.5 %collective-permute-start.1 = (bf16[16,80,128]{2,1,0:T(8,128)(2,1)S(1)}, bf16[16,80,128]{2,1,0:T(8,128)(2,1)S(1)}, u32[]{:S(2)}, u32[]{:S(2)}) collective-permute-start(bf16[16,80,128]{2,1,0:T(8,128)(2,1)S(1)} %reshape_reshape.3.refs_6_), channel_id=1, source_target_pairs={{0,1},{1,2},{2,3},{3,4},{4,5},{5,6},{6,7},{8,9},{9,10},{10,11},{11... | collective-permute-start | bytes 983048 | tf_op jit(solution)/shard_map/ppermute | solution.py:19
  29.8 8.0 %collective-permute-start = (bf16[16,80,128]{2,1,0:T(8,128)(2,1)S(1)}, bf16[16,80,128]{2,1,0:T(8,128)(2,1)S(1)}, u32[]{:S(2)}, u32[]{:S(2)}) collective-permute-start(bf16[16,80,128]{2,1,0:T(8,128)(2,1)S(1)} %reshape_reshape.3.refs_6_), channel_id=1, source_target_pairs={{0,2},{2,4},{3,1},{4,6},{5,3},{7,5},{8,10},{10,12},{11,9},{12,14},... | collective-permute-start | bytes 983048 | tf_op jit(solution)/shard_map/ppermute | solution.py:165
  33.3 2.0 %copy-start = (bf16[16,80,128]{2,1,0:T(8,128)(2,1)}, bf16[16,80,128]{2,1,0:T(8,128)(2,1)S(1)}, u32[]{:S(2)}) copy-start(bf16[16,80,128]{2,1,0:T(8,128)(2,1)S(1)} %collective-permute-done.2.refs_7_) | copy-start | bytes 983044
  33.3 2.0 %copy-start.1 = (bf16[16,80,128]{2,1,0:T(8,128)(2,1)}, bf16[16,80,128]{2,1,0:T(8,128)(2,1)S(1)}, u32[]{:S(2)}) copy-start(bf16[16,80,128]{2,1,0:T(8,128)(2,1)S(1)} %collective-permute-done.1.refs_5_) | copy-start | bytes 983044
  33.4 4.5 %collective-permute-start.3 = (bf16[16,80,128]{2,1,0:T(8,128)(2,1)S(1)}, bf16[16,80,128]{2,1,0:T(8,128)(2,1)S(1)}, u32[]{:S(2)}, u32[]{:S(2)}) collective-permute-start(bf16[16,80,128]{2,1,0:T(8,128)(2,1)S(1)} %broadcast_select_fusion), channel_id=1, source_target_pairs={{0,1},{1,0},{2,3},{3,2},{4,5},{5,4},{6,7},{7,6},{8,9},{9,8},{10,11... | collective-permute-start | bytes 983048 | tf_op jit(solution)/shard_map/ppermute | solution.py:169
  37.8 0.7 %copy-start.3 = (bf16[16,80,128]{2,1,0:T(8,128)(2,1)}, bf16[16,80,128]{2,1,0:T(8,128)(2,1)S(1)}, u32[]{:S(2)}) copy-start(bf16[16,80,128]{2,1,0:T(8,128)(2,1)S(1)} %collective-permute-done.refs_3_) | copy-start | bytes 983044
  37.8 0.8 %copy-start.4 = (bf16[16,80,128]{2,1,0:T(8,128)(2,1)}, bf16[16,80,128]{2,1,0:T(8,128)(2,1)S(1)}, u32[]{:S(2)}) copy-start(bf16[16,80,128]{2,1,0:T(8,128)(2,1)S(1)} %collective-permute-done.3.refs_4_) | copy-start | bytes 983044

commit v14 on v13

--- a/solution.py
+++ b/solution.py
@@ -154,7 +154,7 @@
     nb = width // 2
     spec = (
         regrouped.reshape(stations, windows, 2, nb)
-        .transpose(3, 0, 2, 1)
+        .transpose(3, 0, 1, 2)
         .reshape(nb, stations, 2 * windows)
     )
     paired = spec.reshape(nb // 2, 2 * stations, 2 * windows)
@@ -170,9 +170,11 @@
         relay, "sta", [(i, i + 1 - 2 * (i % 2)) for i in range(peers) if 0 <= i + 1 - 2 * (i % 2) < peers]
     )
     ys = [far, forwarded, left1, paired, right1]
-    x_re = spec[:, :, :windows]
-    x_im = spec[:, :, windows:]
-    lx = jnp.concatenate([spec, jnp.concatenate([-x_im, x_re], axis=2)], axis=1)
+    pairs_view = spec.reshape(nb, stations, windows, 2)
+    x_re = pairs_view[..., 0]
+    x_im = pairs_view[..., 1]
+    swapped = jnp.stack([-x_im, x_re], axis=3).reshape(nb, stations, 2 * windows)
+    lx = jnp.concatenate([spec, swapped], axis=1)
     result = cross_block(partner_row, counts, lx, ys, windows, slots)
     return result[None]
 

time: 45.9 us -> 45.1 us (0.983); the launches traced: 45.1 us -> 44.7 us
  waiting for transfers between devices: 2.51 us -> 0.01 us
  local copies, waits for them, and re-layouts: 5.92 us -> 7.07 us
  other arithmetic: 1.23 us -> 2.1 us
    ppermute x1, waiting for transfers between devices: 2.5 us -> 0.01 us  [body(): lax.ppermute(paired, 'sta', [(i, i + 2 - 4 * (i % 2)) for i in range(peer...]
    reshape x1 -> x2, local copies, waits for them, and re-layouts: 0.28 us -> 2.18 us  [the longest x1 1.09 us: body(): spec = regrouped.reshape(stations, windows, 2, nb).transpose(3, 0, 1, 2)....]
    transpose x1 -> x0, local copies, waits for them, and re-layouts: 1.31 us -> none  [body(): spec = regrouped.reshape(stations, windows, 2, nb).transpose(3, 0, 2, 1)....]
    select_n x1, other arithmetic: 0.04 us -> 0.89 us  [body(): relay = jnp.where(parity == 0, left1, right1)]
    another operation x1 -> x2, local copies, waits for them, and re-layouts: 0.28 us -> 0.96 us  [body(): paired = spec.reshape(nb // 2, 2 * stations, 2 * windows)]
    unnamed x12 -> x10, local copies, waits for them, and re-layouts: 1.75 us -> 1.62 us
  transfers between devices with their start and end apart: 4 -> 4, of which waited for: 1 -> 0; matrix products, arithmetic and copies ran while one was open for 3% -> 10% of each run, Pallas kernels for 0% -> 0%
where the time goes in v14:
time: 45.1 us; the launch traced here: 44.7 us
  Pallas kernels  14.5 us (32%)
  blocking collectives  11.6 us (26%)
  starting transfers between devices  8.73 us (19%)
  local copies, waits for them, and re-layouts  7.07 us (16%)
  other arithmetic  2.1 us (5%)
  between operations  0.82 us (2%)
    all_to_all x1, blocking collectives, body(): lax.all_to_all(own_spec, 'tm', split_axis=3, concat_axis=2, tiled=True)  11.6 us
    pallas_call x1, Pallas kernels, whiten(): pl.pallas_call(dft_kernel, grid=(samples // (fine * coarse_step),), in_sp...  8.07 us
    pallas_call x1, Pallas kernels, cross_block(): pl.pallas_call(kernel, grid_spec=grid_spec, out_shape=jax.ShapeDtypeStruc...  6.39 us
    ppermute x2, starting transfers between devices, passed_along(): return lax.ppermute(array, axis, pairs)  4.34 us
    ppermute x1, starting transfers between devices, body(): lax.ppermute(paired, 'sta', [(i, i + 2 - 4 * (i % 2)) for i in range(peer...  3.49 us
    unnamed x10, local copies, waits for them, and re-layouts  1.62 us
    reshape x2, local copies, waits for them, and re-layouts, whiten(): return white.reshape(1, stations, windows, groups, width // groups)  1.4 us
    reshape x1, local copies, waits for them, and re-layouts, body(): spec = regrouped.reshape(stations, windows, 2, nb).transpose(3, 0, 1, 2)....  1.09 us
  transfers between devices with their start and end apart: 4, of which 0 were waited for; matrix products, arithmetic and copies ran while one was open for 10% of the time, Pallas kernels for 0%

profile of v14, /device:TPU:0, one launch (start us, length us, event | category | flops | bytes accessed | tf_op | source)
XLA Modules:
  0.0 44.7 jit_solution(1397235373280610821)
XLA Ops:
  0.0 8.1 %shard_map.73 = bf16[640,256]{1,0:T(8,128)(2,1)} custom-call(f32[64,256]{1,0:T(8,128)} %constant.26.clone.p1_ref, f32[64,256]{1,0:T(8,128)} %constant.27.clone.q1_ref, f32[64,256]{1,0:T(8,128)} %constant.28.clone.c2_ref, f32[64,256]{1,0:T(8,128)} %constant.29.clone.s2_ref, f32[640,4096]{1,0:T(8,128)} %bitcast.25), custom_call_target="tpu_custom_call" | custom-call | tf_op jit(solution)/shard_map/pallas_call | solution.py:76
  8.1 1.3 %reshape.17 = bf16[1,40,16,4,64]{4,3,2,1,0:T(4,128)(2,1)S(1)} reshape(bf16[640,256]{1,0:T(8,128)(2,1)} %shard_map.73) | data formatting | bytes 655360 | tf_op jit(solution)/shard_map/reshape | solution.py:90
  9.4 0.1 copy.24
  9.5 0.5 %reshape.21 = bf16[4,2,20480]{2,1,0:T(2,128)(2,1)S(1)} reshape(bf16[4,1,40,16,64]{4,3,2,1,0:T(8,128)(2,1)S(1)} %bitcast.27) | data formatting | bytes 655360
  10.0 11.6 %all_to_all.15 = bf16[4,2,20480]{2,1,0:T(2,128)(2,1)S(1)} all-to-all(bf16[4,2,20480]{2,1,0:T(2,128)(2,1)S(1)} %reshape.21), channel_id=1, replica_groups=mesh['tm'=4,'sta'=8] {'tm'}, dimensions={0} | all-to-all | bytes 655360 | tf_op jit(solution)/shard_map/all_to_all | solution.py:152
  21.5 0.4 reshape.22
  22.0 0.1 bitcast_bitcast_fusion
  22.1 0.8 %copy.16 = bf16[1,40,4,16,1,64]{1,5,3,2,4,0:T(8,128)(2,1)S(1)} copy(bf16[1,40,4,16,1,64]{5,3,1,2,4,0:T(8,128)(2,1)S(1)} %bitcast_bitcast_fusion) | data formatting | bytes 655360 | tf_op jit(solution)/shard_map/all_to_all | solution.py:152
  22.9 0.5 %reshape_reshape.3 = bf16[16,80,128]{1,0,2:T(8,128)(2,1)S(1)} reshape(bf16[32,40,64,2]{1,0,3,2:T(8,128)(2,1)S(1)} %bitcast.22) | data formatting | bytes 655360 | tf_op jit(solution)/shard_map/reshape;reshape | solution.py:160
  23.4 0.5 %copy.19.refs_6_ = bf16[16,80,128]{2,1,0:T(8,128)(2,1)S(1)} copy(bf16[16,80,128]{1,0,2:T(8,128)(2,1)S(1)} %reshape_reshape.3) | data formatting | bytes 655360 | tf_op jit(solution)/shard_map/reshape;reshape | solution.py:160
  23.8 0.0 copy-start.2
  23.8 1.3 %collective-permute-start.2 = (bf16[16,80,128]{2,1,0:T(8,128)(2,1)S(1)}, bf16[16,80,128]{2,1,0:T(8,128)(2,1)S(1)}, u32[]{:S(2)}, u32[]{:S(2)}) collective-permute-start(bf16[16,80,128]{2,1,0:T(8,128)(2,1)S(1)} %copy.19.refs_6_), channel_id=1, source_target_pairs={{1,0},{2,1},{3,2},{4,3},{5,4},{6,5},{7,6},{9,8},{10,9},{11,10},{12... | collective-permute-start | bytes 983048 | tf_op jit(solution)/shard_map/ppermute | solution.py:19
  25.1 3.1 %collective-permute-start.1 = (bf16[16,80,128]{2,1,0:T(8,128)(2,1)S(1)}, bf16[16,80,128]{2,1,0:T(8,128)(2,1)S(1)}, u32[]{:S(2)}, u32[]{:S(2)}) collective-permute-start(bf16[16,80,128]{2,1,0:T(8,128)(2,1)S(1)} %copy.19.refs_6_), channel_id=1, source_target_pairs={{0,1},{1,2},{2,3},{3,4},{4,5},{5,6},{6,7},{8,9},{9,10},{10,11},{11... | collective-permute-start | bytes 983048 | tf_op jit(solution)/shard_map/ppermute | solution.py:19
  28.9 3.5 %collective-permute-start = (bf16[16,80,128]{2,1,0:T(8,128)(2,1)S(1)}, bf16[16,80,128]{2,1,0:T(8,128)(2,1)S(1)}, u32[]{:S(2)}, u32[]{:S(2)}) collective-permute-start(bf16[16,80,128]{2,1,0:T(8,128)(2,1)S(1)} %copy.19.refs_6_), channel_id=1, source_target_pairs={{0,2},{2,4},{3,1},{4,6},{5,3},{7,5},{8,10},{10,12},{11,9},{12,14},... | collective-permute-start | bytes 983048 | tf_op jit(solution)/shard_map/ppermute | solution.py:165
  32.4 0.0 collective-permute-done.2.refs_7_
  32.4 0.0 copy-start
  32.4 0.0 collective-permute-done.1.refs_5_
  32.4 0.0 copy-start.1
  32.4 0.9 %broadcast_select_fusion = bf16[16,80,128]{2,1,0:T(8,128)(2,1)} fusion(bf16[16,80,128]{2,1,0:T(8,128)(2,1)S(1)} %collective-permute-done.1.refs_5_, bf16[16,80,128]{2,1,0:T(8,128)(2,1)S(1)} %collective-permute-done.2.refs_7_, pred[]{:T(512)S(6)} %eq.5), kind=kLoop, calls=%fused_computation.3 | loop fusion | flops 163840 | bytes 983041 | tf_op jit(solution)/shard_map/jit(_where)/select_n | solution.py:168
  33.3 0.9 %collective-permute-start.3 = (bf16[16,80,128]{2,1,0:T(8,128)(2,1)}, bf16[16,80,128]{2,1,0:T(8,128)(2,1)}, u32[]{:S(2)}, u32[]{:S(2)}) collective-permute-start(bf16[16,80,128]{2,1,0:T(8,128)(2,1)} %broadcast_select_fusion), channel_id=1, source_target_pairs={{0,1},{1,0},{2,3},{3,2},{4,5},{5,4},{6,7},{7,6},{8,9},{9,8},{10,11... | collective-permute-start | bytes 983048 | tf_op jit(solution)/shard_map/ppermute | solution.py:169
  34.2 0.1 slice_negate_fusion
  34.3 0.0 copy-done.2
  34.3 0.0 copy-done
  34.3 0.0 copy-done.1
  34.3 1.1 %copy.17 = bf16[32,40,128]{2,1,0:T(8,128)(2,1)S(1)} copy(bf16[32,40,128]{1,0,2:T(8,128)(2,1)S(1)} %bitcast.24) | data formatting | bytes 655360 | tf_op jit(solution)/shard_map/reshape | solution.py:158
  35.4 0.2 pad_maximum_fusion
  35.6 1.1 %copy.18 = bf16[32,40,128]{2,1,0:T(8,128)(2,1)S(1)} copy(bf16[32,40,128]{1,0,2:T(8,128)(2,1)S(1)} %bitcast.26) | data formatting | bytes 655360 | tf_op jit(solution)/shard_map/reshape | solution.py:176
  36.7 0.9 %pad_maximum_fusion.1.refs_2_ = bf16[32,80,128]{2,1,0:T(8,128)(2,1)} fusion(bf16[32,40,128]{2,1,0:T(8,128)(2,1)S(1)} %copy.18, bf16[32,40,128]{2,1,0:T(8,128)(2,1)S(1)} %copy.17), kind=kLoop, calls=%fused_computation.1 | loop fusion | flops 1310720 | bytes 1310720 | tf_op jit(solution)/shard_map/concatenate | solution.py:177
  37.6 0.0 collective-permute-done.refs_3_
  37.6 0.0 collective-permute-done.3.refs_4_
  37.6 0.7 %copy-done.3 = bf16[16,80,128]{2,1,0:T(8,128)(2,1)} copy-done((bf16[16,80,128]{2,1,0:T(8,128)(2,1)}, bf16[16,80,128]{2,1,0:T(8,128)(2,1)S(1)}, u32[]{:S(2)}) %copy-start.3) | copy-done | bytes 327704
  38.4 6.4 %shard_map.74 = f32[5,40,2560]{2,1,0:T(8,128)} custom-call(s32[5]{0:T(128)} %bitcast.28, s32[1]{0:T(128)S(6)} %copy.25.refs_1_, bf16[32,80,128]{2,1,0:T(8,128)(2,1)} %pad_maximum_fusion.1.refs_2_, bf16[16,80,128]{2,1,0:T(8,128)(2,1)} %copy-done.3, bf16[16,80,128]{2,1,0:T(8,128)(2,1)} %collective-permute-done.3.refs_4_, bf16[16,80,128]{2,1,0:T(8,128)(2,1)} %copy-done.1, ...), custom_call_target="tpu_custom_call" | custom-call | tf_op jit(solution)/shard_map/pallas_call | solution.py:139
  (1 shorter events, 0.0 us)
Async XLA Ops:
  23.8 10.5 %copy-start.2 = (bf16[16,80,128]{2,1,0:T(8,128)(2,1)}, bf16[16,80,128]{2,1,0:T(8,128)(2,1)S(1)}, u32[]{:S(2)}) copy-start(bf16[16,80,128]{2,1,0:T(8,128)(2,1)S(1)} %copy.19.refs_6_) | copy-start | bytes 983044
  23.8 8.5 %collective-permute-start.2 = (bf16[16,80,128]{2,1,0:T(8,128)(2,1)S(1)}, bf16[16,80,128]{2,1,0:T(8,128)(2,1)S(1)}, u32[]{:S(2)}, u32[]{:S(2)}) collective-permute-start(bf16[16,80,128]{2,1,0:T(8,128)(2,1)S(1)} %copy.19.refs_6_), channel_id=1, source_target_pairs={{1,0},{2,1},{3,2},{4,3},{5,4},{6,5},{7,6},{9,8},{10,9},{11,10},{12... | collective-permute-start | bytes 983048 | tf_op jit(solution)/shard_map/ppermute | solution.py:19
  25.1 7.2 %collective-permute-start.1 = (bf16[16,80,128]{2,1,0:T(8,128)(2,1)S(1)}, bf16[16,80,128]{2,1,0:T(8,128)(2,1)S(1)}, u32[]{:S(2)}, u32[]{:S(2)}) collective-permute-start(bf16[16,80,128]{2,1,0:T(8,128)(2,1)S(1)} %copy.19.refs_6_), channel_id=1, source_target_pairs={{0,1},{1,2},{2,3},{3,4},{4,5},{5,6},{6,7},{8,9},{9,10},{10,11},{11... | collective-permute-start | bytes 983048 | tf_op jit(solution)/shard_map/ppermute | solution.py:19
  28.9 8.8 %collective-permute-start = (bf16[16,80,128]{2,1,0:T(8,128)(2,1)S(1)}, bf16[16,80,128]{2,1,0:T(8,128)(2,1)S(1)}, u32[]{:S(2)}, u32[]{:S(2)}) collective-permute-start(bf16[16,80,128]{2,1,0:T(8,128)(2,1)S(1)} %copy.19.refs_6_), channel_id=1, source_target_pairs={{0,2},{2,4},{3,1},{4,6},{5,3},{7,5},{8,10},{10,12},{11,9},{12,14},... | collective-permute-start | bytes 983048 | tf_op jit(solution)/shard_map/ppermute | solution.py:165
  32.4 1.9 %copy-start = (bf16[16,80,128]{2,1,0:T(8,128)(2,1)}, bf16[16,80,128]{2,1,0:T(8,128)(2,1)S(1)}, u32[]{:S(2)}) copy-start(bf16[16,80,128]{2,1,0:T(8,128)(2,1)S(1)} %collective-permute-done.2.refs_7_) | copy-start | bytes 983044
  32.4 1.9 %copy-start.1 = (bf16[16,80,128]{2,1,0:T(8,128)(2,1)}, bf16[16,80,128]{2,1,0:T(8,128)(2,1)S(1)}, u32[]{:S(2)}) copy-start(bf16[16,80,128]{2,1,0:T(8,128)(2,1)S(1)} %collective-permute-done.1.refs_5_) | copy-start | bytes 983044
  33.3 4.3 %collective-permute-start.3 = (bf16[16,80,128]{2,1,0:T(8,128)(2,1)}, bf16[16,80,128]{2,1,0:T(8,128)(2,1)}, u32[]{:S(2)}, u32[]{:S(2)}) collective-permute-start(bf16[16,80,128]{2,1,0:T(8,128)(2,1)} %broadcast_select_fusion), channel_id=1, source_target_pairs={{0,1},{1,0},{2,3},{3,2},{4,5},{5,4},{6,7},{7,6},{8,9},{9,8},{10,11... | collective-permute-start | bytes 983048 | tf_op jit(solution)/shard_map/ppermute | solution.py:169
  37.6 0.7 %copy-start.3 = (bf16[16,80,128]{2,1,0:T(8,128)(2,1)}, bf16[16,80,128]{2,1,0:T(8,128)(2,1)S(1)}, u32[]{:S(2)}) copy-start(bf16[16,80,128]{2,1,0:T(8,128)(2,1)S(1)} %collective-permute-done.refs_3_) | copy-start | bytes 983044

commit v15 on v14

--- a/solution.py
+++ b/solution.py
@@ -103,25 +103,22 @@
         slot = jnp.where(where_at == 0, parity, where_at + 1)
         slot = jnp.where(where_at == 2 * R, 1 - parity, slot)
         sel.append(jnp.where(p < count_ref[0], slot, -1))
-    for j in range(bins // 2):
+    for b in range(bins):
         picked = []
         for p in range(slots):
             y = jnp.zeros(y_refs[0].shape[1:], y_refs[0].dtype)
             for o, y_ref in enumerate(y_refs):
-                y = jnp.where(sel[p] == o, y_ref[j], y)
-            picked.append(y)
-        ycat = jnp.concatenate(picked, axis=0)
-        for h in range(2):
-            b = 2 * j + h
-            r = lax.dot_general(
-                lx_ref[b], ycat, (((1,), (1,)), ((), ())), preferred_element_type=jnp.float32
-            )
-            r = r * scale
-            for p in range(slots):
-                src = (2 * p + h) * s
-                for x in range(2):
-                    col = (2 * b + x) * s
-                    o_ref[p, :, col:col + s] = r[x * s:(x + 1) * s, src:src + s]
+                y = jnp.where(sel[p] == o, y_ref[b], y)
+            picked.append(y.astype(jnp.float32))
+        ycat = jnp.concatenate(picked, axis=0).astype(lx_ref.dtype)
+        r = lax.dot_general(
+            lx_ref[b], ycat, (((1,), (1,)), ((), ())), preferred_element_type=jnp.float32
+        )
+        r = r * scale
+        for p in range(slots):
+            for x in range(2):
+                col = (2 * b + x) * s
+                o_ref[p, :, col:col + s] = r[x * s:(x + 1) * s, p * s:(p + 1) * s]
 
 
 def cross_block(partner_row, count, lx, ys, windows, slots):
@@ -129,7 +126,7 @@
     s = two_s // 2
     step = BINS_PER_STEP
     kernel = lambda *refs: cross_kernel(1.0 / windows, *refs)
-    y_spec = pl.BlockSpec((step // 2, two_s, k), lambda g, *_: (g, 0, 0))
+    y_spec = pl.BlockSpec((step, s, k), lambda g, *_: (g, 0, 0))
     grid_spec = pltpu.PrefetchScalarGridSpec(
         num_scalar_prefetch=2,
         grid=(nb // step,),
@@ -157,7 +154,7 @@
         .transpose(3, 0, 1, 2)
         .reshape(nb, stations, 2 * windows)
     )
-    paired = spec.reshape(nb // 2, 2 * stations, 2 * windows)
+    paired = spec
     peers = lax.axis_size("sta")
     parity = block_index % 2
     left1 = passed_along(paired, "sta", 1)

time: 45.1 us -> 44.9 us (level)
  waiting for transfers between devices: 0.01 us -> 1.09 us
  other arithmetic: 2.1 us -> 1.24 us
  local copies, waits for them, and re-layouts: 7.07 us -> 6.23 us
    ppermute x1, waiting for transfers between devices: 0.01 us -> 1.09 us  [body(): lax.ppermute(paired, 'sta', [(i, i + 2 - 4 * (i % 2)) for i in range(peer...]
    another operation x2 -> x0, local copies, waits for them, and re-layouts: 0.96 us -> none  [body(): paired = spec.reshape(nb // 2, 2 * stations, 2 * windows)]
    select_n x1, other arithmetic: 0.89 us -> 0.04 us  [body(): relay = jnp.where(parity == 0, left1, right1)]
    unnamed x10 -> x12, local copies, waits for them, and re-layouts: 1.62 us -> 1.75 us
  transfers between devices with their start and end apart: 4 -> 4, of which waited for: 0 -> 1; matrix products, arithmetic and copies ran while one was open for 10% -> 5% of each run, Pallas kernels for 0% -> 0%
where the time goes in v15:
time: 44.9 us; the launch traced here: 44.1 us
  Pallas kernels  14.3 us (32%)
  blocking collectives  11.6 us (26%)
  starting transfers between devices  8.87 us (20%)
  local copies, waits for them, and re-layouts  6.23 us (14%)
  other arithmetic  1.24 us (3%)
  waiting for transfers between devices  1.09 us (2%)
  between operations  0.82 us (2%)
    all_to_all x1, blocking collectives, body(): lax.all_to_all(own_spec, 'tm', split_axis=3, concat_axis=2, tiled=True)  11.6 us
    pallas_call x1, Pallas kernels, whiten(): pl.pallas_call(dft_kernel, grid=(samples // (fine * coarse_step),), in_sp...  8.07 us
    pallas_call x1, Pallas kernels, cross_block(): pl.pallas_call(kernel, grid_spec=grid_spec, out_shape=jax.ShapeDtypeStruc...  6.23 us
    ppermute x2, starting transfers between devices, passed_along(): return lax.ppermute(array, axis, pairs)  4.34 us
    ppermute x1, starting transfers between devices, body(): lax.ppermute(paired, 'sta', [(i, i + 2 - 4 * (i % 2)) for i in range(peer...  3.49 us
    unnamed x12, local copies, waits for them, and re-layouts  1.75 us
    reshape x2, local copies, waits for them, and re-layouts, whiten(): return white.reshape(1, stations, windows, groups, width // groups)  1.4 us
    reshape x1, local copies, waits for them, and re-layouts, body(): spec = regrouped.reshape(stations, windows, 2, nb).transpose(3, 0, 1, 2)....  1.09 us
  transfers between devices with their start and end apart: 4, of which 1 were waited for; matrix products, arithmetic and copies ran while one was open for 5% of the time, Pallas kernels for 0%

profile of v15, /device:TPU:0, one launch (start us, length us, event | category | flops | bytes accessed | tf_op | source)
XLA Modules:
  0.0 44.1 jit_solution(10726767028631895707)
XLA Ops:
  0.0 8.1 %shard_map.73 = bf16[640,256]{1,0:T(8,128)(2,1)} custom-call(f32[64,256]{1,0:T(8,128)} %constant.26.clone.p1_ref, f32[64,256]{1,0:T(8,128)} %constant.27.clone.q1_ref, f32[64,256]{1,0:T(8,128)} %constant.28.clone.c2_ref, f32[64,256]{1,0:T(8,128)} %constant.29.clone.s2_ref, f32[640,4096]{1,0:T(8,128)} %bitcast.18), custom_call_target="tpu_custom_call" | custom-call | tf_op jit(solution)/shard_map/pallas_call | solution.py:76
  8.1 1.3 %reshape.17 = bf16[1,40,16,4,64]{4,3,2,1,0:T(4,128)(2,1)S(1)} reshape(bf16[640,256]{1,0:T(8,128)(2,1)} %shard_map.73) | data formatting | bytes 655360 | tf_op jit(solution)/shard_map/reshape | solution.py:90
  9.4 0.1 copy.24
  9.5 0.5 %reshape.21 = bf16[4,2,20480]{2,1,0:T(2,128)(2,1)S(1)} reshape(bf16[4,1,40,16,64]{4,3,2,1,0:T(8,128)(2,1)S(1)} %bitcast.22) | data formatting | bytes 655360
  10.0 11.6 %all_to_all.15 = bf16[4,2,20480]{2,1,0:T(2,128)(2,1)S(1)} all-to-all(bf16[4,2,20480]{2,1,0:T(2,128)(2,1)S(1)} %reshape.21), channel_id=1, replica_groups=mesh['tm'=4,'sta'=8] {'tm'}, dimensions={0} | all-to-all | bytes 655360 | tf_op jit(solution)/shard_map/all_to_all | solution.py:149
  21.5 0.4 reshape.22
  22.0 0.1 bitcast_bitcast_fusion
  22.1 0.8 %copy.16 = bf16[1,40,4,16,1,64]{1,5,3,2,4,0:T(8,128)(2,1)S(1)} copy(bf16[1,40,4,16,1,64]{5,3,1,2,4,0:T(8,128)(2,1)S(1)} %bitcast_bitcast_fusion) | data formatting | bytes 655360 | tf_op jit(solution)/shard_map/all_to_all | solution.py:149
  22.9 1.1 %copy.17.refs_6_ = bf16[32,40,128]{2,1,0:T(8,128)(2,1)S(1)} copy(bf16[32,40,128]{1,0,2:T(8,128)(2,1)S(1)} %bitcast.19) | data formatting | bytes 655360 | tf_op jit(solution)/shard_map/reshape | solution.py:155
  24.0 0.0 copy-start
  24.0 1.3 %collective-permute-start.2 = (bf16[32,40,128]{2,1,0:T(8,128)(2,1)S(1)}, bf16[32,40,128]{2,1,0:T(8,128)(2,1)S(1)}, u32[]{:S(2)}, u32[]{:S(2)}) collective-permute-start(bf16[32,40,128]{2,1,0:T(8,128)(2,1)S(1)} %copy.17.refs_6_), channel_id=1, source_target_pairs={{1,0},{2,1},{3,2},{4,3},{5,4},{6,5},{7,6},{9,8},{10,9},{11,10},{12... | collective-permute-start | bytes 983048 | tf_op jit(solution)/shard_map/ppermute | solution.py:19
  25.3 3.1 %collective-permute-start.1 = (bf16[32,40,128]{2,1,0:T(8,128)(2,1)S(1)}, bf16[32,40,128]{2,1,0:T(8,128)(2,1)S(1)}, u32[]{:S(2)}, u32[]{:S(2)}) collective-permute-start(bf16[32,40,128]{2,1,0:T(8,128)(2,1)S(1)} %copy.17.refs_6_), channel_id=1, source_target_pairs={{0,1},{1,2},{2,3},{3,4},{4,5},{5,6},{6,7},{8,9},{9,10},{10,11},{11... | collective-permute-start | bytes 983048 | tf_op jit(solution)/shard_map/ppermute | solution.py:19
  29.0 3.5 %collective-permute-start = (bf16[32,40,128]{2,1,0:T(8,128)(2,1)S(1)}, bf16[32,40,128]{2,1,0:T(8,128)(2,1)S(1)}, u32[]{:S(2)}, u32[]{:S(2)}) collective-permute-start(bf16[32,40,128]{2,1,0:T(8,128)(2,1)S(1)} %copy.17.refs_6_), channel_id=1, source_target_pairs={{0,2},{2,4},{3,1},{4,6},{5,3},{7,5},{8,10},{10,12},{11,9},{12,14},... | collective-permute-start | bytes 983048 | tf_op jit(solution)/shard_map/ppermute | solution.py:162
  32.5 0.0 collective-permute-done.2.refs_7_
  32.5 0.0 copy-start.1
  32.5 0.0 collective-permute-done.1.refs_5_
  32.5 0.0 copy-start.2
  32.6 1.0 %collective-permute-start.3 = (bf16[32,40,128]{2,1,0:T(8,128)(2,1)S(1)}, bf16[32,40,128]{2,1,0:T(8,128)(2,1)S(1)}, u32[]{:S(2)}, u32[]{:S(2)}) collective-permute-start(bf16[32,40,128]{2,1,0:T(8,128)(2,1)S(1)} %broadcast_select_fusion), channel_id=1, source_target_pairs={{0,1},{1,0},{2,3},{3,2},{4,5},{5,4},{6,7},{7,6},{8,9},{9,8},{10,11... | collective-permute-start | bytes 983048 | tf_op jit(solution)/shard_map/ppermute | solution.py:166
  33.6 0.1 slice_negate_fusion
  33.7 0.0 copy-done.1
  33.7 0.0 copy-done.2
  33.7 0.2 pad_maximum_fusion
  34.0 1.1 %copy.18 = bf16[32,40,128]{2,1,0:T(8,128)(2,1)S(1)} copy(bf16[32,40,128]{1,0,2:T(8,128)(2,1)S(1)} %bitcast.21) | data formatting | bytes 655360 | tf_op jit(solution)/shard_map/reshape | solution.py:173
  35.1 0.0 copy-done
  35.1 0.9 %pad_maximum_fusion.1.refs_2_ = bf16[32,80,128]{2,1,0:T(8,128)(2,1)} fusion(bf16[32,40,128]{2,1,0:T(8,128)(2,1)S(1)} %copy.18, bf16[32,40,128]{2,1,0:T(8,128)(2,1)S(1)} %copy.17.refs_6_), kind=kLoop, calls=%fused_computation.1 | loop fusion | flops 1310720 | bytes 1310720 | tf_op jit(solution)/shard_map/concatenate | solution.py:174
  36.0 1.1 %collective-permute-done.refs_3_ = bf16[32,40,128]{2,1,0:T(8,128)(2,1)S(1)} collective-permute-done((bf16[32,40,128]{2,1,0:T(8,128)(2,1)S(1)}, bf16[32,40,128]{2,1,0:T(8,128)(2,1)S(1)}, u32[]{:S(2)}, u32[]{:S(2)}) %collective-permute-start) | collective-permute-done | bytes 327712 | tf_op jit(solution)/shard_map/ppermute | solution.py:162
  37.0 0.0 copy-start.3
  37.0 0.0 collective-permute-done.3.refs_4_
  37.0 0.0 copy-start.4
  37.0 0.7 %copy-done.3 = bf16[32,40,128]{2,1,0:T(8,128)(2,1)} copy-done((bf16[32,40,128]{2,1,0:T(8,128)(2,1)}, bf16[32,40,128]{2,1,0:T(8,128)(2,1)S(1)}, u32[]{:S(2)}) %copy-start.3) | copy-done | bytes 327704
  37.8 0.1 copy-done.4
  37.9 6.2 %shard_map.74 = f32[5,40,2560]{2,1,0:T(8,128)} custom-call(s32[5]{0:T(128)} %bitcast.23, s32[1]{0:T(128)S(6)} %copy.25.refs_1_, bf16[32,80,128]{2,1,0:T(8,128)(2,1)} %pad_maximum_fusion.1.refs_2_, bf16[32,40,128]{2,1,0:T(8,128)(2,1)} %copy-done.3, bf16[32,40,128]{2,1,0:T(8,128)(2,1)} %copy-done.4, bf16[32,40,128]{2,1,0:T(8,128)(2,1)} %copy-done.2, ...), custom_call_target="tpu_custom_call" | custom-call | tf_op jit(solution)/shard_map/pallas_call | solution.py:136
  (1 shorter events, 0.0 us)
Async XLA Ops:
  24.0 11.1 %copy-start = (bf16[32,40,128]{2,1,0:T(8,128)(2,1)}, bf16[32,40,128]{2,1,0:T(8,128)(2,1)S(1)}, u32[]{:S(2)}) copy-start(bf16[32,40,128]{2,1,0:T(8,128)(2,1)S(1)} %copy.17.refs_6_) | copy-start | bytes 983044
  24.0 8.5 %collective-permute-start.2 = (bf16[32,40,128]{2,1,0:T(8,128)(2,1)S(1)}, bf16[32,40,128]{2,1,0:T(8,128)(2,1)S(1)}, u32[]{:S(2)}, u32[]{:S(2)}) collective-permute-start(bf16[32,40,128]{2,1,0:T(8,128)(2,1)S(1)} %copy.17.refs_6_), channel_id=1, source_target_pairs={{1,0},{2,1},{3,2},{4,3},{5,4},{6,5},{7,6},{9,8},{10,9},{11,10},{12... | collective-permute-start | bytes 983048 | tf_op jit(solution)/shard_map/ppermute | solution.py:19
  25.3 7.2 %collective-permute-start.1 = (bf16[32,40,128]{2,1,0:T(8,128)(2,1)S(1)}, bf16[32,40,128]{2,1,0:T(8,128)(2,1)S(1)}, u32[]{:S(2)}, u32[]{:S(2)}) collective-permute-start(bf16[32,40,128]{2,1,0:T(8,128)(2,1)S(1)} %copy.17.refs_6_), channel_id=1, source_target_pairs={{0,1},{1,2},{2,3},{3,4},{4,5},{5,6},{6,7},{8,9},{9,10},{10,11},{11... | collective-permute-start | bytes 983048 | tf_op jit(solution)/shard_map/ppermute | solution.py:19
  29.0 8.0 %collective-permute-start = (bf16[32,40,128]{2,1,0:T(8,128)(2,1)S(1)}, bf16[32,40,128]{2,1,0:T(8,128)(2,1)S(1)}, u32[]{:S(2)}, u32[]{:S(2)}) collective-permute-start(bf16[32,40,128]{2,1,0:T(8,128)(2,1)S(1)} %copy.17.refs_6_), channel_id=1, source_target_pairs={{0,2},{2,4},{3,1},{4,6},{5,3},{7,5},{8,10},{10,12},{11,9},{12,14},... | collective-permute-start | bytes 983048 | tf_op jit(solution)/shard_map/ppermute | solution.py:162
  32.5 1.2 %copy-start.1 = (bf16[32,40,128]{2,1,0:T(8,128)(2,1)}, bf16[32,40,128]{2,1,0:T(8,128)(2,1)S(1)}, u32[]{:S(2)}) copy-start(bf16[32,40,128]{2,1,0:T(8,128)(2,1)S(1)} %collective-permute-done.2.refs_7_) | copy-start | bytes 983044
  32.5 1.2 %copy-start.2 = (bf16[32,40,128]{2,1,0:T(8,128)(2,1)}, bf16[32,40,128]{2,1,0:T(8,128)(2,1)S(1)}, u32[]{:S(2)}) copy-start(bf16[32,40,128]{2,1,0:T(8,128)(2,1)S(1)} %collective-permute-done.1.refs_5_) | copy-start | bytes 983044
  32.6 4.5 %collective-permute-start.3 = (bf16[32,40,128]{2,1,0:T(8,128)(2,1)S(1)}, bf16[32,40,128]{2,1,0:T(8,128)(2,1)S(1)}, u32[]{:S(2)}, u32[]{:S(2)}) collective-permute-start(bf16[32,40,128]{2,1,0:T(8,128)(2,1)S(1)} %broadcast_select_fusion), channel_id=1, source_target_pairs={{0,1},{1,0},{2,3},{3,2},{4,5},{5,4},{6,7},{7,6},{8,9},{9,8},{10,11... | collective-permute-start | bytes 983048 | tf_op jit(solution)/shard_map/ppermute | solution.py:166
  37.0 0.7 %copy-start.3 = (bf16[32,40,128]{2,1,0:T(8,128)(2,1)}, bf16[32,40,128]{2,1,0:T(8,128)(2,1)S(1)}, u32[]{:S(2)}) copy-start(bf16[32,40,128]{2,1,0:T(8,128)(2,1)S(1)} %collective-permute-done.refs_3_) | copy-start | bytes 983044
  37.0 0.8 %copy-start.4 = (bf16[32,40,128]{2,1,0:T(8,128)(2,1)}, bf16[32,40,128]{2,1,0:T(8,128)(2,1)S(1)}, u32[]{:S(2)}) copy-start(bf16[32,40,128]{2,1,0:T(8,128)(2,1)S(1)} %collective-permute-done.3.refs_4_) | copy-start | bytes 983044

commit v16 on v15

--- a/solution.py
+++ b/solution.py
@@ -10,7 +10,7 @@
 
 BINS = 128
 R = 2
-BINS_PER_STEP = 8
+BINS_PER_STEP = 16
 
 
 def passed_along(array, axis, by, sources=lambda i: True):
@@ -114,7 +114,6 @@
         r = lax.dot_general(
             lx_ref[b], ycat, (((1,), (1,)), ((), ())), preferred_element_type=jnp.float32
         )
-        r = r * scale
         for p in range(slots):
             for x in range(2):
                 col = (2 * b + x) * s
@@ -172,6 +171,7 @@
     x_im = pairs_view[..., 1]
     swapped = jnp.stack([-x_im, x_re], axis=3).reshape(nb, stations, 2 * windows)
     lx = jnp.concatenate([spec, swapped], axis=1)
+    lx = lx * jnp.asarray(1.0 / windows, lx.dtype)
     result = cross_block(partner_row, counts, lx, ys, windows, slots)
     return result[None]
 

time: 44.9 us -> 44.2 us (0.984)
  Pallas kernels: 14.3 us -> 13.6 us
    mul x0 -> x1, other arithmetic: none -> 0.97 us  [body(): lx = lx * jnp.asarray(1.0 / windows, lx.dtype)]
    concatenate x1 -> x0, other arithmetic: 0.89 us -> none  [body(): lx = jnp.concatenate([spec, swapped], axis=1)]
    pallas_call x1, Pallas kernels: 6.23 us -> 5.48 us  [cross_block(): pl.pallas_call(kernel, grid_spec=grid_spec, out_shape=jax.ShapeDtypeStruc...]
  transfers between devices with their start and end apart: 4 -> 4, of which waited for: 1 -> 1; matrix products, arithmetic and copies ran while one was open for 5% -> 6% of each run, Pallas kernels for 0% -> 0%
where the time goes in v16:
time: 44.2 us; the launch traced here: 43.4 us
  Pallas kernels  13.6 us (31%)
  blocking collectives  11.6 us (26%)
  starting transfers between devices  8.87 us (20%)
  local copies, waits for them, and re-layouts  6.23 us (14%)
  other arithmetic  1.31 us (3%)
  waiting for transfers between devices  1.02 us (2%)
  between operations  0.82 us (2%)
    all_to_all x1, blocking collectives, body(): lax.all_to_all(own_spec, 'tm', split_axis=3, concat_axis=2, tiled=True)  11.6 us
    pallas_call x1, Pallas kernels, whiten(): pl.pallas_call(dft_kernel, grid=(samples // (fine * coarse_step),), in_sp...  8.07 us
    pallas_call x1, Pallas kernels, cross_block(): pl.pallas_call(kernel, grid_spec=grid_spec, out_shape=jax.ShapeDtypeStruc...  5.48 us
    ppermute x2, starting transfers between devices, passed_along(): return lax.ppermute(array, axis, pairs)  4.34 us
    ppermute x1, starting transfers between devices, body(): lax.ppermute(paired, 'sta', [(i, i + 2 - 4 * (i % 2)) for i in range(peer...  3.49 us
    unnamed x12, local copies, waits for them, and re-layouts  1.75 us
    reshape x2, local copies, waits for them, and re-layouts, whiten(): return white.reshape(1, stations, windows, groups, width // groups)  1.4 us
    reshape x1, local copies, waits for them, and re-layouts, body(): spec = regrouped.reshape(stations, windows, 2, nb).transpose(3, 0, 1, 2)....  1.09 us
  transfers between devices with their start and end apart: 4, of which 1 were waited for; matrix products, arithmetic and copies ran while one was open for 6% of the time, Pallas kernels for 0%

profile of v16, /device:TPU:0, one launch (start us, length us, event | category | flops | bytes accessed | tf_op | source)
XLA Modules:
  0.0 43.4 jit_solution(10680230373716711370)
XLA Ops:
  0.0 8.1 %shard_map.73 = bf16[640,256]{1,0:T(8,128)(2,1)} custom-call(f32[64,256]{1,0:T(8,128)} %constant.28.clone.p1_ref, f32[64,256]{1,0:T(8,128)} %constant.29.clone.q1_ref, f32[64,256]{1,0:T(8,128)} %constant.30.clone.c2_ref, f32[64,256]{1,0:T(8,128)} %constant.31.clone.s2_ref, f32[640,4096]{1,0:T(8,128)} %bitcast.18), custom_call_target="tpu_custom_call" | custom-call | tf_op jit(solution)/shard_map/pallas_call | solution.py:76
  8.1 1.3 %reshape.17 = bf16[1,40,16,4,64]{4,3,2,1,0:T(4,128)(2,1)S(1)} reshape(bf16[640,256]{1,0:T(8,128)(2,1)} %shard_map.73) | data formatting | bytes 655360 | tf_op jit(solution)/shard_map/reshape | solution.py:90
  9.4 0.1 copy.24
  9.5 0.5 %reshape.21 = bf16[4,2,20480]{2,1,0:T(2,128)(2,1)S(1)} reshape(bf16[4,1,40,16,64]{4,3,2,1,0:T(8,128)(2,1)S(1)} %bitcast.22) | data formatting | bytes 655360
  10.0 11.6 %all_to_all.15 = bf16[4,2,20480]{2,1,0:T(2,128)(2,1)S(1)} all-to-all(bf16[4,2,20480]{2,1,0:T(2,128)(2,1)S(1)} %reshape.21), channel_id=1, replica_groups=mesh['tm'=4,'sta'=8] {'tm'}, dimensions={0} | all-to-all | bytes 655360 | tf_op jit(solution)/shard_map/all_to_all | solution.py:148
  21.5 0.4 reshape.22
  22.0 0.1 bitcast_bitcast_fusion
  22.1 0.8 %copy.16 = bf16[1,40,4,16,1,64]{1,5,3,2,4,0:T(8,128)(2,1)S(1)} copy(bf16[1,40,4,16,1,64]{5,3,1,2,4,0:T(8,128)(2,1)S(1)} %bitcast_bitcast_fusion) | data formatting | bytes 655360 | tf_op jit(solution)/shard_map/all_to_all | solution.py:148
  22.9 1.1 %copy.17.refs_6_ = bf16[32,40,128]{2,1,0:T(8,128)(2,1)S(1)} copy(bf16[32,40,128]{1,0,2:T(8,128)(2,1)S(1)} %bitcast.19) | data formatting | bytes 655360 | tf_op jit(solution)/shard_map/reshape | solution.py:154
  24.0 0.0 copy-start
  24.0 1.3 %collective-permute-start.2 = (bf16[32,40,128]{2,1,0:T(8,128)(2,1)S(1)}, bf16[32,40,128]{2,1,0:T(8,128)(2,1)S(1)}, u32[]{:S(2)}, u32[]{:S(2)}) collective-permute-start(bf16[32,40,128]{2,1,0:T(8,128)(2,1)S(1)} %copy.17.refs_6_), channel_id=1, source_target_pairs={{1,0},{2,1},{3,2},{4,3},{5,4},{6,5},{7,6},{9,8},{10,9},{11,10},{12... | collective-permute-start | bytes 983048 | tf_op jit(solution)/shard_map/ppermute | solution.py:19
  25.3 3.1 %collective-permute-start.1 = (bf16[32,40,128]{2,1,0:T(8,128)(2,1)S(1)}, bf16[32,40,128]{2,1,0:T(8,128)(2,1)S(1)}, u32[]{:S(2)}, u32[]{:S(2)}) collective-permute-start(bf16[32,40,128]{2,1,0:T(8,128)(2,1)S(1)} %copy.17.refs_6_), channel_id=1, source_target_pairs={{0,1},{1,2},{2,3},{3,4},{4,5},{5,6},{6,7},{8,9},{9,10},{10,11},{11... | collective-permute-start | bytes 983048 | tf_op jit(solution)/shard_map/ppermute | solution.py:19
  29.0 3.5 %collective-permute-start = (bf16[32,40,128]{2,1,0:T(8,128)(2,1)S(1)}, bf16[32,40,128]{2,1,0:T(8,128)(2,1)S(1)}, u32[]{:S(2)}, u32[]{:S(2)}) collective-permute-start(bf16[32,40,128]{2,1,0:T(8,128)(2,1)S(1)} %copy.17.refs_6_), channel_id=1, source_target_pairs={{0,2},{2,4},{3,1},{4,6},{5,3},{7,5},{8,10},{10,12},{11,9},{12,14},... | collective-permute-start | bytes 983048 | tf_op jit(solution)/shard_map/ppermute | solution.py:161
  32.5 0.0 collective-permute-done.2.refs_7_
  32.5 0.0 copy-start.1
  32.5 0.0 collective-permute-done.1.refs_5_
  32.5 0.0 copy-start.2
  32.6 1.0 %collective-permute-start.3 = (bf16[32,40,128]{2,1,0:T(8,128)(2,1)S(1)}, bf16[32,40,128]{2,1,0:T(8,128)(2,1)S(1)}, u32[]{:S(2)}, u32[]{:S(2)}) collective-permute-start(bf16[32,40,128]{2,1,0:T(8,128)(2,1)S(1)} %broadcast_select_fusion), channel_id=1, source_target_pairs={{0,1},{1,0},{2,3},{3,2},{4,5},{5,4},{6,7},{7,6},{8,9},{9,8},{10,11... | collective-permute-start | bytes 983048 | tf_op jit(solution)/shard_map/ppermute | solution.py:165
  33.6 0.1 slice_negate_fusion
  33.7 0.0 copy-done.1
  33.7 0.0 copy-done.2
  33.7 0.2 pad_maximum_fusion
  34.0 1.1 %copy.18 = bf16[32,40,128]{2,1,0:T(8,128)(2,1)S(1)} copy(bf16[32,40,128]{1,0,2:T(8,128)(2,1)S(1)} %bitcast.21) | data formatting | bytes 655360 | tf_op jit(solution)/shard_map/reshape | solution.py:172
  35.1 0.0 copy-done
  35.1 1.0 %maximum_multiply_fusion.refs_2_ = bf16[32,80,128]{2,1,0:T(8,128)(2,1)} fusion(bf16[32,40,128]{2,1,0:T(8,128)(2,1)S(1)} %copy.18, bf16[32,40,128]{2,1,0:T(8,128)(2,1)S(1)} %copy.17.refs_6_), kind=kLoop, calls=%fused_computation.1 | loop fusion | flops 1966080 | bytes 1310720 | tf_op jit(solution)/shard_map/mul | solution.py:174
  36.0 1.0 %collective-permute-done.refs_3_ = bf16[32,40,128]{2,1,0:T(8,128)(2,1)S(1)} collective-permute-done((bf16[32,40,128]{2,1,0:T(8,128)(2,1)S(1)}, bf16[32,40,128]{2,1,0:T(8,128)(2,1)S(1)}, u32[]{:S(2)}, u32[]{:S(2)}) %collective-permute-start) | collective-permute-done | bytes 327712 | tf_op jit(solution)/shard_map/ppermute | solution.py:161
  37.0 0.0 copy-start.3
  37.0 0.0 collective-permute-done.3.refs_4_
  37.0 0.0 copy-start.4
  37.0 0.7 %copy-done.3 = bf16[32,40,128]{2,1,0:T(8,128)(2,1)} copy-done((bf16[32,40,128]{2,1,0:T(8,128)(2,1)}, bf16[32,40,128]{2,1,0:T(8,128)(2,1)S(1)}, u32[]{:S(2)}) %copy-start.3) | copy-done | bytes 327704
  37.8 0.1 copy-done.4
  37.9 5.5 %shard_map.74 = f32[5,40,2560]{2,1,0:T(8,128)} custom-call(s32[5]{0:T(128)} %bitcast.23, s32[1]{0:T(128)S(6)} %copy.25.refs_1_, bf16[32,80,128]{2,1,0:T(8,128)(2,1)} %maximum_multiply_fusion.refs_2_, bf16[32,40,128]{2,1,0:T(8,128)(2,1)} %copy-done.3, bf16[32,40,128]{2,1,0:T(8,128)(2,1)} %copy-done.4, bf16[32,40,128]{2,1,0:T(8,128)(2,1)} %copy-done.2, ...), custom_call_target="tpu_custom_call" | custom-call | tf_op jit(solution)/shard_map/pallas_call | solution.py:135
  (1 shorter events, 0.0 us)
Async XLA Ops:
  24.0 11.1 %copy-start = (bf16[32,40,128]{2,1,0:T(8,128)(2,1)}, bf16[32,40,128]{2,1,0:T(8,128)(2,1)S(1)}, u32[]{:S(2)}) copy-start(bf16[32,40,128]{2,1,0:T(8,128)(2,1)S(1)} %copy.17.refs_6_) | copy-start | bytes 983044
  24.0 8.5 %collective-permute-start.2 = (bf16[32,40,128]{2,1,0:T(8,128)(2,1)S(1)}, bf16[32,40,128]{2,1,0:T(8,128)(2,1)S(1)}, u32[]{:S(2)}, u32[]{:S(2)}) collective-permute-start(bf16[32,40,128]{2,1,0:T(8,128)(2,1)S(1)} %copy.17.refs_6_), channel_id=1, source_target_pairs={{1,0},{2,1},{3,2},{4,3},{5,4},{6,5},{7,6},{9,8},{10,9},{11,10},{12... | collective-permute-start | bytes 983048 | tf_op jit(solution)/shard_map/ppermute | solution.py:19
  25.3 7.2 %collective-permute-start.1 = (bf16[32,40,128]{2,1,0:T(8,128)(2,1)S(1)}, bf16[32,40,128]{2,1,0:T(8,128)(2,1)S(1)}, u32[]{:S(2)}, u32[]{:S(2)}) collective-permute-start(bf16[32,40,128]{2,1,0:T(8,128)(2,1)S(1)} %copy.17.refs_6_), channel_id=1, source_target_pairs={{0,1},{1,2},{2,3},{3,4},{4,5},{5,6},{6,7},{8,9},{9,10},{10,11},{11... | collective-permute-start | bytes 983048 | tf_op jit(solution)/shard_map/ppermute | solution.py:19
  29.0 8.0 %collective-permute-start = (bf16[32,40,128]{2,1,0:T(8,128)(2,1)S(1)}, bf16[32,40,128]{2,1,0:T(8,128)(2,1)S(1)}, u32[]{:S(2)}, u32[]{:S(2)}) collective-permute-start(bf16[32,40,128]{2,1,0:T(8,128)(2,1)S(1)} %copy.17.refs_6_), channel_id=1, source_target_pairs={{0,2},{2,4},{3,1},{4,6},{5,3},{7,5},{8,10},{10,12},{11,9},{12,14},... | collective-permute-start | bytes 983048 | tf_op jit(solution)/shard_map/ppermute | solution.py:161
  32.5 1.2 %copy-start.1 = (bf16[32,40,128]{2,1,0:T(8,128)(2,1)}, bf16[32,40,128]{2,1,0:T(8,128)(2,1)S(1)}, u32[]{:S(2)}) copy-start(bf16[32,40,128]{2,1,0:T(8,128)(2,1)S(1)} %collective-permute-done.2.refs_7_) | copy-start | bytes 983044
  32.5 1.2 %copy-start.2 = (bf16[32,40,128]{2,1,0:T(8,128)(2,1)}, bf16[32,40,128]{2,1,0:T(8,128)(2,1)S(1)}, u32[]{:S(2)}) copy-start(bf16[32,40,128]{2,1,0:T(8,128)(2,1)S(1)} %collective-permute-done.1.refs_5_) | copy-start | bytes 983044
  32.6 4.5 %collective-permute-start.3 = (bf16[32,40,128]{2,1,0:T(8,128)(2,1)S(1)}, bf16[32,40,128]{2,1,0:T(8,128)(2,1)S(1)}, u32[]{:S(2)}, u32[]{:S(2)}) collective-permute-start(bf16[32,40,128]{2,1,0:T(8,128)(2,1)S(1)} %broadcast_select_fusion), channel_id=1, source_target_pairs={{0,1},{1,0},{2,3},{3,2},{4,5},{5,4},{6,7},{7,6},{8,9},{9,8},{10,11... | collective-permute-start | bytes 983048 | tf_op jit(solution)/shard_map/ppermute | solution.py:165
  37.0 0.7 %copy-start.3 = (bf16[32,40,128]{2,1,0:T(8,128)(2,1)}, bf16[32,40,128]{2,1,0:T(8,128)(2,1)S(1)}, u32[]{:S(2)}) copy-start(bf16[32,40,128]{2,1,0:T(8,128)(2,1)S(1)} %collective-permute-done.refs_3_) | copy-start | bytes 983044
  37.0 0.8 %copy-start.4 = (bf16[32,40,128]{2,1,0:T(8,128)(2,1)}, bf16[32,40,128]{2,1,0:T(8,128)(2,1)S(1)}, u32[]{:S(2)}) copy-start(bf16[32,40,128]{2,1,0:T(8,128)(2,1)S(1)} %collective-permute-done.3.refs_4_) | copy-start | bytes 983044

commit v17 on v16

--- a/solution.py
+++ b/solution.py
@@ -44,24 +44,33 @@
     return hi, lo
 
 
-def dft_kernel(p1_ref, q1_ref, c2_ref, s2_ref, x_ref, o_ref, acc_ref):
+def dft_kernel(p1_ref, q1_ref, c2_ref, s2_ref, x_ref, o_ref, acc_ref, th_ref, tl_ref):
     k = pl.program_id(0)
+    i = pl.program_id(1)
+    rows = x_ref.shape[0]
+    here = pl.ds(pl.multiple_of(i * rows, rows), rows)
+
+    @pl.when(i == 0)
+    def _():
+        c2 = c2_ref[...]
+        s2 = s2_ref[...]
+        parts = [p1_ref[a:a + 1, :] * c2 + q1_ref[a:a + 1, :] * s2 for a in range(p1_ref.shape[0])]
+        t_hi, t_lo = split_bf16(jnp.concatenate(parts, axis=0))
+        th_ref[...] = t_hi
+        tl_ref[...] = t_lo
 
     @pl.when(k == 0)
     def _():
-        acc_ref[...] = jnp.zeros(acc_ref.shape, acc_ref.dtype)
+        acc_ref[here, :] = jnp.zeros((rows, acc_ref.shape[1]), acc_ref.dtype)
 
-    c2 = c2_ref[...]
-    s2 = s2_ref[...]
-    rows = [p1_ref[a:a + 1, :] * c2 + q1_ref[a:a + 1, :] * s2 for a in range(p1_ref.shape[0])]
-    t_hi, t_lo = split_bf16(jnp.concatenate(rows, axis=0))
     x_hi, x_lo = split_bf16(x_ref[...])
+    t_hi = th_ref[...]
     dot = lambda a, b: jnp.dot(a, b, preferred_element_type=jnp.float32)
-    acc_ref[...] += dot(x_hi, t_hi) + dot(x_hi, t_lo) + dot(x_lo, t_hi)
+    acc_ref[here, :] += dot(x_hi, t_hi) + dot(x_hi, tl_ref[...]) + dot(x_lo, t_hi)
 
     @pl.when(k == pl.num_programs(0) - 1)
     def _():
-        spectra = acc_ref[...]
+        spectra = acc_ref[here, :]
         mean_power = jnp.mean(spectra * spectra, axis=1, keepdims=True)
         o_ref[...] = (spectra / jnp.sqrt(mean_power + 1e-06)).astype(o_ref.dtype)
 
@@ -73,19 +82,25 @@
     coarse_step = 32
     rows = stations * windows
     x = records.reshape(rows, samples)
+    halves = 2
+    block = fine * coarse_step
     white = pl.pallas_call(
         dft_kernel,
-        grid=(samples // (fine * coarse_step),),
+        grid=(samples // block, halves),
         in_specs=[
-            pl.BlockSpec((coarse_step, width), lambda k: (k, 0)),
-            pl.BlockSpec((coarse_step, width), lambda k: (k, 0)),
-            pl.BlockSpec((fine, width), lambda k: (0, 0)),
-            pl.BlockSpec((fine, width), lambda k: (0, 0)),
-            pl.BlockSpec((rows, fine * coarse_step), lambda k: (0, k)),
+            pl.BlockSpec((coarse_step, width), lambda k, i: (k, 0)),
+            pl.BlockSpec((coarse_step, width), lambda k, i: (k, 0)),
+            pl.BlockSpec((fine, width), lambda k, i: (0, 0)),
+            pl.BlockSpec((fine, width), lambda k, i: (0, 0)),
+            pl.BlockSpec((rows // halves, block), lambda k, i: (i, k)),
         ],
-        out_specs=pl.BlockSpec((rows, width), lambda k: (0, 0)),
+        out_specs=pl.BlockSpec((rows // halves, width), lambda k, i: (i, 0)),
         out_shape=jax.ShapeDtypeStruct((rows, width), jnp.bfloat16),
-        scratch_shapes=[pltpu.VMEM((rows, width), jnp.float32)],
+        scratch_shapes=[
+            pltpu.VMEM((rows, width), jnp.float32),
+            pltpu.VMEM((block, width), jnp.bfloat16),
+            pltpu.VMEM((block, width), jnp.bfloat16),
+        ],
     )(p1, q1, c2, s2, x)
     return white.reshape(1, stations, windows, groups, width // groups)
 

time: 44.2 us -> 45.3 us (1.025)
  Pallas kernels: 13.6 us -> 14.7 us
    pallas_call x1, Pallas kernels: 8.07 us -> 9.2 us  [whiten(): pl.pallas_call(dft_kernel, grid=(samples // block, halves), in_specs=[pl....]
  transfers between devices with their start and end apart: 4 -> 4, of which waited for: 1 -> 1; matrix products, arithmetic and copies ran while one was open for 6% -> 5% of each run, Pallas kernels for 0% -> 0%
where the time goes in v17:
time: 45.3 us; the launch traced here: 44.5 us
  Pallas kernels  14.7 us (32%)
  blocking collectives  11.6 us (26%)
  starting transfers between devices  8.87 us (20%)
  local copies, waits for them, and re-layouts  6.23 us (14%)
  other arithmetic  1.31 us (3%)
  waiting for transfers between devices  1.02 us (2%)
  between operations  0.82 us (2%)
    all_to_all x1, blocking collectives, body(): lax.all_to_all(own_spec, 'tm', split_axis=3, concat_axis=2, tiled=True)  11.6 us
    pallas_call x1, Pallas kernels, whiten(): pl.pallas_call(dft_kernel, grid=(samples // block, halves), in_specs=[pl....  9.2 us
    pallas_call x1, Pallas kernels, cross_block(): pl.pallas_call(kernel, grid_spec=grid_spec, out_shape=jax.ShapeDtypeStruc...  5.49 us
    ppermute x2, starting transfers between devices, passed_along(): return lax.ppermute(array, axis, pairs)  4.34 us
    ppermute x1, starting transfers between devices, body(): lax.ppermute(paired, 'sta', [(i, i + 2 - 4 * (i % 2)) for i in range(peer...  3.49 us
    unnamed x12, local copies, waits for them, and re-layouts  1.75 us
    reshape x2, local copies, waits for them, and re-layouts, whiten(): return white.reshape(1, stations, windows, groups, width // groups)  1.4 us
    reshape x1, local copies, waits for them, and re-layouts, body(): spec = regrouped.reshape(stations, windows, 2, nb).transpose(3, 0, 1, 2)....  1.09 us
  transfers between devices with their start and end apart: 4, of which 1 were waited for; matrix products, arithmetic and copies ran while one was open for 5% of the time, Pallas kernels for 0%

profile of v17, /device:TPU:0, one launch (start us, length us, event | category | flops | bytes accessed | tf_op | source)
XLA Modules:
  0.0 44.5 jit_solution(9233927671798221355)
XLA Ops:
  0.0 9.2 %shard_map.73 = bf16[640,256]{1,0:T(8,128)(2,1)} custom-call(f32[64,256]{1,0:T(8,128)} %constant.28.clone.p1_ref, f32[64,256]{1,0:T(8,128)} %constant.29.clone.q1_ref, f32[64,256]{1,0:T(8,128)} %constant.30.clone.c2_ref, f32[64,256]{1,0:T(8,128)} %constant.31.clone.s2_ref, f32[640,4096]{1,0:T(8,128)} %bitcast.18), custom_call_target="tpu_custom_call" | custom-call | tf_op jit(solution)/shard_map/pallas_call | solution.py:87
  9.2 1.3 %reshape.17 = bf16[1,40,16,4,64]{4,3,2,1,0:T(4,128)(2,1)S(1)} reshape(bf16[640,256]{1,0:T(8,128)(2,1)} %shard_map.73) | data formatting | bytes 655360 | tf_op jit(solution)/shard_map/reshape | solution.py:105
  10.5 0.1 copy.24
  10.6 0.5 %reshape.21 = bf16[4,2,20480]{2,1,0:T(2,128)(2,1)S(1)} reshape(bf16[4,1,40,16,64]{4,3,2,1,0:T(8,128)(2,1)S(1)} %bitcast.22) | data formatting | bytes 655360
  11.1 11.6 %all_to_all.15 = bf16[4,2,20480]{2,1,0:T(2,128)(2,1)S(1)} all-to-all(bf16[4,2,20480]{2,1,0:T(2,128)(2,1)S(1)} %reshape.21), channel_id=1, replica_groups=mesh['tm'=4,'sta'=8] {'tm'}, dimensions={0} | all-to-all | bytes 655360 | tf_op jit(solution)/shard_map/all_to_all | solution.py:163
  22.7 0.4 reshape.22
  23.1 0.1 bitcast_bitcast_fusion
  23.2 0.8 %copy.16 = bf16[1,40,4,16,1,64]{1,5,3,2,4,0:T(8,128)(2,1)S(1)} copy(bf16[1,40,4,16,1,64]{5,3,1,2,4,0:T(8,128)(2,1)S(1)} %bitcast_bitcast_fusion) | data formatting | bytes 655360 | tf_op jit(solution)/shard_map/all_to_all | solution.py:163
  24.0 1.1 %copy.17.refs_6_ = bf16[32,40,128]{2,1,0:T(8,128)(2,1)S(1)} copy(bf16[32,40,128]{1,0,2:T(8,128)(2,1)S(1)} %bitcast.19) | data formatting | bytes 655360 | tf_op jit(solution)/shard_map/reshape | solution.py:169
  25.1 0.0 copy-start
  25.1 1.3 %collective-permute-start.2 = (bf16[32,40,128]{2,1,0:T(8,128)(2,1)S(1)}, bf16[32,40,128]{2,1,0:T(8,128)(2,1)S(1)}, u32[]{:S(2)}, u32[]{:S(2)}) collective-permute-start(bf16[32,40,128]{2,1,0:T(8,128)(2,1)S(1)} %copy.17.refs_6_), channel_id=1, source_target_pairs={{1,0},{2,1},{3,2},{4,3},{5,4},{6,5},{7,6},{9,8},{10,9},{11,10},{12... | collective-permute-start | bytes 983048 | tf_op jit(solution)/shard_map/ppermute | solution.py:19
  26.4 3.1 %collective-permute-start.1 = (bf16[32,40,128]{2,1,0:T(8,128)(2,1)S(1)}, bf16[32,40,128]{2,1,0:T(8,128)(2,1)S(1)}, u32[]{:S(2)}, u32[]{:S(2)}) collective-permute-start(bf16[32,40,128]{2,1,0:T(8,128)(2,1)S(1)} %copy.17.refs_6_), channel_id=1, source_target_pairs={{0,1},{1,2},{2,3},{3,4},{4,5},{5,6},{6,7},{8,9},{9,10},{10,11},{11... | collective-permute-start | bytes 983048 | tf_op jit(solution)/shard_map/ppermute | solution.py:19
  30.1 3.5 %collective-permute-start = (bf16[32,40,128]{2,1,0:T(8,128)(2,1)S(1)}, bf16[32,40,128]{2,1,0:T(8,128)(2,1)S(1)}, u32[]{:S(2)}, u32[]{:S(2)}) collective-permute-start(bf16[32,40,128]{2,1,0:T(8,128)(2,1)S(1)} %copy.17.refs_6_), channel_id=1, source_target_pairs={{0,2},{2,4},{3,1},{4,6},{5,3},{7,5},{8,10},{10,12},{11,9},{12,14},... | collective-permute-start | bytes 983048 | tf_op jit(solution)/shard_map/ppermute | solution.py:176
  33.6 0.0 collective-permute-done.2.refs_7_
  33.6 0.0 copy-start.1
  33.6 0.0 collective-permute-done.1.refs_5_
  33.6 0.0 copy-start.2
  33.7 1.0 %collective-permute-start.3 = (bf16[32,40,128]{2,1,0:T(8,128)(2,1)S(1)}, bf16[32,40,128]{2,1,0:T(8,128)(2,1)S(1)}, u32[]{:S(2)}, u32[]{:S(2)}) collective-permute-start(bf16[32,40,128]{2,1,0:T(8,128)(2,1)S(1)} %broadcast_select_fusion), channel_id=1, source_target_pairs={{0,1},{1,0},{2,3},{3,2},{4,5},{5,4},{6,7},{7,6},{8,9},{9,8},{10,11... | collective-permute-start | bytes 983048 | tf_op jit(solution)/shard_map/ppermute | solution.py:180
  34.7 0.1 slice_negate_fusion
  34.8 0.0 copy-done.1
  34.9 0.0 copy-done.2
  34.9 0.2 pad_maximum_fusion
  35.1 1.1 %copy.18 = bf16[32,40,128]{2,1,0:T(8,128)(2,1)S(1)} copy(bf16[32,40,128]{1,0,2:T(8,128)(2,1)S(1)} %bitcast.21) | data formatting | bytes 655360 | tf_op jit(solution)/shard_map/reshape | solution.py:187
  36.2 0.0 copy-done
  36.2 1.0 %maximum_multiply_fusion.refs_2_ = bf16[32,80,128]{2,1,0:T(8,128)(2,1)} fusion(bf16[32,40,128]{2,1,0:T(8,128)(2,1)S(1)} %copy.18, bf16[32,40,128]{2,1,0:T(8,128)(2,1)S(1)} %copy.17.refs_6_), kind=kLoop, calls=%fused_computation.1 | loop fusion | flops 1966080 | bytes 1310720 | tf_op jit(solution)/shard_map/mul | solution.py:189
  37.2 1.0 %collective-permute-done.refs_3_ = bf16[32,40,128]{2,1,0:T(8,128)(2,1)S(1)} collective-permute-done((bf16[32,40,128]{2,1,0:T(8,128)(2,1)S(1)}, bf16[32,40,128]{2,1,0:T(8,128)(2,1)S(1)}, u32[]{:S(2)}, u32[]{:S(2)}) %collective-permute-start) | collective-permute-done | bytes 327712 | tf_op jit(solution)/shard_map/ppermute | solution.py:176
  38.2 0.0 copy-start.3
  38.2 0.0 collective-permute-done.3.refs_4_
  38.2 0.0 copy-start.4
  38.2 0.7 %copy-done.3 = bf16[32,40,128]{2,1,0:T(8,128)(2,1)} copy-done((bf16[32,40,128]{2,1,0:T(8,128)(2,1)}, bf16[32,40,128]{2,1,0:T(8,128)(2,1)S(1)}, u32[]{:S(2)}) %copy-start.3) | copy-done | bytes 327704
  38.9 0.1 copy-done.4
  39.0 5.5 %shard_map.74 = f32[5,40,2560]{2,1,0:T(8,128)} custom-call(s32[5]{0:T(128)} %bitcast.23, s32[1]{0:T(128)S(6)} %copy.25.refs_1_, bf16[32,80,128]{2,1,0:T(8,128)(2,1)} %maximum_multiply_fusion.refs_2_, bf16[32,40,128]{2,1,0:T(8,128)(2,1)} %copy-done.3, bf16[32,40,128]{2,1,0:T(8,128)(2,1)} %copy-done.4, bf16[32,40,128]{2,1,0:T(8,128)(2,1)} %copy-done.2, ...), custom_call_target="tpu_custom_call" | custom-call | tf_op jit(solution)/shard_map/pallas_call | solution.py:150
  (1 shorter events, 0.0 us)
Async XLA Ops:
  25.1 11.1 %copy-start = (bf16[32,40,128]{2,1,0:T(8,128)(2,1)}, bf16[32,40,128]{2,1,0:T(8,128)(2,1)S(1)}, u32[]{:S(2)}) copy-start(bf16[32,40,128]{2,1,0:T(8,128)(2,1)S(1)} %copy.17.refs_6_) | copy-start | bytes 983044
  25.1 8.5 %collective-permute-start.2 = (bf16[32,40,128]{2,1,0:T(8,128)(2,1)S(1)}, bf16[32,40,128]{2,1,0:T(8,128)(2,1)S(1)}, u32[]{:S(2)}, u32[]{:S(2)}) collective-permute-start(bf16[32,40,128]{2,1,0:T(8,128)(2,1)S(1)} %copy.17.refs_6_), channel_id=1, source_target_pairs={{1,0},{2,1},{3,2},{4,3},{5,4},{6,5},{7,6},{9,8},{10,9},{11,10},{12... | collective-permute-start | bytes 983048 | tf_op jit(solution)/shard_map/ppermute | solution.py:19
  26.4 7.2 %collective-permute-start.1 = (bf16[32,40,128]{2,1,0:T(8,128)(2,1)S(1)}, bf16[32,40,128]{2,1,0:T(8,128)(2,1)S(1)}, u32[]{:S(2)}, u32[]{:S(2)}) collective-permute-start(bf16[32,40,128]{2,1,0:T(8,128)(2,1)S(1)} %copy.17.refs_6_), channel_id=1, source_target_pairs={{0,1},{1,2},{2,3},{3,4},{4,5},{5,6},{6,7},{8,9},{9,10},{10,11},{11... | collective-permute-start | bytes 983048 | tf_op jit(solution)/shard_map/ppermute | solution.py:19
  30.1 8.0 %collective-permute-start = (bf16[32,40,128]{2,1,0:T(8,128)(2,1)S(1)}, bf16[32,40,128]{2,1,0:T(8,128)(2,1)S(1)}, u32[]{:S(2)}, u32[]{:S(2)}) collective-permute-start(bf16[32,40,128]{2,1,0:T(8,128)(2,1)S(1)} %copy.17.refs_6_), channel_id=1, source_target_pairs={{0,2},{2,4},{3,1},{4,6},{5,3},{7,5},{8,10},{10,12},{11,9},{12,14},... | collective-permute-start | bytes 983048 | tf_op jit(solution)/shard_map/ppermute | solution.py:176
  33.6 1.2 %copy-start.1 = (bf16[32,40,128]{2,1,0:T(8,128)(2,1)}, bf16[32,40,128]{2,1,0:T(8,128)(2,1)S(1)}, u32[]{:S(2)}) copy-start(bf16[32,40,128]{2,1,0:T(8,128)(2,1)S(1)} %collective-permute-done.2.refs_7_) | copy-start | bytes 983044
  33.6 1.2 %copy-start.2 = (bf16[32,40,128]{2,1,0:T(8,128)(2,1)}, bf16[32,40,128]{2,1,0:T(8,128)(2,1)S(1)}, u32[]{:S(2)}) copy-start(bf16[32,40,128]{2,1,0:T(8,128)(2,1)S(1)} %collective-permute-done.1.refs_5_) | copy-start | bytes 983044
  33.7 4.5 %collective-permute-start.3 = (bf16[32,40,128]{2,1,0:T(8,128)(2,1)S(1)}, bf16[32,40,128]{2,1,0:T(8,128)(2,1)S(1)}, u32[]{:S(2)}, u32[]{:S(2)}) collective-permute-start(bf16[32,40,128]{2,1,0:T(8,128)(2,1)S(1)} %broadcast_select_fusion), channel_id=1, source_target_pairs={{0,1},{1,0},{2,3},{3,2},{4,5},{5,4},{6,7},{7,6},{8,9},{9,8},{10,11... | collective-permute-start | bytes 983048 | tf_op jit(solution)/shard_map/ppermute | solution.py:180
  38.2 0.7 %copy-start.3 = (bf16[32,40,128]{2,1,0:T(8,128)(2,1)}, bf16[32,40,128]{2,1,0:T(8,128)(2,1)S(1)}, u32[]{:S(2)}) copy-start(bf16[32,40,128]{2,1,0:T(8,128)(2,1)S(1)} %collective-permute-done.refs_3_) | copy-start | bytes 983044
  38.2 0.8 %copy-start.4 = (bf16[32,40,128]{2,1,0:T(8,128)(2,1)}, bf16[32,40,128]{2,1,0:T(8,128)(2,1)S(1)}, u32[]{:S(2)}) copy-start(bf16[32,40,128]{2,1,0:T(8,128)(2,1)S(1)} %collective-permute-done.3.refs_4_) | copy-start | bytes 983044

commit v18 on v16

--- a/solution.py
+++ b/solution.py
@@ -57,7 +57,9 @@
     t_hi, t_lo = split_bf16(jnp.concatenate(rows, axis=0))
     x_hi, x_lo = split_bf16(x_ref[...])
     dot = lambda a, b: jnp.dot(a, b, preferred_element_type=jnp.float32)
-    acc_ref[...] += dot(x_hi, t_hi) + dot(x_hi, t_lo) + dot(x_lo, t_hi)
+    acc_ref[...] += dot(x_lo, t_hi)
+    acc_ref[...] += dot(x_hi, t_lo)
+    acc_ref[...] += dot(x_hi, t_hi)
 
     @pl.when(k == pl.num_programs(0) - 1)
     def _():

time: 44.2 us -> 44.1 us (level)
  no operation moved by 1% of the time
where the time goes in v18:
time: 44.1 us; the launch traced here: 43.4 us
  Pallas kernels  13.5 us (31%)
  blocking collectives  11.6 us (26%)
  starting transfers between devices  8.87 us (20%)
  local copies, waits for them, and re-layouts  6.23 us (14%)
  other arithmetic  1.31 us (3%)
  waiting for transfers between devices  1.02 us (2%)
  between operations  0.82 us (2%)
    all_to_all x1, blocking collectives, body(): lax.all_to_all(own_spec, 'tm', split_axis=3, concat_axis=2, tiled=True)  11.6 us
    pallas_call x1, Pallas kernels, whiten(): pl.pallas_call(dft_kernel, grid=(samples // (fine * coarse_step),), in_sp...  8.06 us
    pallas_call x1, Pallas kernels, cross_block(): pl.pallas_call(kernel, grid_spec=grid_spec, out_shape=jax.ShapeDtypeStruc...  5.48 us
    ppermute x2, starting transfers between devices, passed_along(): return lax.ppermute(array, axis, pairs)  4.34 us
    ppermute x1, starting transfers between devices, body(): lax.ppermute(paired, 'sta', [(i, i + 2 - 4 * (i % 2)) for i in range(peer...  3.49 us
    unnamed x12, local copies, waits for them, and re-layouts  1.75 us
    reshape x2, local copies, waits for them, and re-layouts, whiten(): return white.reshape(1, stations, windows, groups, width // groups)  1.4 us
    reshape x1, local copies, waits for them, and re-layouts, body(): spec = regrouped.reshape(stations, windows, 2, nb).transpose(3, 0, 1, 2)....  1.09 us
  transfers between devices with their start and end apart: 4, of which 1 were waited for; matrix products, arithmetic and copies ran while one was open for 6% of the time, Pallas kernels for 0%

profile of v18, /device:TPU:0, one launch (start us, length us, event | category | flops | bytes accessed | tf_op | source)
XLA Modules:
  0.0 43.4 jit_solution(8897896388582321869)
XLA Ops:
  0.0 8.1 %shard_map.73 = bf16[640,256]{1,0:T(8,128)(2,1)} custom-call(f32[64,256]{1,0:T(8,128)} %constant.28.clone.p1_ref, f32[64,256]{1,0:T(8,128)} %constant.29.clone.q1_ref, f32[64,256]{1,0:T(8,128)} %constant.30.clone.c2_ref, f32[64,256]{1,0:T(8,128)} %constant.31.clone.s2_ref, f32[640,4096]{1,0:T(8,128)} %bitcast.18), custom_call_target="tpu_custom_call" | custom-call | tf_op jit(solution)/shard_map/pallas_call | solution.py:78
  8.1 1.3 %reshape.17 = bf16[1,40,16,4,64]{4,3,2,1,0:T(4,128)(2,1)S(1)} reshape(bf16[640,256]{1,0:T(8,128)(2,1)} %shard_map.73) | data formatting | bytes 655360 | tf_op jit(solution)/shard_map/reshape | solution.py:92
  9.4 0.1 copy.24
  9.5 0.5 %reshape.21 = bf16[4,2,20480]{2,1,0:T(2,128)(2,1)S(1)} reshape(bf16[4,1,40,16,64]{4,3,2,1,0:T(8,128)(2,1)S(1)} %bitcast.22) | data formatting | bytes 655360
  10.0 11.6 %all_to_all.15 = bf16[4,2,20480]{2,1,0:T(2,128)(2,1)S(1)} all-to-all(bf16[4,2,20480]{2,1,0:T(2,128)(2,1)S(1)} %reshape.21), channel_id=1, replica_groups=mesh['tm'=4,'sta'=8] {'tm'}, dimensions={0} | all-to-all | bytes 655360 | tf_op jit(solution)/shard_map/all_to_all | solution.py:150
  21.5 0.4 reshape.22
  21.9 0.1 bitcast_bitcast_fusion
  22.1 0.8 %copy.16 = bf16[1,40,4,16,1,64]{1,5,3,2,4,0:T(8,128)(2,1)S(1)} copy(bf16[1,40,4,16,1,64]{5,3,1,2,4,0:T(8,128)(2,1)S(1)} %bitcast_bitcast_fusion) | data formatting | bytes 655360 | tf_op jit(solution)/shard_map/all_to_all | solution.py:150
  22.9 1.1 %copy.17.refs_6_ = bf16[32,40,128]{2,1,0:T(8,128)(2,1)S(1)} copy(bf16[32,40,128]{1,0,2:T(8,128)(2,1)S(1)} %bitcast.19) | data formatting | bytes 655360 | tf_op jit(solution)/shard_map/reshape | solution.py:156
  24.0 0.0 copy-start
  24.0 1.3 %collective-permute-start.2 = (bf16[32,40,128]{2,1,0:T(8,128)(2,1)S(1)}, bf16[32,40,128]{2,1,0:T(8,128)(2,1)S(1)}, u32[]{:S(2)}, u32[]{:S(2)}) collective-permute-start(bf16[32,40,128]{2,1,0:T(8,128)(2,1)S(1)} %copy.17.refs_6_), channel_id=1, source_target_pairs={{1,0},{2,1},{3,2},{4,3},{5,4},{6,5},{7,6},{9,8},{10,9},{11,10},{12... | collective-permute-start | bytes 983048 | tf_op jit(solution)/shard_map/ppermute | solution.py:19
  25.3 3.1 %collective-permute-start.1 = (bf16[32,40,128]{2,1,0:T(8,128)(2,1)S(1)}, bf16[32,40,128]{2,1,0:T(8,128)(2,1)S(1)}, u32[]{:S(2)}, u32[]{:S(2)}) collective-permute-start(bf16[32,40,128]{2,1,0:T(8,128)(2,1)S(1)} %copy.17.refs_6_), channel_id=1, source_target_pairs={{0,1},{1,2},{2,3},{3,4},{4,5},{5,6},{6,7},{8,9},{9,10},{10,11},{11... | collective-permute-start | bytes 983048 | tf_op jit(solution)/shard_map/ppermute | solution.py:19
  29.0 3.5 %collective-permute-start = (bf16[32,40,128]{2,1,0:T(8,128)(2,1)S(1)}, bf16[32,40,128]{2,1,0:T(8,128)(2,1)S(1)}, u32[]{:S(2)}, u32[]{:S(2)}) collective-permute-start(bf16[32,40,128]{2,1,0:T(8,128)(2,1)S(1)} %copy.17.refs_6_), channel_id=1, source_target_pairs={{0,2},{2,4},{3,1},{4,6},{5,3},{7,5},{8,10},{10,12},{11,9},{12,14},... | collective-permute-start | bytes 983048 | tf_op jit(solution)/shard_map/ppermute | solution.py:163
  32.5 0.0 collective-permute-done.2.refs_7_
  32.5 0.0 copy-start.1
  32.5 0.0 collective-permute-done.1.refs_5_
  32.5 0.0 copy-start.2
  32.6 1.0 %collective-permute-start.3 = (bf16[32,40,128]{2,1,0:T(8,128)(2,1)S(1)}, bf16[32,40,128]{2,1,0:T(8,128)(2,1)S(1)}, u32[]{:S(2)}, u32[]{:S(2)}) collective-permute-start(bf16[32,40,128]{2,1,0:T(8,128)(2,1)S(1)} %broadcast_select_fusion), channel_id=1, source_target_pairs={{0,1},{1,0},{2,3},{3,2},{4,5},{5,4},{6,7},{7,6},{8,9},{9,8},{10,11... | collective-permute-start | bytes 983048 | tf_op jit(solution)/shard_map/ppermute | solution.py:167
  33.6 0.1 slice_negate_fusion
  33.7 0.0 copy-done.1
  33.7 0.0 copy-done.2
  33.7 0.2 pad_maximum_fusion
  33.9 1.1 %copy.18 = bf16[32,40,128]{2,1,0:T(8,128)(2,1)S(1)} copy(bf16[32,40,128]{1,0,2:T(8,128)(2,1)S(1)} %bitcast.21) | data formatting | bytes 655360 | tf_op jit(solution)/shard_map/reshape | solution.py:174
  35.0 0.0 copy-done
  35.1 1.0 %maximum_multiply_fusion.refs_2_ = bf16[32,80,128]{2,1,0:T(8,128)(2,1)} fusion(bf16[32,40,128]{2,1,0:T(8,128)(2,1)S(1)} %copy.18, bf16[32,40,128]{2,1,0:T(8,128)(2,1)S(1)} %copy.17.refs_6_), kind=kLoop, calls=%fused_computation.1 | loop fusion | flops 1966080 | bytes 1310720 | tf_op jit(solution)/shard_map/mul | solution.py:176
  36.0 1.0 %collective-permute-done.refs_3_ = bf16[32,40,128]{2,1,0:T(8,128)(2,1)S(1)} collective-permute-done((bf16[32,40,128]{2,1,0:T(8,128)(2,1)S(1)}, bf16[32,40,128]{2,1,0:T(8,128)(2,1)S(1)}, u32[]{:S(2)}, u32[]{:S(2)}) %collective-permute-start) | collective-permute-done | bytes 327712 | tf_op jit(solution)/shard_map/ppermute | solution.py:163
  37.0 0.0 copy-start.3
  37.0 0.0 collective-permute-done.3.refs_4_
  37.0 0.0 copy-start.4
  37.0 0.7 %copy-done.3 = bf16[32,40,128]{2,1,0:T(8,128)(2,1)} copy-done((bf16[32,40,128]{2,1,0:T(8,128)(2,1)}, bf16[32,40,128]{2,1,0:T(8,128)(2,1)S(1)}, u32[]{:S(2)}) %copy-start.3) | copy-done | bytes 327704
  37.8 0.1 copy-done.4
  37.9 5.5 %shard_map.74 = f32[5,40,2560]{2,1,0:T(8,128)} custom-call(s32[5]{0:T(128)} %bitcast.23, s32[1]{0:T(128)S(6)} %copy.25.refs_1_, bf16[32,80,128]{2,1,0:T(8,128)(2,1)} %maximum_multiply_fusion.refs_2_, bf16[32,40,128]{2,1,0:T(8,128)(2,1)} %copy-done.3, bf16[32,40,128]{2,1,0:T(8,128)(2,1)} %copy-done.4, bf16[32,40,128]{2,1,0:T(8,128)(2,1)} %copy-done.2, ...), custom_call_target="tpu_custom_call" | custom-call | tf_op jit(solution)/shard_map/pallas_call | solution.py:137
  (1 shorter events, 0.0 us)
Async XLA Ops:
  24.0 11.1 %copy-start = (bf16[32,40,128]{2,1,0:T(8,128)(2,1)}, bf16[32,40,128]{2,1,0:T(8,128)(2,1)S(1)}, u32[]{:S(2)}) copy-start(bf16[32,40,128]{2,1,0:T(8,128)(2,1)S(1)} %copy.17.refs_6_) | copy-start | bytes 983044
  24.0 8.5 %collective-permute-start.2 = (bf16[32,40,128]{2,1,0:T(8,128)(2,1)S(1)}, bf16[32,40,128]{2,1,0:T(8,128)(2,1)S(1)}, u32[]{:S(2)}, u32[]{:S(2)}) collective-permute-start(bf16[32,40,128]{2,1,0:T(8,128)(2,1)S(1)} %copy.17.refs_6_), channel_id=1, source_target_pairs={{1,0},{2,1},{3,2},{4,3},{5,4},{6,5},{7,6},{9,8},{10,9},{11,10},{12... | collective-permute-start | bytes 983048 | tf_op jit(solution)/shard_map/ppermute | solution.py:19
  25.3 7.2 %collective-permute-start.1 = (bf16[32,40,128]{2,1,0:T(8,128)(2,1)S(1)}, bf16[32,40,128]{2,1,0:T(8,128)(2,1)S(1)}, u32[]{:S(2)}, u32[]{:S(2)}) collective-permute-start(bf16[32,40,128]{2,1,0:T(8,128)(2,1)S(1)} %copy.17.refs_6_), channel_id=1, source_target_pairs={{0,1},{1,2},{2,3},{3,4},{4,5},{5,6},{6,7},{8,9},{9,10},{10,11},{11... | collective-permute-start | bytes 983048 | tf_op jit(solution)/shard_map/ppermute | solution.py:19
  29.0 8.0 %collective-permute-start = (bf16[32,40,128]{2,1,0:T(8,128)(2,1)S(1)}, bf16[32,40,128]{2,1,0:T(8,128)(2,1)S(1)}, u32[]{:S(2)}, u32[]{:S(2)}) collective-permute-start(bf16[32,40,128]{2,1,0:T(8,128)(2,1)S(1)} %copy.17.refs_6_), channel_id=1, source_target_pairs={{0,2},{2,4},{3,1},{4,6},{5,3},{7,5},{8,10},{10,12},{11,9},{12,14},... | collective-permute-start | bytes 983048 | tf_op jit(solution)/shard_map/ppermute | solution.py:163
  32.5 1.2 %copy-start.1 = (bf16[32,40,128]{2,1,0:T(8,128)(2,1)}, bf16[32,40,128]{2,1,0:T(8,128)(2,1)S(1)}, u32[]{:S(2)}) copy-start(bf16[32,40,128]{2,1,0:T(8,128)(2,1)S(1)} %collective-permute-done.2.refs_7_) | copy-start | bytes 983044
  32.5 1.2 %copy-start.2 = (bf16[32,40,128]{2,1,0:T(8,128)(2,1)}, bf16[32,40,128]{2,1,0:T(8,128)(2,1)S(1)}, u32[]{:S(2)}) copy-start(bf16[32,40,128]{2,1,0:T(8,128)(2,1)S(1)} %collective-permute-done.1.refs_5_) | copy-start | bytes 983044
  32.6 4.5 %collective-permute-start.3 = (bf16[32,40,128]{2,1,0:T(8,128)(2,1)S(1)}, bf16[32,40,128]{2,1,0:T(8,128)(2,1)S(1)}, u32[]{:S(2)}, u32[]{:S(2)}) collective-permute-start(bf16[32,40,128]{2,1,0:T(8,128)(2,1)S(1)} %broadcast_select_fusion), channel_id=1, source_target_pairs={{0,1},{1,0},{2,3},{3,2},{4,5},{5,4},{6,7},{7,6},{8,9},{9,8},{10,11... | collective-permute-start | bytes 983048 | tf_op jit(solution)/shard_map/ppermute | solution.py:167
  37.0 0.7 %copy-start.3 = (bf16[32,40,128]{2,1,0:T(8,128)(2,1)}, bf16[32,40,128]{2,1,0:T(8,128)(2,1)S(1)}, u32[]{:S(2)}) copy-start(bf16[32,40,128]{2,1,0:T(8,128)(2,1)S(1)} %collective-permute-done.refs_3_) | copy-start | bytes 983044
  37.0 0.8 %copy-start.4 = (bf16[32,40,128]{2,1,0:T(8,128)(2,1)}, bf16[32,40,128]{2,1,0:T(8,128)(2,1)S(1)}, u32[]{:S(2)}) copy-start(bf16[32,40,128]{2,1,0:T(8,128)(2,1)S(1)} %collective-permute-done.3.refs_4_) | copy-start | bytes 983044

commit v19 on v16

--- a/solution.py
+++ b/solution.py
@@ -156,11 +156,12 @@
     paired = spec
     peers = lax.axis_size("sta")
     parity = block_index % 2
-    left1 = passed_along(paired, "sta", 1)
-    right1 = passed_along(paired, "sta", -1)
     far = lax.ppermute(
         paired, "sta", [(i, i + 2 - 4 * (i % 2)) for i in range(peers) if 0 <= i + 2 - 4 * (i % 2) < peers]
     )
+    paired_near, far = lax.optimization_barrier((paired, far))
+    left1 = passed_along(paired_near, "sta", 1)
+    right1 = passed_along(paired_near, "sta", -1)
     relay = jnp.where(parity == 0, left1, right1)
     forwarded = lax.ppermute(
         relay, "sta", [(i, i + 1 - 2 * (i % 2)) for i in range(peers) if 0 <= i + 1 - 2 * (i % 2) < peers]

time: 44.2 us -> 52.6 us (1.19); the launches traced: 43.4 us -> 52.3 us
  waiting for transfers between devices: 1.02 us -> 5.1 us
  starting transfers between devices: 8.87 us -> 12.8 us
  local copies, waits for them, and re-layouts: 6.23 us -> 7.22 us
    ppermute x1, starting transfers between devices: 1.04 us -> 4.93 us  [body(): lax.ppermute(relay, 'sta', [(i, i + 1 - 2 * (i % 2)) for i in range(peers...]
    ppermute x1, waiting for transfers between devices: 1.01 us -> 4.56 us  [body(): lax.ppermute(paired, 'sta', [(i, i + 2 - 4 * (i % 2)) for i in range(peer...]
    optimization_barrier x0 -> x1, local copies, waits for them, and re-layouts: none -> 1.09 us  [body(): paired_near, far = lax.optimization_barrier((paired, far))]
    ppermute x2, waiting for transfers between devices: 0.01 us -> 0.54 us  [passed_along(): return lax.ppermute(array, axis, pairs)]
  transfers between devices with their start and end apart: 4 -> 4, of which waited for: 1 -> 2; matrix products, arithmetic and copies ran while one was open for 6% -> 5% of each run, Pallas kernels for 0% -> 0%
where the time goes in v19:
time: 52.6 us; the launch traced here: 52.3 us
  Pallas kernels  13.6 us (26%)
  starting transfers between devices  12.8 us (24%)
  blocking collectives  11.6 us (22%)
  local copies, waits for them, and re-layouts  7.22 us (14%)
  waiting for transfers between devices  5.1 us (10%)
  other arithmetic  1.31 us (2%)
  between operations  0.81 us (2%)
    all_to_all x1, blocking collectives, body(): lax.all_to_all(own_spec, 'tm', split_axis=3, concat_axis=2, tiled=True)  11.6 us
    pallas_call x1, Pallas kernels, whiten(): pl.pallas_call(dft_kernel, grid=(samples // (fine * coarse_step),), in_sp...  8.07 us
    pallas_call x1, Pallas kernels, cross_block(): pl.pallas_call(kernel, grid_spec=grid_spec, out_shape=jax.ShapeDtypeStruc...  5.49 us
    ppermute x1, starting transfers between devices, body(): lax.ppermute(relay, 'sta', [(i, i + 1 - 2 * (i % 2)) for i in range(peers...  4.93 us
    ppermute x1, waiting for transfers between devices, body(): lax.ppermute(paired, 'sta', [(i, i + 2 - 4 * (i % 2)) for i in range(peer...  4.56 us
    ppermute x2, starting transfers between devices, passed_along(): return lax.ppermute(array, axis, pairs)  4.34 us
    ppermute x1, starting transfers between devices, body(): lax.ppermute(paired, 'sta', [(i, i + 2 - 4 * (i % 2)) for i in range(peer...  3.5 us
    unnamed x12, local copies, waits for them, and re-layouts  1.64 us
  transfers between devices with their start and end apart: 4, of which 2 were waited for; matrix products, arithmetic and copies ran while one was open for 5% of the time, Pallas kernels for 0%

profile of v19, /device:TPU:0, one launch (start us, length us, event | category | flops | bytes accessed | tf_op | source)
XLA Modules:
  0.0 52.3 jit_solution(1396154606872236547)
XLA Ops:
  0.0 8.1 %shard_map.73 = bf16[640,256]{1,0:T(8,128)(2,1)} custom-call(f32[64,256]{1,0:T(8,128)} %constant.28.clone.p1_ref, f32[64,256]{1,0:T(8,128)} %constant.29.clone.q1_ref, f32[64,256]{1,0:T(8,128)} %constant.30.clone.c2_ref, f32[64,256]{1,0:T(8,128)} %constant.31.clone.s2_ref, f32[640,4096]{1,0:T(8,128)} %bitcast.21), custom_call_target="tpu_custom_call" | custom-call | tf_op jit(solution)/shard_map/pallas_call | solution.py:76
  8.1 1.3 %reshape.17 = bf16[1,40,16,4,64]{4,3,2,1,0:T(4,128)(2,1)S(1)} reshape(bf16[640,256]{1,0:T(8,128)(2,1)} %shard_map.73) | data formatting | bytes 655360 | tf_op jit(solution)/shard_map/reshape | solution.py:90
  9.4 0.1 copy.24
  9.5 0.5 reshape.21
  10.0 11.6 %all_to_all.15 = bf16[4,2,20480]{2,1,0:T(2,128)(2,1)S(1)} all-to-all(bf16[4,2,20480]{2,1,0:T(2,128)(2,1)S(1)} %reshape.21), channel_id=1, replica_groups=mesh['tm'=4,'sta'=8] {'tm'}, dimensions={0} | all-to-all | bytes 655360 | tf_op jit(solution)/shard_map/all_to_all | solution.py:148
  21.5 0.4 reshape.22
  22.0 0.1 bitcast_bitcast_fusion
  22.1 0.8 %copy.16 = bf16[1,40,4,16,1,64]{1,5,3,2,4,0:T(8,128)(2,1)S(1)} copy(bf16[1,40,4,16,1,64]{5,3,1,2,4,0:T(8,128)(2,1)S(1)} %bitcast_bitcast_fusion) | data formatting | bytes 655360 | tf_op jit(solution)/shard_map/all_to_all | solution.py:148
  22.9 1.1 %copy.17.refs_6_ = bf16[32,40,128]{2,1,0:T(8,128)(2,1)S(1)} copy(bf16[32,40,128]{1,0,2:T(8,128)(2,1)S(1)} %bitcast.18) | data formatting | bytes 655360 | tf_op jit(solution)/shard_map/reshape | solution.py:154
  24.0 0.0 copy-start
  24.0 3.5 %collective-permute-start = (bf16[32,40,128]{2,1,0:T(8,128)(2,1)S(1)}, bf16[32,40,128]{2,1,0:T(8,128)(2,1)S(1)}, u32[]{:S(2)}, u32[]{:S(2)}) collective-permute-start(bf16[32,40,128]{2,1,0:T(8,128)(2,1)S(1)} %copy.17.refs_6_), channel_id=1, source_target_pairs={{0,2},{2,4},{3,1},{4,6},{5,3},{7,5},{8,10},{10,12},{11,9},{12,14},... | collective-permute-start | bytes 983048 | tf_op jit(solution)/shard_map/ppermute | solution.py:159
  27.5 4.6 %collective-permute-done.refs_3_ = bf16[32,40,128]{2,1,0:T(8,128)(2,1)S(1)} collective-permute-done((bf16[32,40,128]{2,1,0:T(8,128)(2,1)S(1)}, bf16[32,40,128]{2,1,0:T(8,128)(2,1)S(1)}, u32[]{:S(2)}, u32[]{:S(2)}) %collective-permute-start) | collective-permute-done | bytes 327712 | tf_op jit(solution)/shard_map/ppermute | solution.py:159
  32.0 0.0 copy-start.3
  32.0 1.1 %copy.20 = bf16[32,40,128]{2,1,0:T(8,128)(2,1)S(1)} copy(bf16[32,40,128]{1,0,2:T(8,128)(2,1)S(1)} %bitcast.19) | data formatting | bytes 655360 | tf_op jit(solution)/shard_map/optimization_barrier | solution.py:162
  33.1 1.3 %collective-permute-start.2 = (bf16[32,40,128]{2,1,0:T(8,128)(2,1)S(1)}, bf16[32,40,128]{2,1,0:T(8,128)(2,1)S(1)}, u32[]{:S(2)}, u32[]{:S(2)}) collective-permute-start(bf16[32,40,128]{2,1,0:T(8,128)(2,1)S(1)} %copy.20), channel_id=1, source_target_pairs={{1,0},{2,1},{3,2},{4,3},{5,4},{6,5},{7,6},{9,8},{10,9},{11,10},{12... | collective-permute-start | bytes 983048 | tf_op jit(solution)/shard_map/ppermute | solution.py:19
  34.4 3.1 %collective-permute-start.1 = (bf16[32,40,128]{2,1,0:T(8,128)(2,1)S(1)}, bf16[32,40,128]{2,1,0:T(8,128)(2,1)S(1)}, u32[]{:S(2)}, u32[]{:S(2)}) collective-permute-start(bf16[32,40,128]{2,1,0:T(8,128)(2,1)S(1)} %copy.20), channel_id=1, source_target_pairs={{0,1},{1,2},{2,3},{3,4},{4,5},{5,6},{6,7},{8,9},{9,10},{10,11},{11... | collective-permute-start | bytes 983048 | tf_op jit(solution)/shard_map/ppermute | solution.py:19
  38.2 0.0 collective-permute-done.2.refs_7_
  38.2 0.0 copy-start.1
  38.2 0.5 %collective-permute-done.1.refs_5_ = bf16[32,40,128]{2,1,0:T(8,128)(2,1)S(1)} collective-permute-done((bf16[32,40,128]{2,1,0:T(8,128)(2,1)S(1)}, bf16[32,40,128]{2,1,0:T(8,128)(2,1)S(1)}, u32[]{:S(2)}, u32[]{:S(2)}) %collective-permute-start.1) | collective-permute-done | bytes 327712 | tf_op jit(solution)/shard_map/ppermute | solution.py:19
  38.7 0.0 copy-start.2
  38.8 4.9 %collective-permute-start.3 = (bf16[32,40,128]{2,1,0:T(8,128)(2,1)S(1)}, bf16[32,40,128]{2,1,0:T(8,128)(2,1)S(1)}, u32[]{:S(2)}, u32[]{:S(2)}) collective-permute-start(bf16[32,40,128]{2,1,0:T(8,128)(2,1)S(1)} %broadcast_select_fusion), channel_id=1, source_target_pairs={{0,1},{1,0},{2,3},{3,2},{4,5},{5,4},{6,7},{7,6},{8,9},{9,8},{10,11... | collective-permute-start | bytes 983048 | tf_op jit(solution)/shard_map/ppermute | solution.py:166
  43.7 0.1 slice_negate_fusion
  43.8 0.0 copy-done.3
  43.8 0.0 copy-done.1
  43.8 0.0 copy-done.2
  43.8 0.2 pad_maximum_fusion
  44.0 1.1 %copy.18 = bf16[32,40,128]{2,1,0:T(8,128)(2,1)S(1)} copy(bf16[32,40,128]{1,0,2:T(8,128)(2,1)S(1)} %bitcast.22) | data formatting | bytes 655360 | tf_op jit(solution)/shard_map/reshape | solution.py:173
  45.1 0.0 copy-done
  45.1 1.0 %maximum_multiply_fusion.refs_2_ = bf16[32,80,128]{2,1,0:T(8,128)(2,1)} fusion(bf16[32,40,128]{2,1,0:T(8,128)(2,1)S(1)} %copy.18, bf16[32,40,128]{2,1,0:T(8,128)(2,1)S(1)} %copy.17.refs_6_), kind=kLoop, calls=%fused_computation.1 | loop fusion | flops 1966080 | bytes 1310720 | tf_op jit(solution)/shard_map/mul | solution.py:175
  46.1 0.0 collective-permute-done.3.refs_4_
  46.1 0.7 %copy-done.4 = bf16[32,40,128]{2,1,0:T(8,128)(2,1)} copy-done((bf16[32,40,128]{2,1,0:T(8,128)(2,1)}, bf16[32,40,128]{2,1,0:T(8,128)(2,1)S(1)}, u32[]{:S(2)}) %copy-start.4) | copy-done | bytes 327704
  46.8 5.5 %shard_map.74 = f32[5,40,2560]{2,1,0:T(8,128)} custom-call(s32[5]{0:T(128)} %bitcast.24, s32[1]{0:T(128)S(6)} %copy.25.refs_1_, bf16[32,80,128]{2,1,0:T(8,128)(2,1)} %maximum_multiply_fusion.refs_2_, bf16[32,40,128]{2,1,0:T(8,128)(2,1)} %copy-done.3, bf16[32,40,128]{2,1,0:T(8,128)(2,1)} %copy-done.4, bf16[32,40,128]{2,1,0:T(8,128)(2,1)} %copy-done.2, ...), custom_call_target="tpu_custom_call" | custom-call | tf_op jit(solution)/shard_map/pallas_call | solution.py:135
  (2 shorter events, 0.0 us)
Async XLA Ops:
  24.0 21.2 %copy-start = (bf16[32,40,128]{2,1,0:T(8,128)(2,1)}, bf16[32,40,128]{2,1,0:T(8,128)(2,1)S(1)}, u32[]{:S(2)}) copy-start(bf16[32,40,128]{2,1,0:T(8,128)(2,1)S(1)} %copy.17.refs_6_) | copy-start | bytes 983044
  24.0 8.1 %collective-permute-start = (bf16[32,40,128]{2,1,0:T(8,128)(2,1)S(1)}, bf16[32,40,128]{2,1,0:T(8,128)(2,1)S(1)}, u32[]{:S(2)}, u32[]{:S(2)}) collective-permute-start(bf16[32,40,128]{2,1,0:T(8,128)(2,1)S(1)} %copy.17.refs_6_), channel_id=1, source_target_pairs={{0,2},{2,4},{3,1},{4,6},{5,3},{7,5},{8,10},{10,12},{11,9},{12,14},... | collective-permute-start | bytes 983048 | tf_op jit(solution)/shard_map/ppermute | solution.py:159
  32.0 11.8 %copy-start.3 = (bf16[32,40,128]{2,1,0:T(8,128)(2,1)}, bf16[32,40,128]{2,1,0:T(8,128)(2,1)S(1)}, u32[]{:S(2)}) copy-start(bf16[32,40,128]{2,1,0:T(8,128)(2,1)S(1)} %collective-permute-done.refs_3_) | copy-start | bytes 983044
  33.1 5.0 %collective-permute-start.2 = (bf16[32,40,128]{2,1,0:T(8,128)(2,1)S(1)}, bf16[32,40,128]{2,1,0:T(8,128)(2,1)S(1)}, u32[]{:S(2)}, u32[]{:S(2)}) collective-permute-start(bf16[32,40,128]{2,1,0:T(8,128)(2,1)S(1)} %copy.20), channel_id=1, source_target_pairs={{1,0},{2,1},{3,2},{4,3},{5,4},{6,5},{7,6},{9,8},{10,9},{11,10},{12... | collective-permute-start | bytes 983048 | tf_op jit(solution)/shard_map/ppermute | solution.py:19
  34.4 4.3 %collective-permute-start.1 = (bf16[32,40,128]{2,1,0:T(8,128)(2,1)S(1)}, bf16[32,40,128]{2,1,0:T(8,128)(2,1)S(1)}, u32[]{:S(2)}, u32[]{:S(2)}) collective-permute-start(bf16[32,40,128]{2,1,0:T(8,128)(2,1)S(1)} %copy.20), channel_id=1, source_target_pairs={{0,1},{1,2},{2,3},{3,4},{4,5},{5,6},{6,7},{8,9},{9,10},{10,11},{11... | collective-permute-start | bytes 983048 | tf_op jit(solution)/shard_map/ppermute | solution.py:19
  38.2 5.6 %copy-start.1 = (bf16[32,40,128]{2,1,0:T(8,128)(2,1)}, bf16[32,40,128]{2,1,0:T(8,128)(2,1)S(1)}, u32[]{:S(2)}) copy-start(bf16[32,40,128]{2,1,0:T(8,128)(2,1)S(1)} %collective-permute-done.2.refs_7_) | copy-start | bytes 983044
  38.7 5.1 %copy-start.2 = (bf16[32,40,128]{2,1,0:T(8,128)(2,1)}, bf16[32,40,128]{2,1,0:T(8,128)(2,1)S(1)}, u32[]{:S(2)}) copy-start(bf16[32,40,128]{2,1,0:T(8,128)(2,1)S(1)} %collective-permute-done.1.refs_5_) | copy-start | bytes 983044
  38.8 7.4 %collective-permute-start.3 = (bf16[32,40,128]{2,1,0:T(8,128)(2,1)S(1)}, bf16[32,40,128]{2,1,0:T(8,128)(2,1)S(1)}, u32[]{:S(2)}, u32[]{:S(2)}) collective-permute-start(bf16[32,40,128]{2,1,0:T(8,128)(2,1)S(1)} %broadcast_select_fusion), channel_id=1, source_target_pairs={{0,1},{1,0},{2,3},{3,2},{4,5},{5,4},{6,7},{7,6},{8,9},{9,8},{10,11... | collective-permute-start | bytes 983048 | tf_op jit(solution)/shard_map/ppermute | solution.py:166
  46.1 0.7 %copy-start.4 = (bf16[32,40,128]{2,1,0:T(8,128)(2,1)}, bf16[32,40,128]{2,1,0:T(8,128)(2,1)S(1)}, u32[]{:S(2)}) copy-start(bf16[32,40,128]{2,1,0:T(8,128)(2,1)S(1)} %collective-permute-done.3.refs_4_) | copy-start | bytes 983044
